TPU v7x, 128 devices: a whole 4x4x4 slice. The times are simulated.
128 devices in a mesh: grp: 4 (over x), gx: 4 (over y), gy: 8 (over z, core).
Axes of the slice: x: 4, y: 4, z: 4, core: 2. Of those that a mesh axis runs over, the one named last changes fastest.
Arguments:
- modes_now: float32 [4, 32, 512, 1024], P('grp', ('gx', 'gy')), may hold values from -6 to 6
- modes_old: float32 [4, 32, 512, 1024], P('grp', ('gx', 'gy')), may hold values from -6 to 6
- pressure_now: float32 [4, 32, 512, 1024], P('grp', None, 'gx', 'gy'), may hold values from -6 to 6
- source: float32 [4, 32, 512, 1024], P('grp', None, 'gx', 'gy'), may hold values from -6 to 6
- strip_slot: int32 [4, 512, 8], P('grp', 'gx', 'gy'), may hold values from 0 to 255, as said below
- strip_row: int32 [4, 512, 8], P('grp', 'gx', 'gy'), may hold values from 0 to 127, as said below
Outputs:
- modes_new: float32 [4, 32, 512, 1024], P('grp', ('gx', 'gy'))
- pressure_next: float32 [4, 32, 512, 1024], P('grp', None, 'gx', 'gy')
Inputs may be any that keep to these rules, and one draw needn't show every extreme that they name: The 128 strips of one device take distinct values of strip_slot. Each device sends to every other device (itself included) either no strip or exactly 2, and every bottom-face strip of every device is met by exactly one top-face strip. `strip_row`: see strip_slot.
All inputs are finite; a program needn't handle non-finite values.
Results may differ from a plain program's by a relative error of at most 0.00007.
Values sent between devices are 32-bit elements; how exact they have to be, the bound alone decides.
No kernel may reach another device: no remote copies, remote signals or barrier semaphores. Data moves between devices by JAX's collectives and lax.ppermute only.
A program may use at most 64 MiB of HBM per device.

v0:
```python
import jax
import jax.numpy as jnp
from jax import lax
from jax.sharding import PartitionSpec as P

COURANT = 0.5
WEIGHTS = (1.5, -0.15, 2.0 / 180.0)
HIGH = lax.Precision.HIGHEST
FAST = lax.Precision.HIGH


def cosine_table(count):
    rows = jnp.arange(count, dtype=jnp.int32).astype(jnp.float32)[:, None]
    cols = jnp.arange(count, dtype=jnp.int32).astype(jnp.float32)[None, :]
    scale = jnp.where(rows == 0, jnp.sqrt(1.0 / count), jnp.sqrt(2.0 / count))
    return scale * jnp.cos(jnp.pi * rows * (cols + 0.5) / count)


def face_stencil(diff):
    first = diff[..., 0, :]
    second = diff[..., 1, :]
    third = diff[..., 2, :]
    return jnp.stack(
        [
            WEIGHTS[0] * first + WEIGHTS[1] * second + WEIGHTS[2] * third,
            WEIGHTS[1] * first + WEIGHTS[2] * second,
            WEIGHTS[2] * first,
        ],
        axis=-2,
    )


def to_modes(field, table_z, table_x, table_y):
    width_x = lax.axis_size("gx")
    width_y = lax.axis_size("gy")
    rows_x = field.shape[2]
    cols_y = field.shape[3]
    part = jnp.einsum("kz,zxy->kxy", table_z, field[0], precision=HIGH)
    part = lax.all_to_all(part, ("gx", "gy"), split_axis=0, concat_axis=0, tiled=True)
    part = part.reshape(width_x, width_y, rows_x, cols_y)
    split_x = table_x.reshape(table_x.shape[0], width_x, rows_x)
    split_y = table_y.reshape(table_y.shape[0], width_y, cols_y)
    part = jnp.einsum("bix,ijxy->bjy", split_x, part, precision=FAST)
    return jnp.einsum("cjy,bjy->bc", split_y, part, precision=FAST)[None, None]


def to_cells(modes, table_z, table_x, table_y):
    width_x = lax.axis_size("gx")
    width_y = lax.axis_size("gy")
    rows_x = modes.shape[2] // width_x
    cols_y = modes.shape[3] // width_y
    split_x = table_x.reshape(table_x.shape[0], width_x, rows_x)
    split_y = table_y.reshape(table_y.shape[0], width_y, cols_y)
    part = jnp.einsum("cjy,bc->bjy", split_y, modes[0, 0], precision=FAST)
    part = jnp.einsum("bix,bjy->ijxy", split_x, part, precision=FAST)
    part = part.reshape(width_x * width_y, rows_x, cols_y)
    cells = lax.all_to_all(part, ("gx", "gy"), split_axis=0, concat_axis=0, tiled=True)
    return jnp.einsum("kz,kxy->zxy", table_z, cells, precision=HIGH)[None]


def advance_terms(depth_index, depth, long_x, long_y):
    index_x = jnp.arange(long_x, dtype=jnp.int32).astype(jnp.float32)
    index_y = jnp.arange(long_y, dtype=jnp.int32).astype(jnp.float32)
    part_z = depth_index / depth * (depth_index / depth)
    part_x = index_x / long_x * (index_x / long_x)
    part_y = index_y / long_y * (index_y / long_y)
    theta = (
        COURANT
        * jnp.pi
        * jnp.sqrt(part_z[:, None, None] + part_x[None, :, None] + part_y[None, None, :])
    )
    shape = jnp.sinc(theta / (2.0 * jnp.pi))
    return 2.0 * jnp.cos(theta), COURANT * COURANT * shape * shape


def one_hot(index, count):
    return (index[:, None] == jnp.arange(count, dtype=jnp.int32)[None, :]).astype(jnp.float32)


def shards(modes_now, modes_old, pressure_now, source, strip_slot, strip_row):
    depth = source.shape[1]
    rows_x = source.shape[2]
    cols_y = source.shape[3]
    planes = modes_now.shape[1]
    long_x = modes_now.shape[2]
    long_y = modes_now.shape[3]
    block = lax.axis_index(("gx", "gy"))
    depth_index = (block * planes + jnp.arange(planes, dtype=jnp.int32)).astype(jnp.float32)
    table_z, table_x, table_y, scale_now, scale_spec = lax.optimization_barrier(
        (cosine_table(depth), cosine_table(long_x), cosine_table(long_y))
        + advance_terms(depth_index, depth, long_x, long_y)
    )
    top = jnp.stack(
        [pressure_now[0, depth - 1], pressure_now[0, depth - 2], pressure_now[0, depth - 3]], axis=1
    ).reshape(rows_x, 3 * cols_y)
    bottom = jnp.transpose(pressure_now[0, 0:3], (1, 0, 2)).reshape(rows_x, 3 * cols_y)
    devices = lax.axis_size(("grp", "gx", "gy"))
    slots_per = max(2, rows_x // devices)
    total = devices * slots_per
    slots = strip_slot.reshape(-1)
    rows = strip_row.reshape(-1)
    label = jnp.broadcast_to((rows + 1).astype(jnp.float32)[:, None], (rows_x, cols_y))
    send = one_hot(slots, total)
    payload = jnp.concatenate([top, label], axis=1)
    buffer = jnp.einsum("sk,sf->kf", send, payload, precision=HIGH)
    got = lax.all_to_all(buffer, ("grp", "gx", "gy"), split_axis=0, concat_axis=0, tiled=True)
    rims = got[:, : 3 * cols_y].reshape(total, 3, cols_y)
    marks = jnp.round(got[:, 3 * cols_y]).astype(jnp.int32) - 1
    live = marks >= 0
    meet = one_hot(marks, rows_x)
    met = jnp.einsum("kr,rf->kf", meet, bottom, precision=HIGH).reshape(total, 3, cols_y)
    force = face_stencil(met - rims) * live[:, None, None].astype(jnp.float32)
    force = force.reshape(total, 3 * cols_y)
    back = lax.all_to_all(force, ("grp", "gx", "gy"), split_axis=0, concat_axis=0, tiled=True)
    top_force = jnp.einsum("sk,kf->sf", send, back, precision=HIGH).reshape(rows_x, 3, cols_y)
    bottom_force = jnp.einsum("kr,kf->rf", meet, -force, precision=HIGH).reshape(rows_x, 3, cols_y)
    forcing = source.at[:, 0:3].add(jnp.transpose(bottom_force, (1, 0, 2))[None])
    forcing = forcing.at[:, depth - 1].add(top_force[:, 0][None])
    forcing = forcing.at[:, depth - 2].add(top_force[:, 1][None])
    forcing = forcing.at[:, depth - 3].add(top_force[:, 2][None])
    spectrum = to_modes(forcing, table_z, table_x, table_y)
    modes_new = (scale_now * modes_now[0] - modes_old[0] + scale_spec * spectrum[0])[None]
    pressure_next = to_cells(modes_new, table_z, table_x, table_y)
    return (modes_new, pressure_next)


def solution(mesh):
    placed = (
        P("grp", ("gx", "gy"), None, None),
        P("grp", ("gx", "gy"), None, None),
        P("grp", None, "gx", "gy"),
        P("grp", None, "gx", "gy"),
        P("grp", "gx", "gy"),
        P("grp", "gx", "gy"),
    )
    return jax.shard_map(
        shards,
        mesh=mesh,
        in_specs=placed,
        out_specs=(P("grp", ("gx", "gy"), None, None), P("grp", None, "gx", "gy")),
        check_vma=False,
    )
```

profile of v0, /device:TPU:1, one launch (start us, length us, event | category | flops | bytes accessed | tf_op | source)
XLA Modules:
  0.0 167.5 jit_solution(6861575030150739126)
XLA Ops:
  0.7 0.8 copy-done.11
  1.5 0.8 copy-done.7
  2.6 0.5 fusion.34
  3.1 1.1 all_to_all.20
  4.2 11.5 %all-to-all-start = ((f32[128,2,512]{2,1,0:T(2,128)}), f32[128,2,512]{2,1,0:T(2,128)S(1)}, u32[]{:S(2)}, u32[]{:S(2)}) async-start(f32[128,2,512]{2,1,0:T(2,128)} %all_to_all.20), calls=%async_computation | async-start | bytes 1048576 | tf_op jit(solution)/shard_map/all_to_all | solution.py:106
  16.0 11.3 %multiply_multiply_fusion = (f32[1,512,1024]{2,1,0:T(8,128)}, f32[1,512,1024]{2,1,0:T(8,128)}) fusion(f32[1024]{0:T(1024)S(1)} %multiply_multiply_fusion.5, f32[512]{0:T(512)S(1)} %multiply_add_fusion.2), kind=kLoop, calls=%fused_computation.1 | loop fusion | flops 20447232 | bytes 4200448 | tf_op jit(solution)/shard_map/mul | solution.py:73
  27.3 3.5 %cosine_multiply_fusion.2 = f32[512,512]{0,1:T(8,128)S(1)} fusion(f32[512]{0:T(512)S(1)} %get-tuple-element.80, f32[512]{0:T(512)S(1)} %get-tuple-element.81, f32[512]{0:T(512)S(1)} %fusion.65), kind=kLoop, calls=%fused_computation.47 | loop fusion | flops 786432 | bytes 1054720 | tf_op jit(solution)/shard_map/mul | solution.py:16
  30.9 15.1 %cosine_multiply_fusion = f32[1024,1024]{0,1:T(8,128)} fusion(f32[1024]{0:T(1024)S(1)} %get-tuple-element.82, f32[1024]{0:T(1024)S(1)} %get-tuple-element.83, f32[1024]{0:T(1024)S(1)} %fusion.64), kind=kLoop, calls=%fused_computation | loop fusion | flops 3145728 | bytes 4206592 | tf_op jit(solution)/shard_map/mul | solution.py:16
  46.0 0.4 all_to_all.22
  46.9 0.3 convolution_subtract_fusion
  47.2 0.8 reshape.559
  48.1 1.0 copy.72
  49.1 2.1 %stack.16 = f32[128,2,384]{2,1,0:T(2,128)} reshape(f32[256,3,128]{2,1,0:T(4,128)} %copy.72) | data formatting | bytes 786432 | tf_op jit(solution)/shard_map/stack | solution.py:23
  51.2 2.0 %broadcast_multiply_fusion = f32[128,2,384]{2,1,0:T(2,128)} fusion(f32[128,2,384]{2,1,0:T(2,128)} %stack.16, f32[128,2]{1,0:T(8,128)} %reshape.559), kind=kLoop, calls=%fused_computation.57 | loop fusion | flops 98304 | bytes 787456 | tf_op jit(solution)/shard_map/mul | solution.py:112
  53.2 10.2 %all-to-all-start.1 = ((f32[128,2,384]{2,1,0:T(2,128)}), f32[128,2,384]{2,1,0:T(2,128)}, u32[]{:S(2)}, u32[]{:S(2)}) async-start(f32[128,2,384]{2,1,0:T(2,128)} %broadcast_multiply_fusion), calls=%async_computation.1 | async-start | bytes 786432 | tf_op jit(solution)/shard_map/all_to_all | solution.py:114
  63.3 0.7 fusion.33
  64.0 1.0 fusion.32
  65.1 10.1 %all-to-all-done.1 = f32[128,2,384]{2,1,0:T(2,128)} async-done(((f32[128,2,384]{2,1,0:T(2,128)}), f32[128,2,384]{2,1,0:T(2,128)}, u32[]{:S(2)}, u32[]{:S(2)}) %all-to-all-start.1) | async-done | bytes 393248 | tf_op jit(solution)/shard_map/all_to_all | solution.py:114
  75.2 1.3 all_to_all.24
  76.5 0.9 copy.73
  77.4 1.4 fusion.44
  79.0 3.0 %fusion.16 = f32[32,128,128]{2,0,1:T(8,128)S(1)} fusion(f32[32,128,128]{2,1,0:T(8,128)S(1)} %fusion.53, f32[32,32]{0,1:T(8,128)S(1)} %cosine_multiply_fusion.3), kind=kOutput, calls=%fused_computation.27 | convolution fusion | flops 201326592 | bytes 4198400 | tf_op jit(solution)/shard_map/kz,zxy->kxy/dot_general | solution.py:38
  82.1 1.2 copy.76
  83.3 32.9 %all_to_all.31 = f32[32,128,128]{2,1,0:T(8,128)S(1)} all-to-all(f32[32,128,128]{2,1,0:T(8,128)S(1)} %copy.76), channel_id=1, replica_groups=mesh['grp'=4,'gx'=4,'gy'=8] {'gx','gy'}, dimensions={0} | all-to-all | bytes 4194304 | tf_op jit(solution)/shard_map/all_to_all | solution.py:39
  116.2 2.0 %fusion.68 = f32[512,8,128,1]{2,0,1,3:T(8,128)S(1)} fusion(f32[512,4,128,1]{0,2,3,1:T(8,128)S(1)} %bitcast.131, f32[4,8,128,128]{3,2,1,0:T(8,128)S(1)} %bitcast.133), kind=kOutput, calls=%fused_computation.106 | convolution fusion | flops 1610612736 | bytes 5242880 | tf_op jit(solution)/shard_map/bix,ijxy->bjy/dot_general | solution.py:43
  118.4 4.3 %fusion.13 = f32[1,512,1024]{2,1,0:T(8,128)S(1)} fusion(f32[1,512,1024]{2,1,0:T(8,128)S(1)} %copy-done.2, f32[1,1,512,1024]{3,2,1,0:T(8,128)S(1)} %copy-done.5, f32[1,512,1024]{2,1,0:T(8,128)S(1)} %copy-done.3, f32[1,1,512,1024]{3,2,1,0:T(8,128)S(1)} %copy-done.6, f32[1024,8,128]{0,2,1:T(8,128)S(1)} %bitcast.128, f32[512,8,128,1]{2,0,1,3:T(8,128)S(1)} %fusion.68), kind=kOutput, calls=%fused_computation.22 | convolution fusion | flops 3223322624 | bytes 16777216 | tf_op jit(solution)/shard_map/cjy,bjy->bc/dot_general | solution.py:44
  122.7 3.5 %fusion.11 = f32[512,8,128]{0,2,1:T(8,128)S(1)} fusion(f32[1024,8,128]{0,2,1:T(8,128)S(1)} %bitcast.129, f32[1,512,1024]{2,1,0:T(8,128)S(1)} %fusion.13), kind=kOutput, calls=%fused_computation.19 | convolution fusion | flops 3221225472 | bytes 8388608 | tf_op jit(solution)/shard_map/cjy,bc->bjy/dot_general | solution.py:54
  126.3 1.8 %fusion.26 = f32[4,8,128,128]{2,3,0,1:T(8,128)S(1)} fusion(f32[512,4,128,1]{0,2,1,3:T(8,128)S(1)} %bitcast.132, f32[512,8,128]{0,2,1:T(8,128)S(1)} %fusion.11), kind=kOutput, calls=%fused_computation.42 | convolution fusion | flops 1610612736 | bytes 5242880 | tf_op jit(solution)/shard_map/bix,bjy->ijxy/dot_general | solution.py:55
  128.1 1.8 %copy.83 = f32[4,8,128,128]{3,2,1,0:T(8,128)} copy(f32[4,8,128,128]{2,3,0,1:T(8,128)S(1)} %fusion.26) | data formatting | bytes 4194304 | tf_op jit(solution)/shard_map/bix,bjy->ijxy/transpose | solution.py:55
  129.9 32.1 %all_to_all.32 = f32[32,128,128]{2,1,0:T(8,128)S(1)} all-to-all(f32[32,128,128]{2,1,0:T(8,128)} %bitcast.134), channel_id=1, replica_groups=mesh['grp'=4,'gx'=4,'gy'=8] {'gx','gy'}, dimensions={0} | all-to-all | bytes 4194304 | tf_op jit(solution)/shard_map/all_to_all | solution.py:57
  162.0 3.0 %fusion.23 = f32[1,32,128,128]{3,1,2,0:T(8,128)S(1)} fusion(f32[32,128,128]{2,1,0:T(8,128)S(1)} %all_to_all.32, f32[32,32]{0,1:T(8,128)S(1)} %cosine_multiply_fusion.3), kind=kOutput, calls=%fused_computation.41 | convolution fusion | flops 201326592 | bytes 4198400 | tf_op jit(solution)/shard_map/kz,kxy->zxy/dot_general | solution.py:58
  165.0 2.5 %copy.85 = f32[1,32,128,128]{3,2,1,0:T(8,128)} copy(f32[1,32,128,128]{3,1,2,0:T(8,128)S(1)} %fusion.23) | data formatting | bytes 4194304
  (52 shorter events, 1.6 us)
Async XLA Ops:
  0.6 1.6 copy-start.7
  0.6 2.0 %copy-start.10 = (s32[1,128,1]{1,2,0:T(1,128)S(1)}, s32[1,128,1]{1,2,0:T(1,128)}, u32[]{:S(2)}) copy-start(s32[1,128,1]{1,2,0:T(1,128)} %param.18) | copy-start | bytes 1540
  0.7 0.8 copy-start.11
  2.3 13.6 %slice-start = ((f32[1,32,128,128]{3,2,1,0:T(8,128)}), f32[1,3,128,128]{3,2,1,0:T(8,128)S(1)}, s32[]{:S(2)}) async-start(f32[1,32,128,128]{3,2,1,0:T(8,128)} %param.16), calls=%async_computation.4 | async-start | bytes 393216 | tf_op jit(solution)/shard_map/slice | solution.py:96
  4.2 41.8 %all-to-all-start = ((f32[128,2,512]{2,1,0:T(2,128)}), f32[128,2,512]{2,1,0:T(2,128)S(1)}, u32[]{:S(2)}, u32[]{:S(2)}) async-start(f32[128,2,512]{2,1,0:T(2,128)} %all_to_all.20), calls=%async_computation | async-start | bytes 1048576 | tf_op jit(solution)/shard_map/all_to_all | solution.py:106
  46.5 1.5 copy-start.9
  46.6 1.4 copy-start.8
  48.0 16.0 %copy-start.1 = (f32[1,32,128,128]{3,2,1,0:T(8,128)S(1)}, f32[1,32,128,128]{3,2,1,0:T(8,128)}, u32[]{:S(2)}) copy-start(f32[1,32,128,128]{3,2,1,0:T(8,128)} %param.17) | copy-start | bytes 6291460
  53.2 22.0 %all-to-all-start.1 = ((f32[128,2,384]{2,1,0:T(2,128)}), f32[128,2,384]{2,1,0:T(2,128)}, u32[]{:S(2)}, u32[]{:S(2)}) async-start(f32[128,2,384]{2,1,0:T(2,128)} %broadcast_multiply_fusion), calls=%async_computation.1 | async-start | bytes 786432 | tf_op jit(solution)/shard_map/all_to_all | solution.py:114
  82.1 36.2 %copy-start.5 = (f32[1,1,512,1024]{3,2,1,0:T(8,128)S(1)}, f32[1,1,512,1024]{3,2,1,0:T(8,128)}, u32[]{:S(2)}) copy-start(f32[1,1,512,1024]{3,2,1,0:T(8,128)} %param.15) | copy-start | bytes 6291460
  82.1 36.2 %copy-start.6 = (f32[1,1,512,1024]{3,2,1,0:T(8,128)S(1)}, f32[1,1,512,1024]{3,2,1,0:T(8,128)}, u32[]{:S(2)}) copy-start(f32[1,1,512,1024]{3,2,1,0:T(8,128)} %param.14) | copy-start | bytes 6291460
  83.3 34.9 %copy-start.2 = (f32[1,512,1024]{2,1,0:T(8,128)S(1)}, f32[1,512,1024]{2,1,0:T(8,128)}, u32[]{:S(2)}) copy-start(f32[1,512,1024]{2,1,0:T(8,128)} %get-tuple-element.56) | copy-start | bytes 6291460
  83.3 34.9 %copy-start.3 = (f32[1,512,1024]{2,1,0:T(8,128)S(1)}, f32[1,512,1024]{2,1,0:T(8,128)}, u32[]{:S(2)}) copy-start(f32[1,512,1024]{2,1,0:T(8,128)} %get-tuple-element.55) | copy-start | bytes 6291460
  116.2 2.2 %copy-start = (f32[1024,1024]{0,1:T(8,128)S(1)}, f32[1024,1024]{0,1:T(8,128)}, u32[]{:S(2)}) copy-start(f32[1024,1024]{0,1:T(8,128)} %cosine_multiply_fusion) | copy-start | bytes 12582916
  122.7 3.6 %copy-start.4 = (f32[1,512,1024]{2,1,0:T(8,128)}, f32[1,512,1024]{2,1,0:T(8,128)S(1)}, u32[]{:S(2)}) copy-start(f32[1,512,1024]{2,1,0:T(8,128)S(1)} %fusion.13) | copy-start | bytes 6291460
where the time goes:
time: 168 us
  blocking collectives  65 us (39%)
  other arithmetic  33.1 us (20%)
  starting transfers between devices  21.7 us (13%)
  matrix products  20.9 us (12%)
  local copies, waits for them, and re-layouts  15.8 us (9%)
  waiting for transfers between devices  10.1 us (6%)
    all_to_all x1, blocking collectives, to_modes(): lax.all_to_all(part, ('gx', 'gy'), split_axis=0, concat_axis=0, tiled=True)  32.9 us
    all_to_all x1, blocking collectives, to_cells(): lax.all_to_all(part, ('gx', 'gy'), split_axis=0, concat_axis=0, tiled=True)  32.1 us
    mul x4, other arithmetic, cosine_table(): return scale * jnp.cos(jnp.pi * rows * (cols + 0.5) / count)  18.7 us
    all_to_all x1, starting transfers between devices, shards(): lax.all_to_all(buffer, ('grp', 'gx', 'gy'), split_axis=0, concat_axis=0,...  11.5 us
    mul x1, other arithmetic, advance_terms(): return (2.0 * jnp.cos(theta), COURANT * COURANT * shape * shape)  11.3 us
    all_to_all x1, starting transfers between devices, shards(): lax.all_to_all(force, ('grp', 'gx', 'gy'), split_axis=0, concat_axis=0, t...  10.2 us
    all_to_all x1, waiting for transfers between devices, shards(): lax.all_to_all(force, ('grp', 'gx', 'gy'), split_axis=0, concat_axis=0, t...  10.1 us
    unnamed x30, local copies, waits for them, and re-layouts  4.93 us
  transfers between devices with their start and end apart: 2, of which 1 were waited for; matrix products, arithmetic and copies ran while one was open for 19% of the time, Pallas kernels for 0%

commit v1 on v0

--- a/solution.py
+++ b/solution.py
@@ -86,10 +86,12 @@
     long_y = modes_now.shape[3]
     block = lax.axis_index(("gx", "gy"))
     depth_index = (block * planes + jnp.arange(planes, dtype=jnp.int32)).astype(jnp.float32)
-    table_z, table_x, table_y, scale_now, scale_spec = lax.optimization_barrier(
-        (cosine_table(depth), cosine_table(long_x), cosine_table(long_y))
-        + advance_terms(depth_index, depth, long_x, long_y)
-    )
+    table_z = lax.optimization_barrier(cosine_table(depth))
+    table_x = lax.optimization_barrier(cosine_table(long_x))
+    table_y = lax.optimization_barrier(cosine_table(long_y))
+    scale_now, scale_spec = advance_terms(depth_index, depth, long_x, long_y)
+    scale_now = lax.optimization_barrier(scale_now)
+    scale_spec = lax.optimization_barrier(scale_spec)
     top = jnp.stack(
         [pressure_now[0, depth - 1], pressure_now[0, depth - 2], pressure_now[0, depth - 3]], axis=1
     ).reshape(rows_x, 3 * cols_y)
@@ -104,13 +106,23 @@
     payload = jnp.concatenate([top, label], axis=1)
     buffer = jnp.einsum("sk,sf->kf", send, payload, precision=HIGH)
     got = lax.all_to_all(buffer, ("grp", "gx", "gy"), split_axis=0, concat_axis=0, tiled=True)
-    rims = got[:, : 3 * cols_y].reshape(total, 3, cols_y)
+    rims = got[:, : 3 * cols_y]
     marks = jnp.round(got[:, 3 * cols_y]).astype(jnp.int32) - 1
-    live = marks >= 0
+    live = (marks >= 0).astype(jnp.float32)[:, None]
     meet = one_hot(marks, rows_x)
-    met = jnp.einsum("kr,rf->kf", meet, bottom, precision=HIGH).reshape(total, 3, cols_y)
-    force = face_stencil(met - rims) * live[:, None, None].astype(jnp.float32)
-    force = force.reshape(total, 3 * cols_y)
+    met = jnp.einsum("kr,rf->kf", meet, bottom, precision=HIGH)
+    diff = met - rims
+    first = diff[:, :cols_y]
+    second = diff[:, cols_y : 2 * cols_y]
+    third = diff[:, 2 * cols_y :]
+    force = jnp.concatenate(
+        [
+            WEIGHTS[0] * first + WEIGHTS[1] * second + WEIGHTS[2] * third,
+            WEIGHTS[1] * first + WEIGHTS[2] * second,
+            WEIGHTS[2] * first,
+        ],
+        axis=1,
+    ) * live
     back = lax.all_to_all(force, ("grp", "gx", "gy"), split_axis=0, concat_axis=0, tiled=True)
     top_force = jnp.einsum("sk,kf->sf", send, back, precision=HIGH).reshape(rows_x, 3, cols_y)
     bottom_force = jnp.einsum("kr,kf->rf", meet, -force, precision=HIGH).reshape(rows_x, 3, cols_y)

time: 168 us -> 148 us (0.88)
  blocking collectives: 65 us -> 35.6 us
  waiting for transfers between devices: 10.1 us -> 24.7 us
  local copies, waits for them, and re-layouts: 15.8 us -> 11.6 us
    all_to_all x1 -> x0, blocking collectives: 32.9 us -> none  [to_modes(): lax.all_to_all(part, ('gx', 'gy'), split_axis=0, concat_axis=0, tiled=True)]
    all_to_all x1, waiting for transfers between devices: 0.01 us -> 13.2 us  [shards(): lax.all_to_all(buffer, ('grp', 'gx', 'gy'), split_axis=0, concat_axis=0,...]
    all_to_all x1, starting transfers between devices: 10.2 us -> 4.71 us  [shards(): lax.all_to_all(force, ('grp', 'gx', 'gy'), split_axis=0, concat_axis=0, t...]
    all_to_all x0 -> x1, starting transfers between devices: none -> 4.92 us  [to_modes(): lax.all_to_all(part, ('gx', 'gy'), split_axis=0, concat_axis=0, tiled=True)]
    all_to_all x1, blocking collectives: 32.1 us -> 35.6 us  [to_cells(): lax.all_to_all(part, ('gx', 'gy'), split_axis=0, concat_axis=0, tiled=True)]
    another operation x2 -> x0, local copies, waits for them, and re-layouts: 3.14 us -> none  [face_stencil(): jnp.stack([WEIGHTS[0] * first + WEIGHTS[1] * second + WEIGHTS[2] * third,...]
    dot_general x1, matrix products: 4.27 us -> 7.03 us  [to_modes(): return jnp.einsum('cjy,bjy->bc', split_y, part, precision=FAST)[None, None]]
    unnamed x30 -> x18, local copies, waits for them, and re-layouts: 4.93 us -> 5.02 us
  transfers between devices with their start and end apart: 2 -> 3, of which waited for: 1 -> 2; matrix products, arithmetic and copies ran while one was open for 19% -> 21% of each run, Pallas kernels for 0% -> 0%
where the time goes in v1:
time: 148 us
  blocking collectives  35.6 us (24%)
  other arithmetic  31.5 us (21%)
  waiting for transfers between devices  24.7 us (17%)
  matrix products  22.1 us (15%)
  starting transfers between devices  21.1 us (14%)
  local copies, waits for them, and re-layouts  11.6 us (8%)
    all_to_all x1, blocking collectives, to_cells(): lax.all_to_all(part, ('gx', 'gy'), split_axis=0, concat_axis=0, tiled=True)  35.6 us
    mul x4, other arithmetic, cosine_table(): return scale * jnp.cos(jnp.pi * rows * (cols + 0.5) / count)  18.7 us
    all_to_all x1, waiting for transfers between devices, shards(): lax.all_to_all(buffer, ('grp', 'gx', 'gy'), split_axis=0, concat_axis=0,...  13.2 us
    all_to_all x1, starting transfers between devices, shards(): lax.all_to_all(buffer, ('grp', 'gx', 'gy'), split_axis=0, concat_axis=0,...  11.5 us
    all_to_all x1, waiting for transfers between devices, shards(): lax.all_to_all(force, ('grp', 'gx', 'gy'), split_axis=0, concat_axis=0, t...  11.4 us
    mul x1, other arithmetic, advance_terms(): return (2.0 * jnp.cos(theta), COURANT * COURANT * shape * shape)  11.3 us
    dot_general x1, matrix products, to_modes(): return jnp.einsum('cjy,bjy->bc', split_y, part, precision=FAST)[None, None]  7.03 us
    unnamed x18, local copies, waits for them, and re-layouts  5.02 us
  transfers between devices with their start and end apart: 3, of which 2 were waited for; matrix products, arithmetic and copies ran while one was open for 21% of the time, Pallas kernels for 0%

profile of v1, /device:TPU:1, one launch (start us, length us, event | category | flops | bytes accessed | tf_op | source)
XLA Modules:
  0.0 147.6 jit_solution(11355463611150572499)
XLA Ops:
  0.7 0.8 copy-done.5
  1.5 0.8 copy-done.3
  2.6 0.5 fusion.38
  3.1 1.1 all_to_all.20
  4.2 11.5 %all-to-all-start = ((f32[128,2,512]{2,1,0:T(2,128)}), f32[128,2,512]{2,1,0:T(2,128)S(1)}, u32[]{:S(2)}, u32[]{:S(2)}) async-start(f32[128,2,512]{2,1,0:T(2,128)} %all_to_all.20), calls=%async_computation | async-start | bytes 1048576 | tf_op jit(solution)/shard_map/all_to_all | solution.py:108
  15.7 0.1 cosine_multiply_fusion.3
  16.0 13.2 %all-to-all-done = f32[128,2,512]{2,1,0:T(2,128)S(1)} async-done(((f32[128,2,512]{2,1,0:T(2,128)}), f32[128,2,512]{2,1,0:T(2,128)S(1)}, u32[]{:S(2)}, u32[]{:S(2)}) %all-to-all-start) | async-done | bytes 524320 | tf_op jit(solution)/shard_map/all_to_all | solution.py:108
  29.2 0.4 all_to_all.22
  29.9 0.4 convolution_subtract_fusion
  30.4 1.0 maximum_multiply_fusion.1
  31.4 4.7 %all-to-all-start.1 = ((f32[128,2,384]{2,1,0:T(2,128)}), f32[128,2,384]{2,1,0:T(2,128)S(1)}, u32[]{:S(2)}, u32[]{:S(2)}) async-start(f32[128,2,384]{2,1,0:T(2,128)} %maximum_multiply_fusion.1), calls=%async_computation.1 | async-start | bytes 786432 | tf_op jit(solution)/shard_map/all_to_all | solution.py:126
  36.1 0.6 fusion.32
  36.9 11.4 %all-to-all-done.1 = f32[128,2,384]{2,1,0:T(2,128)S(1)} async-done(((f32[128,2,384]{2,1,0:T(2,128)}), f32[128,2,384]{2,1,0:T(2,128)S(1)}, u32[]{:S(2)}, u32[]{:S(2)}) %all-to-all-start.1) | async-done | bytes 393248 | tf_op jit(solution)/shard_map/all_to_all | solution.py:126
  48.4 0.3 all_to_all.24
  48.7 0.2 copy.51
  48.8 0.4 fusion.49
  49.2 0.2 copy.89
  49.5 3.0 %fusion.16 = f32[32,128,128]{2,0,1:T(8,128)S(1)} fusion(f32[32,128,128]{2,1,0:T(8,128)S(1)} %fusion.55, f32[32,32]{0,1:T(8,128)S(1)} %cosine_multiply_fusion.3), kind=kOutput, calls=%fused_computation.27 | convolution fusion | flops 201326592 | bytes 4198400 | tf_op jit(solution)/shard_map/kz,zxy->kxy/dot_general | solution.py:38
  52.5 2.6 %copy.54 = f32[32,128,128]{2,1,0:T(8,128)} copy(f32[32,128,128]{2,0,1:T(8,128)S(1)} %fusion.16) | data formatting | bytes 4194304 | tf_op jit(solution)/shard_map/kz,zxy->kxy/dot_general | solution.py:38
  55.1 4.9 %all-to-all-start.2 = ((f32[32,128,128]{2,1,0:T(8,128)}), f32[32,128,128]{2,1,0:T(8,128)S(1)}, u32[]{:S(2)}, u32[]{:S(2)}) async-start(f32[32,128,128]{2,1,0:T(8,128)} %copy.54), calls=%async_computation.2 | async-start | bytes 4194304 | tf_op jit(solution)/shard_map/all_to_all | solution.py:39
  60.0 3.5 %cosine_multiply_fusion.2 = f32[512,512]{0,1:T(8,128)S(1)} fusion(f32[512]{0:T(512)S(1)} %get-tuple-element.68, f32[512]{0:T(512)S(1)} %get-tuple-element.69, f32[512]{0:T(512)S(1)} %fusion.67), kind=kLoop, calls=%fused_computation.44 | loop fusion | flops 786432 | bytes 1054720 | tf_op jit(solution)/shard_map/mul | solution.py:16
  63.6 15.1 %cosine_multiply_fusion = f32[1024,1024]{0,1:T(8,128)} fusion(f32[1024]{0:T(1024)S(1)} %get-tuple-element.66, f32[1024]{0:T(1024)S(1)} %get-tuple-element.67, f32[1024]{0:T(1024)S(1)} %fusion.66), kind=kLoop, calls=%fused_computation | loop fusion | flops 3145728 | bytes 4206592 | tf_op jit(solution)/shard_map/mul | solution.py:16
  78.6 11.3 %cosine_multiply_fusion.1 = (f32[1,512,1024]{2,1,0:T(8,128)}, f32[1,512,1024]{2,1,0:T(8,128)}) fusion(f32[1024]{0:T(1024)S(1)} %multiply_multiply_fusion.5, f32[512]{0:T(512)S(1)} %multiply_add_fusion.2), kind=kLoop, calls=%fused_computation.39 | loop fusion | flops 20447232 | bytes 4200448 | tf_op jit(solution)/shard_map/mul | solution.py:73
  90.0 1.9 %fusion.71 = f32[512,8,128,1]{2,0,1,3:T(8,128)S(1)} fusion(f32[512,4,128,1]{0,2,3,1:T(8,128)S(1)} %bitcast.115, f32[4,8,128,128]{3,2,1,0:T(8,128)S(1)} %bitcast.117), kind=kOutput, calls=%fused_computation.109 | convolution fusion | flops 1610612736 | bytes 5242880 | tf_op jit(solution)/shard_map/bix,ijxy->bjy/dot_general | solution.py:43
  91.9 0.3 copy-done
  92.2 7.0 %fusion.13 = f32[1,512,1024]{2,1,0:T(8,128)S(1)} fusion(f32[1,512,1024]{2,1,0:T(8,128)} %get-tuple-element.65, f32[1,1,512,1024]{3,2,1,0:T(8,128)} %param.15, f32[1,512,1024]{2,1,0:T(8,128)} %get-tuple-element.64, f32[1,1,512,1024]{3,2,1,0:T(8,128)} %param.14, f32[1024,8,128]{0,2,1:T(8,128)S(1)} %bitcast.112, f32[512,8,128,1]{2,0,1,3:T(8,128)S(1)} %fusion.71), kind=kOutput, calls=%fused_computation.22 | convolution fusion | flops 3223322624 | bytes 16777216 | tf_op jit(solution)/shard_map/cjy,bjy->bc/dot_general | solution.py:44
  99.2 3.5 %fusion.11 = f32[512,8,128]{0,2,1:T(8,128)S(1)} fusion(f32[1024,8,128]{0,2,1:T(8,128)S(1)} %bitcast.113, f32[1,512,1024]{2,1,0:T(8,128)S(1)} %fusion.13), kind=kOutput, calls=%fused_computation.19 | convolution fusion | flops 3221225472 | bytes 8388608 | tf_op jit(solution)/shard_map/cjy,bc->bjy/dot_general | solution.py:54
  102.8 1.8 %fusion.26 = f32[4,8,128,128]{2,3,0,1:T(8,128)S(1)} fusion(f32[512,4,128,1]{0,2,1,3:T(8,128)S(1)} %bitcast.116, f32[512,8,128]{0,2,1:T(8,128)S(1)} %fusion.11), kind=kOutput, calls=%fused_computation.42 | convolution fusion | flops 1610612736 | bytes 5242880 | tf_op jit(solution)/shard_map/bix,bjy->ijxy/dot_general | solution.py:55
  104.6 1.8 %copy.61 = f32[4,8,128,128]{3,2,1,0:T(8,128)} copy(f32[4,8,128,128]{2,3,0,1:T(8,128)S(1)} %fusion.26) | data formatting | bytes 4194304 | tf_op jit(solution)/shard_map/bix,bjy->ijxy/transpose | solution.py:55
  106.4 35.6 %all_to_all.31 = f32[32,128,128]{2,1,0:T(8,128)S(1)} all-to-all(f32[32,128,128]{2,1,0:T(8,128)} %bitcast.118), channel_id=1, replica_groups=mesh['grp'=4,'gx'=4,'gy'=8] {'gx','gy'}, dimensions={0} | all-to-all | bytes 4194304 | tf_op jit(solution)/shard_map/all_to_all | solution.py:57
  142.1 3.0 %fusion.23 = f32[1,32,128,128]{3,1,2,0:T(8,128)S(1)} fusion(f32[32,128,128]{2,1,0:T(8,128)S(1)} %all_to_all.31, f32[32,32]{0,1:T(8,128)S(1)} %cosine_multiply_fusion.3), kind=kOutput, calls=%fused_computation.41 | convolution fusion | flops 201326592 | bytes 4198400 | tf_op jit(solution)/shard_map/kz,kxy->zxy/dot_general | solution.py:58
  145.1 2.5 %copy.63 = f32[1,32,128,128]{3,2,1,0:T(8,128)} copy(f32[1,32,128,128]{3,1,2,0:T(8,128)S(1)} %fusion.23) | data formatting | bytes 4194304
  (37 shorter events, 1.1 us)
Async XLA Ops:
  0.6 1.6 %copy-start.3 = (f32[1,32,128,128]{3,2,1,0:T(8,128)S(1)}, f32[1,32,128,128]{3,2,1,0:T(8,128)}, u32[]{:S(2)}) copy-start(f32[1,32,128,128]{3,2,1,0:T(8,128)} %param.16) | copy-start | bytes 6291460
  0.6 2.0 %copy-start.4 = (s32[1,128,1]{1,2,0:T(1,128)S(1)}, s32[1,128,1]{1,2,0:T(1,128)}, u32[]{:S(2)}) copy-start(s32[1,128,1]{1,2,0:T(1,128)} %param.18) | copy-start | bytes 1540
  0.7 0.8 copy-start.5
  2.3 13.6 %slice-start = ((f32[1,32,128,128]{3,2,1,0:T(8,128)}), f32[1,3,128,128]{3,2,1,0:T(8,128)S(1)}, s32[]{:S(2)}) async-start(f32[1,32,128,128]{3,2,1,0:T(8,128)} %param.16), calls=%async_computation.4 | async-start | bytes 393216 | tf_op jit(solution)/shard_map/slice | solution.py:98
  4.2 25.0 %all-to-all-start = ((f32[128,2,512]{2,1,0:T(2,128)}), f32[128,2,512]{2,1,0:T(2,128)S(1)}, u32[]{:S(2)}, u32[]{:S(2)}) async-start(f32[128,2,512]{2,1,0:T(2,128)} %all_to_all.20), calls=%async_computation | async-start | bytes 1048576 | tf_op jit(solution)/shard_map/all_to_all | solution.py:108
  29.8 7.0 %copy-start.1 = (f32[1,32,128,128]{3,2,1,0:T(8,128)S(1)}, f32[1,32,128,128]{3,2,1,0:T(8,128)}, u32[]{:S(2)}) copy-start(f32[1,32,128,128]{3,2,1,0:T(8,128)} %param.17) | copy-start | bytes 6291460
  31.4 17.0 %all-to-all-start.1 = ((f32[128,2,384]{2,1,0:T(2,128)}), f32[128,2,384]{2,1,0:T(2,128)S(1)}, u32[]{:S(2)}, u32[]{:S(2)}) async-start(f32[128,2,384]{2,1,0:T(2,128)} %maximum_multiply_fusion.1), calls=%async_computation.1 | async-start | bytes 786432 | tf_op jit(solution)/shard_map/all_to_all | solution.py:126
  55.1 34.9 %all-to-all-start.2 = ((f32[32,128,128]{2,1,0:T(8,128)}), f32[32,128,128]{2,1,0:T(8,128)S(1)}, u32[]{:S(2)}, u32[]{:S(2)}) async-start(f32[32,128,128]{2,1,0:T(8,128)} %copy.54), calls=%async_computation.2 | async-start | bytes 4194304 | tf_op jit(solution)/shard_map/all_to_all | solution.py:39
  90.0 2.2 %copy-start = (f32[1024,1024]{0,1:T(8,128)S(1)}, f32[1024,1024]{0,1:T(8,128)}, u32[]{:S(2)}) copy-start(f32[1024,1024]{0,1:T(8,128)} %cosine_multiply_fusion) | copy-start | bytes 12582916
  99.2 3.6 %copy-start.2 = (f32[1,512,1024]{2,1,0:T(8,128)}, f32[1,512,1024]{2,1,0:T(8,128)S(1)}, u32[]{:S(2)}) copy-start(f32[1,512,1024]{2,1,0:T(8,128)S(1)} %fusion.13) | copy-start | bytes 6291460

commit v2 on v1

--- a/solution.py
+++ b/solution.py
@@ -73,6 +73,20 @@
     return 2.0 * jnp.cos(theta), COURANT * COURANT * shape * shape
 
 
+def lane_stencil(diff, cols):
+    first = diff[:, :cols]
+    second = diff[:, cols : 2 * cols]
+    third = diff[:, 2 * cols :]
+    return jnp.concatenate(
+        [
+            WEIGHTS[0] * first + WEIGHTS[1] * second + WEIGHTS[2] * third,
+            WEIGHTS[1] * first + WEIGHTS[2] * second,
+            WEIGHTS[2] * first,
+        ],
+        axis=1,
+    )
+
+
 def one_hot(index, count):
     return (index[:, None] == jnp.arange(count, dtype=jnp.int32)[None, :]).astype(jnp.float32)
 
@@ -96,36 +110,32 @@
         [pressure_now[0, depth - 1], pressure_now[0, depth - 2], pressure_now[0, depth - 3]], axis=1
     ).reshape(rows_x, 3 * cols_y)
     bottom = jnp.transpose(pressure_now[0, 0:3], (1, 0, 2)).reshape(rows_x, 3 * cols_y)
-    devices = lax.axis_size(("grp", "gx", "gy"))
+    every = ("grp", "gx", "gy")
+    devices = lax.axis_size(every)
     slots_per = max(2, rows_x // devices)
     total = devices * slots_per
     slots = strip_slot.reshape(-1)
-    rows = strip_row.reshape(-1)
-    label = jnp.broadcast_to((rows + 1).astype(jnp.float32)[:, None], (rows_x, cols_y))
+    codes = lax.all_gather(slots * rows_x + strip_row.reshape(-1), every, tiled=True)
+    codes = codes.reshape(devices, rows_x)
+    want = lax.axis_index(every) * slots_per + jnp.arange(slots_per, dtype=jnp.int32)
+    hit = (codes // rows_x)[:, :, None] == want[None, None, :]
+    found = jnp.any(hit, axis=1).reshape(total)
+    marks = jnp.sum(jnp.where(hit, (codes % rows_x)[:, :, None], 0), axis=1).reshape(total)
+    marks = jnp.where(found, marks, -1)
     send = one_hot(slots, total)
-    payload = jnp.concatenate([top, label], axis=1)
-    buffer = jnp.einsum("sk,sf->kf", send, payload, precision=HIGH)
-    got = lax.all_to_all(buffer, ("grp", "gx", "gy"), split_axis=0, concat_axis=0, tiled=True)
+    meet = one_hot(marks, rows_x)
+    rims_out = jnp.einsum("sk,sf->kf", send, top, precision=HIGH)
+    met = jnp.einsum("kr,rf->kf", meet, bottom, precision=HIGH)
+    got = lax.all_to_all(
+        jnp.concatenate([rims_out, met], axis=1), every, split_axis=0, concat_axis=0, tiled=True
+    )
     rims = got[:, : 3 * cols_y]
-    marks = jnp.round(got[:, 3 * cols_y]).astype(jnp.int32) - 1
-    live = (marks >= 0).astype(jnp.float32)[:, None]
-    meet = one_hot(marks, rows_x)
-    met = jnp.einsum("kr,rf->kf", meet, bottom, precision=HIGH)
-    diff = met - rims
-    first = diff[:, :cols_y]
-    second = diff[:, cols_y : 2 * cols_y]
-    third = diff[:, 2 * cols_y :]
-    force = jnp.concatenate(
-        [
-            WEIGHTS[0] * first + WEIGHTS[1] * second + WEIGHTS[2] * third,
-            WEIGHTS[1] * first + WEIGHTS[2] * second,
-            WEIGHTS[2] * first,
-        ],
-        axis=1,
-    ) * live
-    back = lax.all_to_all(force, ("grp", "gx", "gy"), split_axis=0, concat_axis=0, tiled=True)
-    top_force = jnp.einsum("sk,kf->sf", send, back, precision=HIGH).reshape(rows_x, 3, cols_y)
+    far = got[:, 3 * cols_y :]
+    live = found.astype(jnp.float32)[:, None]
+    force = lane_stencil(met - rims, cols_y) * live
     bottom_force = jnp.einsum("kr,kf->rf", meet, -force, precision=HIGH).reshape(rows_x, 3, cols_y)
+    partner = jnp.einsum("sk,kf->sf", send, far, precision=HIGH)
+    top_force = lane_stencil(partner - top, cols_y).reshape(rows_x, 3, cols_y)
     forcing = source.at[:, 0:3].add(jnp.transpose(bottom_force, (1, 0, 2))[None])
     forcing = forcing.at[:, depth - 1].add(top_force[:, 0][None])
     forcing = forcing.at[:, depth - 2].add(top_force[:, 1][None])

time: 148 us -> 171 us (1.16)
  blocking collectives: 35.6 us -> 70.1 us
  waiting for transfers between devices: 24.7 us -> 13.9 us
  starting transfers between devices: 21.1 us -> 11.7 us
  local copies, waits for them, and re-layouts: 11.6 us -> 18.6 us
    all_gather x0 -> x1, blocking collectives: none -> 34.4 us  [shards(): lax.all_gather(slots * rows_x + strip_row.reshape(-1), every, tiled=True)]
    all_to_all x2 -> x1, waiting for transfers between devices: 24.7 us -> 13.9 us  [shards(): lax.all_to_all(jnp.concatenate([rims_out, met], axis=1), every, split_axi...]
    all_to_all x2 -> x1, starting transfers between devices: 16.2 us -> 6.76 us  [shards(): lax.all_to_all(jnp.concatenate([rims_out, met], axis=1), every, split_axi...]
    scatter-add x0 -> x1, local copies, waits for them, and re-layouts: none -> 2.37 us  [shards(): forcing = forcing.at[:, depth - 3].add(top_force[:, 2][None])]
    unnamed x18 -> x13, local copies, waits for them, and re-layouts: 5.02 us -> 6.48 us
  transfers between devices with their start and end apart: 3 -> 2, of which waited for: 2 -> 1; matrix products, arithmetic and copies ran while one was open for 21% -> 19% of each run, Pallas kernels for 0% -> 0%
where the time goes in v2:
time: 171 us; the launch traced here: 170 us
  blocking collectives  70.1 us (41%)
  other arithmetic  33.1 us (19%)
  matrix products  21.9 us (13%)
  local copies, waits for them, and re-layouts  18.6 us (11%)
  waiting for transfers between devices  13.9 us (8%)
  starting transfers between devices  11.7 us (7%)
    all_to_all x1, blocking collectives, to_cells(): lax.all_to_all(part, ('gx', 'gy'), split_axis=0, concat_axis=0, tiled=True)  35.6 us
    all_gather x1, blocking collectives, shards(): lax.all_gather(slots * rows_x + strip_row.reshape(-1), every, tiled=True)  34.4 us
    mul x4, other arithmetic, cosine_table(): return scale * jnp.cos(jnp.pi * rows * (cols + 0.5) / count)  18.7 us
    all_to_all x1, waiting for transfers between devices, shards(): lax.all_to_all(jnp.concatenate([rims_out, met], axis=1), every, split_axi...  13.9 us
    mul x1, other arithmetic, advance_terms(): return (2.0 * jnp.cos(theta), COURANT * COURANT * shape * shape)  11.3 us
    dot_general x1, matrix products, to_modes(): return jnp.einsum('cjy,bjy->bc', split_y, part, precision=FAST)[None, None]  7.03 us
    all_to_all x1, starting transfers between devices, shards(): lax.all_to_all(jnp.concatenate([rims_out, met], axis=1), every, split_axi...  6.76 us
    unnamed x13, local copies, waits for them, and re-layouts  6.48 us
  transfers between devices with their start and end apart: 2, of which 1 were waited for; matrix products, arithmetic and copies ran while one was open for 19% of the time, Pallas kernels for 0%

profile of v2, /device:TPU:1, one launch (start us, length us, event | category | flops | bytes accessed | tf_op | source)
XLA Modules:
  0.0 170.2 jit_solution(3968402348808569980)
XLA Ops:
  0.6 0.9 slice.156
  1.6 0.9 fusion.66
  2.5 0.7 fusion.64
  3.2 34.4 %all-gather = s32[128,1,128]{2,1,0:T(1,128)S(1)} all-gather(s32[1,1,128]{2,1,0:T(1,128)S(1)} %fusion.64), channel_id=1, replica_groups=mesh['grp'=4,'gx'=4,'gy'=8] {'grp','gx','gy'}, dimensions={0}, use_global_device_ids=true | all-gather | bytes 66048 | tf_op jit(solution)/shard_map/all_gather | solution.py:118
  38.8 0.4 fusion.42
  39.2 0.4 fusion.43
  39.7 1.3 all_to_all.14
  41.0 6.8 %all-to-all-start = ((f32[128,2,768]{2,1,0:T(2,128)}), f32[128,2,768]{2,1,0:T(2,128)S(1)}, u32[]{:S(2)}, u32[]{:S(2)}) async-start(f32[128,2,768]{2,1,0:T(2,128)} %all_to_all.14), calls=%async_computation | async-start | bytes 1572864 | tf_op jit(solution)/shard_map/all_to_all | solution.py:129
  48.4 1.9 %copy.81 = f32[1,32,128,128]{2,3,1,0:T(8,128)S(1)} copy(f32[1,32,128,128]{3,2,1,0:T(8,128)} %param.17) | data formatting | bytes 4194304 | tf_op args[3]
  50.3 13.9 %all-to-all-done = f32[128,2,768]{2,1,0:T(2,128)S(1)} async-done(((f32[128,2,768]{2,1,0:T(2,128)}), f32[128,2,768]{2,1,0:T(2,128)S(1)}, u32[]{:S(2)}, u32[]{:S(2)}) %all-to-all-start) | async-done | bytes 786464 | tf_op jit(solution)/shard_map/all_to_all | solution.py:129
  64.2 1.4 all_to_all.16
  65.6 1.0 slice_subtract_fusion
  66.6 1.3 convolution_subtract_fusion
  68.2 0.6 fusion.31
  68.9 1.3 copy.119
  70.2 0.6 fusion.47
  70.9 2.4 %copy.85 = f32[32,128,128]{2,0,1:T(8,128)S(1)} copy(f32[32,128,128]{1,2,0:T(8,128)} %fusion.47) | data formatting | bytes 4194304 | tf_op jit(solution)/shard_map/scatter-add | solution.py:142
  73.3 1.9 %fusion.60 = f32[32,128,128]{2,0,1:T(8,128)S(1)} fusion(f32[32,128,128]{2,0,1:T(8,128)S(1)} %copy.85, f32[32,32]{0,1:T(8,128)S(1)} %cosine_multiply_fusion.3), kind=kOutput, calls=%fused_computation.97 | convolution fusion | flops 201326592 | bytes 4198400 | tf_op jit(solution)/shard_map/kz,zxy->kxy/dot_general | solution.py:38
  75.2 2.5 %copy.86 = f32[32,128,128]{2,1,0:T(8,128)} copy(f32[32,128,128]{2,0,1:T(8,128)S(1)} %fusion.60) | data formatting | bytes 4194304 | tf_op jit(solution)/shard_map/kz,zxy->kxy/dot_general | solution.py:38
  77.7 4.9 %all-to-all-start.1 = ((f32[32,128,128]{2,1,0:T(8,128)}), f32[32,128,128]{2,1,0:T(8,128)S(1)}, u32[]{:S(2)}, u32[]{:S(2)}) async-start(f32[32,128,128]{2,1,0:T(8,128)} %copy.86), calls=%async_computation.1 | async-start | bytes 4194304 | tf_op jit(solution)/shard_map/all_to_all | solution.py:39
  82.6 3.5 %cosine_multiply_fusion.2 = f32[512,512]{0,1:T(8,128)S(1)} fusion(f32[512]{0:T(512)S(1)} %get-tuple-element.75, f32[512]{0:T(512)S(1)} %get-tuple-element.76, f32[512]{0:T(512)S(1)} %fusion.63), kind=kLoop, calls=%fused_computation.42 | loop fusion | flops 786432 | bytes 1054720 | tf_op jit(solution)/shard_map/mul | solution.py:16
  86.2 15.1 %cosine_multiply_fusion = f32[1024,1024]{0,1:T(8,128)} fusion(f32[1024]{0:T(1024)S(1)} %get-tuple-element.73, f32[1024]{0:T(1024)S(1)} %get-tuple-element.74, f32[1024]{0:T(1024)S(1)} %fusion.62), kind=kLoop, calls=%fused_computation | loop fusion | flops 3145728 | bytes 4206592 | tf_op jit(solution)/shard_map/mul | solution.py:16
  101.3 11.3 %cosine_multiply_fusion.1 = (f32[1,512,1024]{2,1,0:T(8,128)}, f32[1,512,1024]{2,1,0:T(8,128)}) fusion(f32[1024]{0:T(1024)S(1)} %multiply_multiply_fusion.5, f32[512]{0:T(512)S(1)} %multiply_add_fusion.3), kind=kLoop, calls=%fused_computation.37 | loop fusion | flops 20447232 | bytes 4200448 | tf_op jit(solution)/shard_map/mul | solution.py:73
  112.6 1.9 %fusion.67 = f32[512,8,128,1]{2,0,1,3:T(8,128)S(1)} fusion(f32[512,4,128,1]{0,2,3,1:T(8,128)S(1)} %bitcast.112, f32[4,8,128,128]{3,2,1,0:T(8,128)S(1)} %bitcast.114), kind=kOutput, calls=%fused_computation.119 | convolution fusion | flops 1610612736 | bytes 5242880 | tf_op jit(solution)/shard_map/bix,ijxy->bjy/dot_general | solution.py:43
  114.5 0.3 copy-done
  114.8 7.0 %fusion.13 = f32[1,512,1024]{2,1,0:T(8,128)S(1)} fusion(f32[1,512,1024]{2,1,0:T(8,128)} %get-tuple-element.72, f32[1,1,512,1024]{3,2,1,0:T(8,128)} %param.15, f32[1,512,1024]{2,1,0:T(8,128)} %get-tuple-element.71, f32[1,1,512,1024]{3,2,1,0:T(8,128)} %param.14, f32[1024,8,128]{0,2,1:T(8,128)S(1)} %bitcast.109, f32[512,8,128,1]{2,0,1,3:T(8,128)S(1)} %fusion.67), kind=kOutput, calls=%fused_computation.22 | convolution fusion | flops 3223322624 | bytes 16777216 | tf_op jit(solution)/shard_map/cjy,bjy->bc/dot_general | solution.py:44
  121.8 3.5 %fusion.11 = f32[512,8,128]{0,2,1:T(8,128)S(1)} fusion(f32[1024,8,128]{0,2,1:T(8,128)S(1)} %bitcast.110, f32[1,512,1024]{2,1,0:T(8,128)S(1)} %fusion.13), kind=kOutput, calls=%fused_computation.19 | convolution fusion | flops 3221225472 | bytes 8388608 | tf_op jit(solution)/shard_map/cjy,bc->bjy/dot_general | solution.py:54
  125.4 1.8 %fusion.24 = f32[4,8,128,128]{2,3,0,1:T(8,128)S(1)} fusion(f32[512,4,128,1]{0,2,1,3:T(8,128)S(1)} %bitcast.113, f32[512,8,128]{0,2,1:T(8,128)S(1)} %fusion.11), kind=kOutput, calls=%fused_computation.40 | convolution fusion | flops 1610612736 | bytes 5242880 | tf_op jit(solution)/shard_map/bix,bjy->ijxy/dot_general | solution.py:55
  127.2 1.8 %copy.93 = f32[4,8,128,128]{3,2,1,0:T(8,128)} copy(f32[4,8,128,128]{2,3,0,1:T(8,128)S(1)} %fusion.24) | data formatting | bytes 4194304 | tf_op jit(solution)/shard_map/bix,bjy->ijxy/transpose | solution.py:55
  129.1 35.6 %all_to_all.22 = f32[32,128,128]{2,1,0:T(8,128)S(1)} all-to-all(f32[32,128,128]{2,1,0:T(8,128)} %bitcast.115), channel_id=1, replica_groups=mesh['grp'=4,'gx'=4,'gy'=8] {'gx','gy'}, dimensions={0} | all-to-all | bytes 4194304 | tf_op jit(solution)/shard_map/all_to_all | solution.py:57
  164.7 3.0 %fusion.21 = f32[1,32,128,128]{3,1,2,0:T(8,128)S(1)} fusion(f32[32,128,128]{2,1,0:T(8,128)S(1)} %all_to_all.22, f32[32,32]{0,1:T(8,128)S(1)} %cosine_multiply_fusion.3), kind=kOutput, calls=%fused_computation.39 | convolution fusion | flops 201326592 | bytes 4198400 | tf_op jit(solution)/shard_map/kz,kxy->zxy/dot_general | solution.py:58
  167.7 2.5 %copy.95 = f32[1,32,128,128]{3,2,1,0:T(8,128)} copy(f32[1,32,128,128]{3,1,2,0:T(8,128)S(1)} %fusion.21) | data formatting | bytes 4194304
  (39 shorter events, 2.0 us)
Async XLA Ops:
  0.6 38.5 %copy-start.2 = (s32[1,128,1]{1,2,0:T(1,128)S(1)}, s32[1,128,1]{1,2,0:T(1,128)}, u32[]{:S(2)}) copy-start(s32[1,128,1]{1,2,0:T(1,128)} %param.18) | copy-start | bytes 1540
  41.0 23.2 %all-to-all-start = ((f32[128,2,768]{2,1,0:T(2,128)}), f32[128,2,768]{2,1,0:T(2,128)S(1)}, u32[]{:S(2)}, u32[]{:S(2)}) async-start(f32[128,2,768]{2,1,0:T(2,128)} %all_to_all.14), calls=%async_computation | async-start | bytes 1572864 | tf_op jit(solution)/shard_map/all_to_all | solution.py:129
  77.7 34.9 %all-to-all-start.1 = ((f32[32,128,128]{2,1,0:T(8,128)}), f32[32,128,128]{2,1,0:T(8,128)S(1)}, u32[]{:S(2)}, u32[]{:S(2)}) async-start(f32[32,128,128]{2,1,0:T(8,128)} %copy.86), calls=%async_computation.1 | async-start | bytes 4194304 | tf_op jit(solution)/shard_map/all_to_all | solution.py:39
  112.6 2.2 %copy-start = (f32[1024,1024]{0,1:T(8,128)S(1)}, f32[1024,1024]{0,1:T(8,128)}, u32[]{:S(2)}) copy-start(f32[1024,1024]{0,1:T(8,128)} %cosine_multiply_fusion) | copy-start | bytes 12582916
  121.8 3.6 %copy-start.1 = (f32[1,512,1024]{2,1,0:T(8,128)}, f32[1,512,1024]{2,1,0:T(8,128)S(1)}, u32[]{:S(2)}) copy-start(f32[1,512,1024]{2,1,0:T(8,128)S(1)} %fusion.13) | copy-start | bytes 6291460

commit v3 on v2

--- a/solution.py
+++ b/solution.py
@@ -115,8 +115,10 @@
     slots_per = max(2, rows_x // devices)
     total = devices * slots_per
     slots = strip_slot.reshape(-1)
-    codes = lax.all_gather(slots * rows_x + strip_row.reshape(-1), every, tiled=True)
-    codes = codes.reshape(devices, rows_x)
+    mine = (slots * rows_x + strip_row.reshape(-1)).astype(jnp.float32)
+    owner = jnp.arange(devices, dtype=jnp.int32)[:, None] == lax.axis_index(every)
+    codes = lax.psum(jnp.where(owner, mine[None, :], 0.0), every)
+    codes = jnp.round(codes).astype(jnp.int32)
     want = lax.axis_index(every) * slots_per + jnp.arange(slots_per, dtype=jnp.int32)
     hit = (codes // rows_x)[:, :, None] == want[None, None, :]
     found = jnp.any(hit, axis=1).reshape(total)

time: 171 us -> 295 us (1.73)
  waiting for transfers between devices: 13.9 us -> 157 us
  blocking collectives: 70.1 us -> 35.6 us
  between operations: 0.99 us -> 14.4 us
    psum x0 -> x1, waiting for transfers between devices: none -> 145 us  [shards(): codes = lax.psum(jnp.where(owner, mine[None, :], 0.0), every)]
    all_gather x1 -> x0, blocking collectives: 34.4 us -> none  [shards(): lax.all_gather(slots * rows_x + strip_row.reshape(-1), every, tiled=True)]
    unnamed x13 -> x19, local copies, waits for them, and re-layouts: 6.48 us -> 7.02 us
  transfers between devices with their start and end apart: 2 -> 3, of which waited for: 1 -> 2; matrix products, arithmetic and copies ran while one was open for 19% -> 12% of each run, Pallas kernels for 0% -> 0%
where the time goes in v3:
time: 295 us
  waiting for transfers between devices  157 us (53%)
  blocking collectives  35.6 us (12%)
  other arithmetic  35.3 us (12%)
  matrix products  22.6 us (8%)
  local copies, waits for them, and re-layouts  19.4 us (7%)
  between operations  14.4 us (5%)
  starting transfers between devices  10 us (3%)
    psum x1, waiting for transfers between devices, shards(): codes = lax.psum(jnp.where(owner, mine[None, :], 0.0), every)  145 us
    all_to_all x1, blocking collectives, to_cells(): lax.all_to_all(part, ('gx', 'gy'), split_axis=0, concat_axis=0, tiled=True)  35.6 us
    mul x4, other arithmetic, cosine_table(): return scale * jnp.cos(jnp.pi * rows * (cols + 0.5) / count)  18.7 us
    all_to_all x1, waiting for transfers between devices, shards(): lax.all_to_all(jnp.concatenate([rims_out, met], axis=1), every, split_axi...  12.1 us
    mul x1, other arithmetic, advance_terms(): return (2.0 * jnp.cos(theta), COURANT * COURANT * shape * shape)  11.3 us
    dot_general x1, matrix products, to_modes(): return jnp.einsum('cjy,bjy->bc', split_y, part, precision=FAST)[None, None]  7.03 us
    unnamed x19, local copies, waits for them, and re-layouts  7.02 us
  transfers between devices with their start and end apart: 3, of which 2 were waited for; matrix products, arithmetic and copies ran while one was open for 12% of the time, Pallas kernels for 0%

profile of v3, /device:TPU:1, one launch (start us, length us, event | category | flops | bytes accessed | tf_op | source)
XLA Modules:
  0.0 294.6 jit_solution(2548714859366596820)
XLA Ops:
  7.2 0.7 fusion.64
  8.0 0.7 broadcast_select_fusion
  8.7 0.9 fusion.66
  9.9 1.1 fusion.43
  11.2 145.1 %all-reduce.2.cloned.1.call-done = f32[128,128]{1,0:T(8,128)} async-done(((f32[128,128]{1,0:T(8,128)}), f32[128,128]{1,0:T(8,128)}) %all-reduce.2.cloned.1.call-update) | async-done | bytes 65552 | tf_op jit(solution)/shard_map/psum | solution.py:120
  156.3 0.9 add_select_fusion
  158.8 1.3 all_to_all.14
  160.1 5.1 %all-to-all-start = ((f32[128,2,768]{2,1,0:T(2,128)}), f32[128,2,768]{2,1,0:T(2,128)S(1)}, u32[]{:S(2)}, u32[]{:S(2)}) async-start(f32[128,2,768]{2,1,0:T(2,128)} %all_to_all.14), calls=%async_computation | async-start | bytes 1572864 | tf_op jit(solution)/shard_map/all_to_all | solution.py:131
  165.5 1.9 copy.81
  168.0 0.8 copy.79
  168.8 0.7 reshape.563
  169.5 12.1 %all-to-all-done = f32[128,2,768]{2,1,0:T(2,128)S(1)} async-done(((f32[128,2,768]{2,1,0:T(2,128)}), f32[128,2,768]{2,1,0:T(2,128)S(1)}, u32[]{:S(2)}, u32[]{:S(2)}) %all-to-all-start) | async-done | bytes 786464 | tf_op jit(solution)/shard_map/all_to_all | solution.py:131
  181.6 1.4 all_to_all.16
  183.1 1.1 slice_subtract_fusion
  184.1 1.3 convolution_subtract_fusion
  186.4 1.3 copy.120
  187.7 0.6 fusion.47
  188.4 2.4 copy.85
  190.8 1.9 fusion.60
  192.7 2.6 copy.86
  195.2 4.9 %all-to-all-start.1 = ((f32[32,128,128]{2,1,0:T(8,128)}), f32[32,128,128]{2,1,0:T(8,128)S(1)}, u32[]{:S(2)}, u32[]{:S(2)}) async-start(f32[32,128,128]{2,1,0:T(8,128)} %copy.86), calls=%async_computation.1 | async-start | bytes 4194304 | tf_op jit(solution)/shard_map/all_to_all | solution.py:39
  200.2 3.5 %cosine_multiply_fusion.2 = f32[512,512]{0,1:T(8,128)S(1)} fusion(f32[512]{0:T(512)S(1)} %get-tuple-element.75, f32[512]{0:T(512)S(1)} %get-tuple-element.76, f32[512]{0:T(512)S(1)} %fusion.63), kind=kLoop, calls=%fused_computation.42 | loop fusion | flops 786432 | bytes 1054720 | tf_op jit(solution)/shard_map/mul | solution.py:16
  203.7 15.1 %cosine_multiply_fusion = f32[1024,1024]{0,1:T(8,128)} fusion(f32[1024]{0:T(1024)S(1)} %get-tuple-element.73, f32[1024]{0:T(1024)S(1)} %get-tuple-element.74, f32[1024]{0:T(1024)S(1)} %fusion.62), kind=kLoop, calls=%fused_computation | loop fusion | flops 3145728 | bytes 4206592 | tf_op jit(solution)/shard_map/mul | solution.py:16
  218.8 11.3 %cosine_multiply_fusion.1 = (f32[1,512,1024]{2,1,0:T(8,128)}, f32[1,512,1024]{2,1,0:T(8,128)}) fusion(f32[1024]{0:T(1024)S(1)} %multiply_multiply_fusion.5, f32[512]{0:T(512)S(1)} %multiply_add_fusion.3), kind=kLoop, calls=%fused_computation.37 | loop fusion | flops 20447232 | bytes 4200448 | tf_op jit(solution)/shard_map/mul | solution.py:73
  230.1 1.9 fusion.67
  232.3 7.0 %fusion.13 = f32[1,512,1024]{2,1,0:T(8,128)S(1)} fusion(f32[1,512,1024]{2,1,0:T(8,128)} %get-tuple-element.72, f32[1,1,512,1024]{3,2,1,0:T(8,128)} %param.15, f32[1,512,1024]{2,1,0:T(8,128)} %get-tuple-element.71, f32[1,1,512,1024]{3,2,1,0:T(8,128)} %param.14, f32[1024,8,128]{0,2,1:T(8,128)S(1)} %bitcast.106, f32[512,8,128,1]{2,0,1,3:T(8,128)S(1)} %fusion.67), kind=kOutput, calls=%fused_computation.22 | convolution fusion | flops 3223322624 | bytes 16777216 | tf_op jit(solution)/shard_map/cjy,bjy->bc/dot_general | solution.py:44
  239.4 3.5 %fusion.11 = f32[512,8,128]{0,2,1:T(8,128)S(1)} fusion(f32[1024,8,128]{0,2,1:T(8,128)S(1)} %bitcast.107, f32[1,512,1024]{2,1,0:T(8,128)S(1)} %fusion.13), kind=kOutput, calls=%fused_computation.19 | convolution fusion | flops 3221225472 | bytes 8388608 | tf_op jit(solution)/shard_map/cjy,bc->bjy/dot_general | solution.py:54
  242.9 1.8 fusion.24
  244.8 1.8 copy.93
  246.6 35.6 %all_to_all.22 = f32[32,128,128]{2,1,0:T(8,128)S(1)} all-to-all(f32[32,128,128]{2,1,0:T(8,128)} %bitcast.112), channel_id=1, replica_groups=mesh['grp'=4,'gx'=4,'gy'=8] {'gx','gy'}, dimensions={0} | all-to-all | bytes 4194304 | tf_op jit(solution)/shard_map/all_to_all | solution.py:57
  282.2 3.0 %fusion.21 = f32[1,32,128,128]{3,1,2,0:T(8,128)S(1)} fusion(f32[32,128,128]{2,1,0:T(8,128)S(1)} %all_to_all.22, f32[32,32]{0,1:T(8,128)S(1)} %cosine_multiply_fusion.3), kind=kOutput, calls=%fused_computation.39 | convolution fusion | flops 201326592 | bytes 4198400 | tf_op jit(solution)/shard_map/kz,kxy->zxy/dot_general | solution.py:58
  285.2 2.5 copy.95
  (50 shorter events, 4.1 us)
Async XLA Ops:
  7.2 3.9 %slice-start = ((f32[1,32,128,128]{3,2,1,0:T(8,128)}), f32[1,3,128,128]{3,2,1,0:T(8,128)S(1)}, s32[]{:S(2)}) async-start(f32[1,32,128,128]{3,2,1,0:T(8,128)} %param.16), calls=%async_computation.4 | async-start | bytes 393216 | tf_op jit(solution)/shard_map/slice | solution.py:112
  7.2 149.1 %all-reduce.2.cloned.1.call-start = ((), (), s32[]{:S(2)}) async-start(), calls=%async_computation.3 | async-start | bytes 131072 | tf_op jit(solution)/shard_map/psum | solution.py:120
  157.8 0.5 copy-start.2
  160.1 21.5 %all-to-all-start = ((f32[128,2,768]{2,1,0:T(2,128)}), f32[128,2,768]{2,1,0:T(2,128)S(1)}, u32[]{:S(2)}, u32[]{:S(2)}) async-start(f32[128,2,768]{2,1,0:T(2,128)} %all_to_all.14), calls=%async_computation | async-start | bytes 1572864 | tf_op jit(solution)/shard_map/all_to_all | solution.py:131
  169.5 14.6 %copy-start.4 = (s32[1,128,1]{1,2,0:T(1,128)S(1)}, s32[1,128,1]{1,2,0:T(1,128)}, u32[]{:S(2)}) copy-start(s32[1,128,1]{1,2,0:T(1,128)} %param.18) | copy-start | bytes 1540
  183.0 2.7 copy-start.3
  183.1 2.7 copy-start.5
  195.2 34.9 %all-to-all-start.1 = ((f32[32,128,128]{2,1,0:T(8,128)}), f32[32,128,128]{2,1,0:T(8,128)S(1)}, u32[]{:S(2)}, u32[]{:S(2)}) async-start(f32[32,128,128]{2,1,0:T(8,128)} %copy.86), calls=%async_computation.1 | async-start | bytes 4194304 | tf_op jit(solution)/shard_map/all_to_all | solution.py:39
  230.1 2.2 copy-start
  239.4 3.6 %copy-start.1 = (f32[1,512,1024]{2,1,0:T(8,128)}, f32[1,512,1024]{2,1,0:T(8,128)S(1)}, u32[]{:S(2)}) copy-start(f32[1,512,1024]{2,1,0:T(8,128)S(1)} %fusion.13) | copy-start | bytes 6291460
Sparse Core Ops, SparseCore 0:
  13.3 142.9 all-reduce.1

commit v4 on v1

--- a/solution.py
+++ b/solution.py
@@ -30,12 +30,12 @@
     )
 
 
-def to_modes(field, table_z, table_x, table_y):
+def to_modes(zsource, layers, table_edge, table_x, table_y):
     width_x = lax.axis_size("gx")
     width_y = lax.axis_size("gy")
-    rows_x = field.shape[2]
-    cols_y = field.shape[3]
-    part = jnp.einsum("kz,zxy->kxy", table_z, field[0], precision=HIGH)
+    rows_x = zsource.shape[1]
+    cols_y = zsource.shape[2]
+    part = zsource + jnp.einsum("kz,zxy->kxy", table_edge, layers, precision=HIGH)
     part = lax.all_to_all(part, ("gx", "gy"), split_axis=0, concat_axis=0, tiled=True)
     part = part.reshape(width_x, width_y, rows_x, cols_y)
     split_x = table_x.reshape(table_x.shape[0], width_x, rows_x)
@@ -49,13 +49,14 @@
     width_y = lax.axis_size("gy")
     rows_x = modes.shape[2] // width_x
     cols_y = modes.shape[3] // width_y
-    split_x = table_x.reshape(table_x.shape[0], width_x, rows_x)
     split_y = table_y.reshape(table_y.shape[0], width_y, cols_y)
-    part = jnp.einsum("cjy,bc->bjy", split_y, modes[0, 0], precision=FAST)
-    part = jnp.einsum("bix,bjy->ijxy", split_x, part, precision=FAST)
+    part = jnp.einsum("cjy,bc->jby", split_y, modes[0, 0], precision=FAST)
+    part = jnp.einsum("bn,jby->jny", table_x, part, precision=FAST)
     part = part.reshape(width_x * width_y, rows_x, cols_y)
-    cells = lax.all_to_all(part, ("gx", "gy"), split_axis=0, concat_axis=0, tiled=True)
-    return jnp.einsum("kz,kxy->zxy", table_z, cells, precision=HIGH)[None]
+    cells = lax.all_to_all(part, ("gy", "gx"), split_axis=0, concat_axis=0, tiled=True)
+    depth = table_z.shape[1]
+    table_p = table_z.reshape(width_x, width_y, depth).transpose(1, 0, 2).reshape(-1, depth)
+    return jnp.einsum("kz,kxy->zxy", table_p, cells, precision=HIGH)[None]
 
 
 def advance_terms(depth_index, depth, long_x, long_y):
@@ -90,8 +91,11 @@
     table_x = lax.optimization_barrier(cosine_table(long_x))
     table_y = lax.optimization_barrier(cosine_table(long_y))
     scale_now, scale_spec = advance_terms(depth_index, depth, long_x, long_y)
-    scale_now = lax.optimization_barrier(scale_now)
+    base = lax.optimization_barrier(scale_now * modes_now[0] - modes_old[0])
     scale_spec = lax.optimization_barrier(scale_spec)
+    zsource = lax.optimization_barrier(
+        jnp.einsum("kz,zxy->kxy", table_z, source[0], precision=HIGH)
+    )
     top = jnp.stack(
         [pressure_now[0, depth - 1], pressure_now[0, depth - 2], pressure_now[0, depth - 3]], axis=1
     ).reshape(rows_x, 3 * cols_y)
@@ -126,12 +130,19 @@
     back = lax.all_to_all(force, ("grp", "gx", "gy"), split_axis=0, concat_axis=0, tiled=True)
     top_force = jnp.einsum("sk,kf->sf", send, back, precision=HIGH).reshape(rows_x, 3, cols_y)
     bottom_force = jnp.einsum("kr,kf->rf", meet, -force, precision=HIGH).reshape(rows_x, 3, cols_y)
-    forcing = source.at[:, 0:3].add(jnp.transpose(bottom_force, (1, 0, 2))[None])
-    forcing = forcing.at[:, depth - 1].add(top_force[:, 0][None])
-    forcing = forcing.at[:, depth - 2].add(top_force[:, 1][None])
-    forcing = forcing.at[:, depth - 3].add(top_force[:, 2][None])
-    spectrum = to_modes(forcing, table_z, table_x, table_y)
-    modes_new = (scale_now * modes_now[0] - modes_old[0] + scale_spec * spectrum[0])[None]
+    table_x, top_force = lax.optimization_barrier((table_x, top_force))
+    layers = jnp.concatenate(
+        [
+            jnp.transpose(bottom_force, (1, 0, 2)),
+            top_force[:, 2][None],
+            top_force[:, 1][None],
+            top_force[:, 0][None],
+        ],
+        axis=0,
+    )
+    edges = jnp.concatenate([table_z[:, :3], table_z[:, depth - 3 :]], axis=1)
+    spectrum = to_modes(zsource, layers, edges, table_x, table_y)
+    modes_new = (base + scale_spec * spectrum[0])[None]
     pressure_next = to_cells(modes_new, table_z, table_x, table_y)
     return (modes_new, pressure_next)
 

time: 148 us -> 159 us (1.074)
  blocking collectives: 35.6 us -> 0 us
  waiting for transfers between devices: 24.7 us -> 35 us
  matrix products: 22.1 us -> 32.4 us
  other arithmetic: 31.5 us -> 41.7 us
  starting transfers between devices: 21.1 us -> 29.1 us
  local copies, waits for them, and re-layouts: 11.6 us -> 19.3 us
    all_to_all x1 -> x0, blocking collectives: 35.6 us -> none  [to_cells(): lax.all_to_all(part, ('gx', 'gy'), split_axis=0, concat_axis=0, tiled=True)]
    all_to_all x0 -> x1, waiting for transfers between devices: none -> 21.6 us  [to_cells(): lax.all_to_all(part, ('gy', 'gx'), split_axis=0, concat_axis=0, tiled=True)]
    all_to_all x1, waiting for transfers between devices: 13.2 us -> 4.96 us  [shards(): lax.all_to_all(buffer, ('grp', 'gx', 'gy'), split_axis=0, concat_axis=0,...]
    dot_general x4 -> x5, matrix products: 11.4 us -> 19.4 us  [the longest x1 4.56 us: to_cells(): return jnp.einsum('kz,kxy->zxy', table_p, cells, precision=HIGH)[None]]
    all_to_all x0 -> x1, starting transfers between devices: none -> 6.72 us  [to_cells(): lax.all_to_all(part, ('gy', 'gx'), split_axis=0, concat_axis=0, tiled=True)]
    broadcast_in_dim x0 -> x1, other arithmetic: none -> 5.05 us  [shards(): modes_new = (base + scale_spec * spectrum[0])[None]]
    all_to_all x1, waiting for transfers between devices: 11.4 us -> 7.53 us  [shards(): lax.all_to_all(force, ('grp', 'gx', 'gy'), split_axis=0, concat_axis=0, t...]
    dot_general x1, matrix products: 7.03 us -> 3.56 us  [to_modes(): return jnp.einsum('cjy,bjy->bc', split_y, part, precision=FAST)[None, None]]
  transfers between devices with their start and end apart: 3 -> 4, of which waited for: 2 -> 4; matrix products, arithmetic and copies ran while one was open for 21% -> 29% of each run, Pallas kernels for 0% -> 0%
where the time goes in v4:
time: 159 us; the launch traced here: 158 us
  other arithmetic  41.7 us (26%)
  waiting for transfers between devices  35 us (22%)
  matrix products  32.4 us (20%)
  starting transfers between devices  29.1 us (18%)
  local copies, waits for them, and re-layouts  19.3 us (12%)
    all_to_all x1, waiting for transfers between devices, to_cells(): lax.all_to_all(part, ('gy', 'gx'), split_axis=0, concat_axis=0, tiled=True)  21.6 us
    mul x4, other arithmetic, cosine_table(): return scale * jnp.cos(jnp.pi * rows * (cols + 0.5) / count)  18.8 us
    mul x1, other arithmetic, advance_terms(): return (2.0 * jnp.cos(theta), COURANT * COURANT * shape * shape)  12.5 us
    all_to_all x1, starting transfers between devices, shards(): lax.all_to_all(buffer, ('grp', 'gx', 'gy'), split_axis=0, concat_axis=0,...  11.9 us
    all_to_all x1, waiting for transfers between devices, shards(): lax.all_to_all(force, ('grp', 'gx', 'gy'), split_axis=0, concat_axis=0, t...  7.53 us
    all_to_all x1, starting transfers between devices, to_cells(): lax.all_to_all(part, ('gy', 'gx'), split_axis=0, concat_axis=0, tiled=True)  6.72 us
    all_to_all x1, starting transfers between devices, to_modes(): lax.all_to_all(part, ('gx', 'gy'), split_axis=0, concat_axis=0, tiled=True)  5.59 us
    broadcast_in_dim x1, other arithmetic, shards(): modes_new = (base + scale_spec * spectrum[0])[None]  5.05 us
  transfers between devices with their start and end apart: 4, of which 4 were waited for; matrix products, arithmetic and copies ran while one was open for 29% of the time, Pallas kernels for 0%

profile of v4, /device:TPU:1, one launch (start us, length us, event | category | flops | bytes accessed | tf_op | source)
XLA Modules:
  0.0 158.4 jit_solution(1845560338602053639)
XLA Ops:
  2.7 1.1 fusion.48
  3.9 1.1 all_to_all.20
  5.0 11.9 %all-to-all-start = ((f32[128,2,512]{2,1,0:T(2,128)}), f32[128,2,512]{2,1,0:T(2,128)}, u32[]{:S(2)}, u32[]{:S(2)}) async-start(f32[128,2,512]{2,1,0:T(2,128)} %all_to_all.20), calls=%async_computation | async-start | bytes 1048576 | tf_op jit(solution)/shard_map/all_to_all | solution.py:112
  17.2 3.6 %cosine_multiply_fusion.1 = f32[512,512]{1,0:T(8,128)S(1)} fusion(f32[512]{0:T(512)S(1)} %get-tuple-element.27, f32[512]{0:T(512)S(1)} %get-tuple-element.28, f32[512]{0:T(512)S(1)} %fusion.70), kind=kLoop, calls=%fused_computation.49 | loop fusion | flops 786432 | bytes 1054720 | tf_op jit(solution)/shard_map/mul | solution.py:16
  20.8 4.3 %fusion.16 = f32[32,128,128]{2,0,1:T(8,128)} fusion(f32[32,128,128]{2,1,0:T(8,128)S(1)} %bitcast.106, f32[32,32]{0,1:T(8,128)S(1)} %cosine_multiply_fusion.2), kind=kOutput, calls=%fused_computation.27 | convolution fusion | flops 201326592 | bytes 4198400 | tf_op jit(solution)/shard_map/kz,zxy->kxy/dot_general | solution.py:97
  25.1 5.0 %all-to-all-done = f32[128,2,512]{2,1,0:T(2,128)} async-done(((f32[128,2,512]{2,1,0:T(2,128)}), f32[128,2,512]{2,1,0:T(2,128)}, u32[]{:S(2)}, u32[]{:S(2)}) %all-to-all-start) | async-done | bytes 524320 | tf_op jit(solution)/shard_map/all_to_all | solution.py:112
  30.1 2.2 %all_to_all.22 = f32[256,512]{1,0:T(8,128)} reshape(f32[128,2,512]{2,1,0:T(2,128)} %all-to-all-done) | data formatting | bytes 1048576 | tf_op jit(solution)/shard_map/all_to_all | solution.py:112
  32.3 1.6 %convert_reduce_fusion = f32[256]{0:T(256)} fusion(f32[256,512]{1,0:T(8,128)} %all_to_all.22), kind=kLoop, calls=%fused_computation.76 | loop fusion | flops 1280 | bytes 2048 | tf_op jit(solution)/shard_map/convert_element_type | solution.py:115
  35.5 1.4 convolution_subtract_fusion
  37.0 1.4 mul.390
  38.4 1.8 %maximum_multiply_fusion = f32[128,2,384]{2,1,0:T(2,128)} fusion(f32[128,2,128]{2,1,0:T(2,128)S(1)} %bitcast.116, f32[128,2,128]{2,1,0:T(2,128)S(1)} %bitcast.115, f32[128,2,128]{2,1,0:T(2,128)S(1)} %bitcast.114, f32[128,2]{1,0:T(8,128)} %mul.390), kind=kLoop, calls=%fused_computation.57 | loop fusion | flops 294912 | bytes 787456 | tf_op jit(solution)/shard_map/mul | solution.py:122
  40.2 4.8 %all-to-all-start.1 = ((f32[128,2,384]{2,1,0:T(2,128)}), f32[128,2,384]{2,1,0:T(2,128)S(1)}, u32[]{:S(2)}, u32[]{:S(2)}) async-start(f32[128,2,384]{2,1,0:T(2,128)} %maximum_multiply_fusion), calls=%async_computation.1 | async-start | bytes 786432 | tf_op jit(solution)/shard_map/all_to_all | solution.py:130
  45.6 2.3 %fusion.42 = f32[128,384]{0,1:T(8,128)} fusion(f32[256,128]{1,0:T(8,128)} %copy-done.7, f32[256,128]{1,0:T(8,128)} %copy-done.6, f32[256,128]{1,0:T(8,128)} %copy-done.5, f32[256]{0:T(256)} %convert_reduce_fusion, s32[256]{0:T(256)} %copy-done.8), kind=kOutput, calls=%fused_computation.60 | convolution fusion | flops 151420928 | bytes 591872 | tf_op jit(solution)/shard_map/kr,kf->rf/dot_general | solution.py:132
  47.9 1.8 %copy.66 = f32[128,3,128]{2,1,0:T(4,128)} copy(f32[128,3,128]{0,2,1:T(8,128)} %bitcast.123) | data formatting | bytes 393216 | tf_op jit(solution)/shard_map/reshape | solution.py:132
  49.7 7.5 %all-to-all-done.1 = f32[128,2,384]{2,1,0:T(2,128)S(1)} async-done(((f32[128,2,384]{2,1,0:T(2,128)}), f32[128,2,384]{2,1,0:T(2,128)S(1)}, u32[]{:S(2)}, u32[]{:S(2)}) %all-to-all-start.1) | async-done | bytes 393248 | tf_op jit(solution)/shard_map/all_to_all | solution.py:130
  57.2 1.0 all_to_all.24
  58.2 1.2 copy.62
  60.4 3.8 %convolution_add_fusion = f32[32,128,128]{2,0,1:T(8,128)S(1)} fusion(f32[32,128,128]{2,0,1:T(8,128)} %fusion.16, f32[1,128,128]{2,0,1:T(1,128)S(1)} %bitcast.118, f32[1,128,128]{2,0,1:T(1,128)S(1)} %bitcast.119, f32[1,128,128]{2,0,1:T(1,128)S(1)} %bitcast.117, f32[3,128,128]{2,0,1:T(4,128)} %bitcast.111, f32[32,3]{0,1:T(4,128)} %get-tuple-element.24, ...), kind=kOutput, calls=%fused_computation.43 | convolution fusion | flops 38568128 | bytes 4588288 | tf_op jit(solution)/shard_map/kz,zxy->kxy/dot_general | solution.py:38
  64.3 2.6 %copy.70 = f32[32,128,128]{2,1,0:T(8,128)} copy(f32[32,128,128]{2,0,1:T(8,128)S(1)} %convolution_add_fusion) | data formatting | bytes 4194304 | tf_op jit(solution)/shard_map/add | solution.py:38
  66.8 5.6 %all-to-all-start.2 = ((f32[32,128,128]{2,1,0:T(8,128)}), f32[32,128,128]{2,1,0:T(8,128)}, u32[]{:S(2)}, u32[]{:S(2)}) async-start(f32[32,128,128]{2,1,0:T(8,128)} %copy.70), calls=%async_computation.2 | async-start | bytes 4194304 | tf_op jit(solution)/shard_map/all_to_all | solution.py:39
  72.5 15.1 %cosine_multiply_fusion = f32[1024,1024]{0,1:T(8,128)} fusion(f32[1024]{0:T(1024)S(1)} %get-tuple-element.29, f32[1024]{0:T(1024)S(1)} %get-tuple-element.30, f32[1024]{0:T(1024)S(1)} %fusion.69), kind=kLoop, calls=%fused_computation | loop fusion | flops 3145728 | bytes 4206592 | tf_op jit(solution)/shard_map/mul | solution.py:16
  87.5 12.5 %multiply_multiply_fusion = (f32[1,512,1024]{2,1,0:T(8,128)}, f32[1,512,1024]{2,1,0:T(8,128)}) fusion(f32[1024]{0:T(1024)S(1)} %multiply_multiply_fusion.5, f32[512]{0:T(512)S(1)} %multiply_add_fusion.2, f32[1,1,512,1024]{3,2,1,0:T(8,128)} %param.7, f32[1,1,512,1024]{3,2,1,0:T(8,128)} %param.6), kind=kLoop, calls=%fused_computation.1 | loop fusion | flops 21495808 | bytes 8394752 | tf_op jit(solution)/shard_map/mul | solution.py:74
  100.9 3.6 %fusion.31 = f32[512,8,128,1]{2,0,1,3:T(8,128)S(1)} fusion(f32[4,8,128,128]{3,2,1,0:T(8,128)} %bitcast.29, f32[512,512]{1,0:T(8,128)S(1)} %cosine_multiply_fusion.1), kind=kOutput, calls=%fused_computation.46 | convolution fusion | flops 1610612736 | bytes 5242880 | tf_op jit(solution)/shard_map/bix,ijxy->bjy/dot_general | solution.py:43
  104.6 3.6 %fusion.7 = f32[512,1024,1]{1,0,2:T(8,128)S(1)} fusion(f32[1024,8,128]{0,2,1:T(8,128)S(1)} %bitcast.107, f32[512,8,128,1]{2,0,1,3:T(8,128)S(1)} %fusion.31), kind=kOutput, calls=%fused_computation.15 | convolution fusion | flops 3221225472 | bytes 8388608 | tf_op jit(solution)/shard_map/cjy,bjy->bc/dot_general | solution.py:44
  108.2 3.6 %fusion.11 = f32[512,8,128]{2,0,1:T(8,128)S(1)} fusion(f32[1024,8,128]{0,2,1:T(8,128)S(1)} %bitcast.108, f32[1,512,1024]{2,1,0:T(8,128)S(1)} %copy-done.3, f32[1,512,1024]{2,1,0:T(8,128)S(1)} %copy-done.2, f32[512,1024,1]{1,0,2:T(8,128)S(1)} %fusion.7), kind=kOutput, calls=%fused_computation.19 | convolution fusion | flops 3222274048 | bytes 12582912 | tf_op jit(solution)/shard_map/cjy,bc->jby/dot_general | solution.py:53
  111.7 3.2 %fusion.28 = f32[8,512,128]{1,2,0:T(8,128)} fusion(f32[512,8,128]{2,0,1:T(8,128)S(1)} %fusion.11, f32[512,512]{1,0:T(8,128)S(1)} %cosine_multiply_fusion.1), kind=kOutput, calls=%fused_computation.42 | convolution fusion | flops 1610612736 | bytes 5242880 | tf_op jit(solution)/shard_map/bn,jby->jny/dot_general | solution.py:54
  114.9 2.9 %copy.78 = f32[8,512,128]{2,1,0:T(8,128)} copy(f32[8,512,128]{1,2,0:T(8,128)} %fusion.28) | data formatting | bytes 4194304 | tf_op jit(solution)/shard_map/bn,jby->jny/transpose | solution.py:54
  117.8 6.7 %all-to-all-start.3 = ((f32[32,128,128]{2,1,0:T(8,128)}), f32[32,128,128]{2,1,0:T(8,128)}, u32[]{:S(2)}, u32[]{:S(2)}) async-start(f32[32,128,128]{2,1,0:T(8,128)} %bitcast.109), calls=%async_computation.3 | async-start | bytes 4194304 | tf_op jit(solution)/shard_map/all_to_all | solution.py:56
  124.6 5.1 %fusion.24 = f32[1,1,512,1024]{3,2,1,0:T(8,128)} fusion(f32[1,512,1024]{2,1,0:T(8,128)} %get-tuple-element.26, f32[1,512,1024]{2,1,0:T(8,128)} %get-tuple-element.25, f32[512,1024,1]{1,0,2:T(8,128)} %copy-done.4), kind=kLoop, calls=%fused_computation.40 | loop fusion | flops 1048576 | bytes 8388608 | tf_op jit(solution)/shard_map/broadcast_in_dim | solution.py:145
  129.7 21.6 %all-to-all-done.3 = f32[32,128,128]{2,1,0:T(8,128)} async-done(((f32[32,128,128]{2,1,0:T(8,128)}), f32[32,128,128]{2,1,0:T(8,128)}, u32[]{:S(2)}, u32[]{:S(2)}) %all-to-all-start.3) | async-done | bytes 2097184 | tf_op jit(solution)/shard_map/all_to_all | solution.py:56
  151.3 4.6 %fusion.25 = f32[1,32,128,128]{3,1,2,0:T(8,128)S(1)} fusion(f32[32,32,1]{1,0,2:T(8,128)S(1)} %bitcast.124, f32[32,128,128]{2,1,0:T(8,128)} %all-to-all-done.3), kind=kOutput, calls=%fused_computation.41 | convolution fusion | flops 201326592 | bytes 4198400 | tf_op jit(solution)/shard_map/kz,kxy->zxy/dot_general | solution.py:59
  155.9 2.5 %copy.81 = f32[1,32,128,128]{3,2,1,0:T(8,128)} copy(f32[1,32,128,128]{3,1,2,0:T(8,128)S(1)} %fusion.25) | data formatting | bytes 4194304
  (45 shorter events, 6.6 us)
Async XLA Ops:
  0.6 20.2 %copy-start = (f32[1,32,128,128]{3,2,1,0:T(8,128)S(1)}, f32[1,32,128,128]{3,2,1,0:T(8,128)}, u32[]{:S(2)}) copy-start(f32[1,32,128,128]{3,2,1,0:T(8,128)} %param.9) | copy-start | bytes 6291460
  2.4 14.7 %slice-start = ((f32[1,32,128,128]{3,2,1,0:T(8,128)}), f32[1,3,128,128]{3,2,1,0:T(8,128)S(1)}, s32[]{:S(2)}) async-start(f32[1,32,128,128]{3,2,1,0:T(8,128)} %param.8), calls=%async_computation.4 | async-start | bytes 393216 | tf_op jit(solution)/shard_map/slice | solution.py:102
  5.0 25.1 %all-to-all-start = ((f32[128,2,512]{2,1,0:T(2,128)}), f32[128,2,512]{2,1,0:T(2,128)}, u32[]{:S(2)}, u32[]{:S(2)}) async-start(f32[128,2,512]{2,1,0:T(2,128)} %all_to_all.20), calls=%async_computation | async-start | bytes 1048576 | tf_op jit(solution)/shard_map/all_to_all | solution.py:112
  34.9 0.6 copy-start.8
  36.9 3.3 %copy-start.5 = (f32[256,128]{1,0:T(8,128)}, f32[256,128]{1,0:T(8,128)S(1)}, u32[]{:S(2)}) copy-start(f32[256,128]{1,0:T(8,128)S(1)} %get-tuple-element.17) | copy-start | bytes 393220
  36.9 3.3 %copy-start.6 = (f32[256,128]{1,0:T(8,128)}, f32[256,128]{1,0:T(8,128)S(1)}, u32[]{:S(2)}) copy-start(f32[256,128]{1,0:T(8,128)S(1)} %get-tuple-element.18) | copy-start | bytes 393220
  37.0 3.3 %copy-start.7 = (f32[256,128]{1,0:T(8,128)}, f32[256,128]{1,0:T(8,128)S(1)}, u32[]{:S(2)}) copy-start(f32[256,128]{1,0:T(8,128)S(1)} %get-tuple-element.19) | copy-start | bytes 393220
  40.2 17.0 %all-to-all-start.1 = ((f32[128,2,384]{2,1,0:T(2,128)}), f32[128,2,384]{2,1,0:T(2,128)S(1)}, u32[]{:S(2)}, u32[]{:S(2)}) async-start(f32[128,2,384]{2,1,0:T(2,128)} %maximum_multiply_fusion), calls=%async_computation.1 | async-start | bytes 786432 | tf_op jit(solution)/shard_map/all_to_all | solution.py:130
  66.8 34.1 %all-to-all-start.2 = ((f32[32,128,128]{2,1,0:T(8,128)}), f32[32,128,128]{2,1,0:T(8,128)}, u32[]{:S(2)}, u32[]{:S(2)}) async-start(f32[32,128,128]{2,1,0:T(8,128)} %copy.70), calls=%async_computation.2 | async-start | bytes 4194304 | tf_op jit(solution)/shard_map/all_to_all | solution.py:39
  100.9 3.6 %copy-start.1 = (f32[1024,1024]{0,1:T(8,128)S(1)}, f32[1024,1024]{0,1:T(8,128)}, u32[]{:S(2)}) copy-start(f32[1024,1024]{0,1:T(8,128)} %cosine_multiply_fusion) | copy-start | bytes 12582916
  104.5 3.6 %copy-start.2 = (f32[1,512,1024]{2,1,0:T(8,128)S(1)}, f32[1,512,1024]{2,1,0:T(8,128)}, u32[]{:S(2)}) copy-start(f32[1,512,1024]{2,1,0:T(8,128)} %get-tuple-element.25) | copy-start | bytes 6291460
  104.5 3.6 %copy-start.3 = (f32[1,512,1024]{2,1,0:T(8,128)S(1)}, f32[1,512,1024]{2,1,0:T(8,128)}, u32[]{:S(2)}) copy-start(f32[1,512,1024]{2,1,0:T(8,128)} %get-tuple-element.26) | copy-start | bytes 6291460
  108.1 3.6 %copy-start.4 = (f32[512,1024,1]{1,0,2:T(8,128)}, f32[512,1024,1]{1,0,2:T(8,128)S(1)}, u32[]{:S(2)}) copy-start(f32[512,1024,1]{1,0,2:T(8,128)S(1)} %fusion.7) | copy-start | bytes 6291460
  117.8 33.5 %all-to-all-start.3 = ((f32[32,128,128]{2,1,0:T(8,128)}), f32[32,128,128]{2,1,0:T(8,128)}, u32[]{:S(2)}, u32[]{:S(2)}) async-start(f32[32,128,128]{2,1,0:T(8,128)} %bitcast.109), calls=%async_computation.3 | async-start | bytes 4194304 | tf_op jit(solution)/shard_map/all_to_all | solution.py:56

commit v5 on v1

--- a/solution.py
+++ b/solution.py
@@ -90,7 +90,7 @@
     table_x = lax.optimization_barrier(cosine_table(long_x))
     table_y = lax.optimization_barrier(cosine_table(long_y))
     scale_now, scale_spec = advance_terms(depth_index, depth, long_x, long_y)
-    scale_now = lax.optimization_barrier(scale_now)
+    base = lax.optimization_barrier(scale_now * modes_now[0] - modes_old[0])
     scale_spec = lax.optimization_barrier(scale_spec)
     top = jnp.stack(
         [pressure_now[0, depth - 1], pressure_now[0, depth - 2], pressure_now[0, depth - 3]], axis=1
@@ -131,7 +131,7 @@
     forcing = forcing.at[:, depth - 2].add(top_force[:, 1][None])
     forcing = forcing.at[:, depth - 3].add(top_force[:, 2][None])
     spectrum = to_modes(forcing, table_z, table_x, table_y)
-    modes_new = (scale_now * modes_now[0] - modes_old[0] + scale_spec * spectrum[0])[None]
+    modes_new = (base + scale_spec * spectrum[0])[None]
     pressure_next = to_cells(modes_new, table_z, table_x, table_y)
     return (modes_new, pressure_next)
 

time: 148 us -> 152 us (1.027)
  blocking collectives: 35.6 us -> 0 us
  waiting for transfers between devices: 24.7 us -> 48.8 us
  starting transfers between devices: 21.1 us -> 29.4 us
  other arithmetic: 31.5 us -> 36.8 us
    all_to_all x1 -> x0, blocking collectives: 35.6 us -> none  [to_cells(): lax.all_to_all(part, ('gx', 'gy'), split_axis=0, concat_axis=0, tiled=True)]
    all_to_all x0 -> x1, waiting for transfers between devices: none -> 24.2 us  [to_cells(): lax.all_to_all(part, ('gx', 'gy'), split_axis=0, concat_axis=0, tiled=True)]
    all_to_all x0 -> x1, starting transfers between devices: none -> 7.55 us  [to_cells(): lax.all_to_all(part, ('gx', 'gy'), split_axis=0, concat_axis=0, tiled=True)]
    broadcast_in_dim x0 -> x1, other arithmetic: none -> 4.22 us  [shards(): modes_new = (base + scale_spec * spectrum[0])[None]]
    dot_general x1, matrix products: 7.03 us -> 3.56 us  [to_modes(): return jnp.einsum('cjy,bjy->bc', split_y, part, precision=FAST)[None, None]]
    dot_general x1, matrix products: 1.9 us -> 3.63 us  [to_modes(): part = jnp.einsum('bix,ijxy->bjy', split_x, part, precision=FAST)]
    dot_general x1, matrix products: 3 us -> 4.53 us  [to_cells(): return jnp.einsum('kz,kxy->zxy', table_z, cells, precision=HIGH)[None]]
    unnamed x18 -> x20, local copies, waits for them, and re-layouts: 5.02 us -> 4.75 us
  transfers between devices with their start and end apart: 3 -> 4, of which waited for: 2 -> 3; matrix products, arithmetic and copies ran while one was open for 21% -> 24% of each run, Pallas kernels for 0% -> 0%
where the time goes in v5:
time: 152 us
  waiting for transfers between devices  48.8 us (32%)
  other arithmetic  36.8 us (24%)
  starting transfers between devices  29.4 us (19%)
  matrix products  23.2 us (15%)
  local copies, waits for them, and re-layouts  12.4 us (8%)
    all_to_all x1, waiting for transfers between devices, to_cells(): lax.all_to_all(part, ('gx', 'gy'), split_axis=0, concat_axis=0, tiled=True)  24.2 us
    mul x4, other arithmetic, cosine_table(): return scale * jnp.cos(jnp.pi * rows * (cols + 0.5) / count)  18.8 us
    all_to_all x1, waiting for transfers between devices, shards(): lax.all_to_all(buffer, ('grp', 'gx', 'gy'), split_axis=0, concat_axis=0,...  13.2 us
    mul x1, other arithmetic, advance_terms(): return (2.0 * jnp.cos(theta), COURANT * COURANT * shape * shape)  12.5 us
    all_to_all x1, starting transfers between devices, shards(): lax.all_to_all(buffer, ('grp', 'gx', 'gy'), split_axis=0, concat_axis=0,...  11.5 us
    all_to_all x1, waiting for transfers between devices, shards(): lax.all_to_all(force, ('grp', 'gx', 'gy'), split_axis=0, concat_axis=0, t...  11.4 us
    all_to_all x1, starting transfers between devices, to_cells(): lax.all_to_all(part, ('gx', 'gy'), split_axis=0, concat_axis=0, tiled=True)  7.55 us
    all_to_all x1, starting transfers between devices, to_modes(): lax.all_to_all(part, ('gx', 'gy'), split_axis=0, concat_axis=0, tiled=True)  5.6 us
  transfers between devices with their start and end apart: 4, of which 3 were waited for; matrix products, arithmetic and copies ran while one was open for 24% of the time, Pallas kernels for 0%

profile of v5, /device:TPU:1, one launch (start us, length us, event | category | flops | bytes accessed | tf_op | source)
XLA Modules:
  0.0 151.6 jit_solution(3662965307870264013)
XLA Ops:
  0.7 0.8 copy-done.6
  1.5 0.8 copy-done.4
  2.6 0.5 fusion.38
  3.1 1.1 all_to_all.20
  4.2 11.5 %all-to-all-start = ((f32[128,2,512]{2,1,0:T(2,128)}), f32[128,2,512]{2,1,0:T(2,128)S(1)}, u32[]{:S(2)}, u32[]{:S(2)}) async-start(f32[128,2,512]{2,1,0:T(2,128)} %all_to_all.20), calls=%async_computation | async-start | bytes 1048576 | tf_op jit(solution)/shard_map/all_to_all | solution.py:108
  16.0 13.2 %all-to-all-done = f32[128,2,512]{2,1,0:T(2,128)S(1)} async-done(((f32[128,2,512]{2,1,0:T(2,128)}), f32[128,2,512]{2,1,0:T(2,128)S(1)}, u32[]{:S(2)}, u32[]{:S(2)}) %all-to-all-start) | async-done | bytes 524320 | tf_op jit(solution)/shard_map/all_to_all | solution.py:108
  29.2 0.4 all_to_all.22
  29.9 0.4 convolution_subtract_fusion
  30.4 1.0 maximum_multiply_fusion.1
  31.4 4.7 %all-to-all-start.1 = ((f32[128,2,384]{2,1,0:T(2,128)}), f32[128,2,384]{2,1,0:T(2,128)S(1)}, u32[]{:S(2)}, u32[]{:S(2)}) async-start(f32[128,2,384]{2,1,0:T(2,128)} %maximum_multiply_fusion.1), calls=%async_computation.1 | async-start | bytes 786432 | tf_op jit(solution)/shard_map/all_to_all | solution.py:126
  36.1 0.6 fusion.32
  36.9 11.4 %all-to-all-done.1 = f32[128,2,384]{2,1,0:T(2,128)S(1)} async-done(((f32[128,2,384]{2,1,0:T(2,128)}), f32[128,2,384]{2,1,0:T(2,128)S(1)}, u32[]{:S(2)}, u32[]{:S(2)}) %all-to-all-start.1) | async-done | bytes 393248 | tf_op jit(solution)/shard_map/all_to_all | solution.py:126
  48.4 0.3 all_to_all.24
  48.7 0.2 copy.51
  48.8 0.4 fusion.49
  49.2 0.2 copy.89
  49.5 3.0 %fusion.16 = f32[32,128,128]{2,0,1:T(8,128)S(1)} fusion(f32[32,128,128]{2,1,0:T(8,128)S(1)} %fusion.55, f32[32,32]{0,1:T(8,128)S(1)} %cosine_multiply_fusion.2), kind=kOutput, calls=%fused_computation.27 | convolution fusion | flops 201326592 | bytes 4198400 | tf_op jit(solution)/shard_map/kz,zxy->kxy/dot_general | solution.py:38
  52.5 2.5 %copy.54 = f32[32,128,128]{2,1,0:T(8,128)} copy(f32[32,128,128]{2,0,1:T(8,128)S(1)} %fusion.16) | data formatting | bytes 4194304 | tf_op jit(solution)/shard_map/kz,zxy->kxy/dot_general | solution.py:38
  55.0 5.6 %all-to-all-start.2 = ((f32[32,128,128]{2,1,0:T(8,128)}), f32[32,128,128]{2,1,0:T(8,128)}, u32[]{:S(2)}, u32[]{:S(2)}) async-start(f32[32,128,128]{2,1,0:T(8,128)} %copy.54), calls=%async_computation.2 | async-start | bytes 4194304 | tf_op jit(solution)/shard_map/all_to_all | solution.py:39
  60.7 3.5 %cosine_multiply_fusion.1 = f32[512,512]{0,1:T(8,128)S(1)} fusion(f32[512]{0:T(512)S(1)} %get-tuple-element.68, f32[512]{0:T(512)S(1)} %get-tuple-element.69, f32[512]{0:T(512)S(1)} %fusion.67), kind=kLoop, calls=%fused_computation.44 | loop fusion | flops 786432 | bytes 1054720 | tf_op jit(solution)/shard_map/mul | solution.py:16
  64.2 15.1 %cosine_multiply_fusion = f32[1024,1024]{0,1:T(8,128)} fusion(f32[1024]{0:T(1024)S(1)} %get-tuple-element.66, f32[1024]{0:T(1024)S(1)} %get-tuple-element.67, f32[1024]{0:T(1024)S(1)} %fusion.66), kind=kLoop, calls=%fused_computation | loop fusion | flops 3145728 | bytes 4206592 | tf_op jit(solution)/shard_map/mul | solution.py:16
  79.3 12.5 %multiply_multiply_fusion = (f32[1,512,1024]{2,1,0:T(8,128)S(1)}, f32[1,512,1024]{2,1,0:T(8,128)}) fusion(f32[1024]{0:T(1024)S(1)} %multiply_multiply_fusion.5, f32[512]{0:T(512)S(1)} %multiply_add_fusion.2, f32[1,1,512,1024]{3,2,1,0:T(8,128)} %param.15, f32[1,1,512,1024]{3,2,1,0:T(8,128)} %param.14), kind=kLoop, calls=%fused_computation.1 | loop fusion | flops 21495808 | bytes 8394752 | tf_op jit(solution)/shard_map/mul | solution.py:73
  91.8 3.6 %fusion.71 = f32[512,8,128,1]{2,0,1,3:T(8,128)S(1)} fusion(f32[512,4,128,1]{0,2,3,1:T(8,128)S(1)} %bitcast.117, f32[4,8,128,128]{3,2,1,0:T(8,128)} %bitcast.28), kind=kOutput, calls=%fused_computation.109 | convolution fusion | flops 1610612736 | bytes 5242880 | tf_op jit(solution)/shard_map/bix,ijxy->bjy/dot_general | solution.py:43
  95.4 3.6 %fusion.7 = f32[512,1024,1]{1,0,2:T(8,128)S(1)} fusion(f32[1024,8,128]{0,2,1:T(8,128)S(1)} %bitcast.114, f32[512,8,128,1]{2,0,1,3:T(8,128)S(1)} %fusion.71), kind=kOutput, calls=%fused_computation.15 | convolution fusion | flops 3221225472 | bytes 8388608 | tf_op jit(solution)/shard_map/cjy,bjy->bc/dot_general | solution.py:44
  99.0 3.5 %fusion.11 = f32[512,8,128]{0,2,1:T(8,128)S(1)} fusion(f32[1024,8,128]{0,2,1:T(8,128)S(1)} %bitcast.115, f32[1,512,1024]{2,1,0:T(8,128)S(1)} %copy-done.1, f32[1,512,1024]{2,1,0:T(8,128)S(1)} %get-tuple-element.64, f32[512,1024,1]{1,0,2:T(8,128)S(1)} %fusion.7), kind=kOutput, calls=%fused_computation.19 | convolution fusion | flops 3222274048 | bytes 12582912 | tf_op jit(solution)/shard_map/cjy,bc->bjy/dot_general | solution.py:54
  102.5 3.2 %fusion.28 = f32[4,8,128,128]{2,3,0,1:T(8,128)} fusion(f32[512,4,128,1]{0,2,1,3:T(8,128)S(1)} %bitcast.118, f32[512,8,128]{0,2,1:T(8,128)S(1)} %fusion.11), kind=kOutput, calls=%fused_computation.42 | convolution fusion | flops 1610612736 | bytes 5242880 | tf_op jit(solution)/shard_map/bix,bjy->ijxy/dot_general | solution.py:55
  105.7 2.9 %copy.61 = f32[4,8,128,128]{3,2,1,0:T(8,128)} copy(f32[4,8,128,128]{2,3,0,1:T(8,128)} %fusion.28) | data formatting | bytes 4194304 | tf_op jit(solution)/shard_map/bix,bjy->ijxy/transpose | solution.py:55
  108.6 7.6 %all-to-all-start.3 = ((f32[32,128,128]{2,1,0:T(8,128)}), f32[32,128,128]{2,1,0:T(8,128)}, u32[]{:S(2)}, u32[]{:S(2)}) async-start(f32[32,128,128]{2,1,0:T(8,128)} %bitcast.119), calls=%async_computation.3 | async-start | bytes 4194304 | tf_op jit(solution)/shard_map/all_to_all | solution.py:57
  116.2 4.2 %fusion.24 = f32[1,1,512,1024]{3,2,1,0:T(8,128)} fusion(f32[1,512,1024]{2,1,0:T(8,128)} %get-tuple-element.65, f32[1,512,1024]{2,1,0:T(8,128)S(1)} %get-tuple-element.64, f32[512,1024,1]{1,0,2:T(8,128)} %copy-done.2), kind=kLoop, calls=%fused_computation.40 | loop fusion | flops 1048576 | bytes 8388608 | tf_op jit(solution)/shard_map/broadcast_in_dim | solution.py:134
  120.4 24.2 %all-to-all-done.3 = f32[32,128,128]{2,1,0:T(8,128)} async-done(((f32[32,128,128]{2,1,0:T(8,128)}), f32[32,128,128]{2,1,0:T(8,128)}, u32[]{:S(2)}, u32[]{:S(2)}) %all-to-all-start.3) | async-done | bytes 2097184 | tf_op jit(solution)/shard_map/all_to_all | solution.py:57
  144.6 4.5 %fusion.25 = f32[1,32,128,128]{3,1,2,0:T(8,128)S(1)} fusion(f32[32,128,128]{2,1,0:T(8,128)} %all-to-all-done.3, f32[32,32]{0,1:T(8,128)S(1)} %cosine_multiply_fusion.2), kind=kOutput, calls=%fused_computation.41 | convolution fusion | flops 201326592 | bytes 4198400 | tf_op jit(solution)/shard_map/kz,kxy->zxy/dot_general | solution.py:58
  149.1 2.5 %copy.63 = f32[1,32,128,128]{3,2,1,0:T(8,128)} copy(f32[1,32,128,128]{3,1,2,0:T(8,128)S(1)} %fusion.25) | data formatting | bytes 4194304
  (41 shorter events, 1.3 us)
Async XLA Ops:
  0.6 1.6 %copy-start.4 = (f32[1,32,128,128]{3,2,1,0:T(8,128)S(1)}, f32[1,32,128,128]{3,2,1,0:T(8,128)}, u32[]{:S(2)}) copy-start(f32[1,32,128,128]{3,2,1,0:T(8,128)} %param.16) | copy-start | bytes 6291460
  0.6 2.0 %copy-start.5 = (s32[1,128,1]{1,2,0:T(1,128)S(1)}, s32[1,128,1]{1,2,0:T(1,128)}, u32[]{:S(2)}) copy-start(s32[1,128,1]{1,2,0:T(1,128)} %param.18) | copy-start | bytes 1540
  0.7 0.8 copy-start.6
  2.3 13.6 %slice-start = ((f32[1,32,128,128]{3,2,1,0:T(8,128)}), f32[1,3,128,128]{3,2,1,0:T(8,128)S(1)}, s32[]{:S(2)}) async-start(f32[1,32,128,128]{3,2,1,0:T(8,128)} %param.16), calls=%async_computation.4 | async-start | bytes 393216 | tf_op jit(solution)/shard_map/slice | solution.py:98
  4.2 25.0 %all-to-all-start = ((f32[128,2,512]{2,1,0:T(2,128)}), f32[128,2,512]{2,1,0:T(2,128)S(1)}, u32[]{:S(2)}, u32[]{:S(2)}) async-start(f32[128,2,512]{2,1,0:T(2,128)} %all_to_all.20), calls=%async_computation | async-start | bytes 1048576 | tf_op jit(solution)/shard_map/all_to_all | solution.py:108
  29.8 7.0 %copy-start.3 = (f32[1,32,128,128]{3,2,1,0:T(8,128)S(1)}, f32[1,32,128,128]{3,2,1,0:T(8,128)}, u32[]{:S(2)}) copy-start(f32[1,32,128,128]{3,2,1,0:T(8,128)} %param.17) | copy-start | bytes 6291460
  31.4 17.0 %all-to-all-start.1 = ((f32[128,2,384]{2,1,0:T(2,128)}), f32[128,2,384]{2,1,0:T(2,128)S(1)}, u32[]{:S(2)}, u32[]{:S(2)}) async-start(f32[128,2,384]{2,1,0:T(2,128)} %maximum_multiply_fusion.1), calls=%async_computation.1 | async-start | bytes 786432 | tf_op jit(solution)/shard_map/all_to_all | solution.py:126
  55.0 36.7 %all-to-all-start.2 = ((f32[32,128,128]{2,1,0:T(8,128)}), f32[32,128,128]{2,1,0:T(8,128)}, u32[]{:S(2)}, u32[]{:S(2)}) async-start(f32[32,128,128]{2,1,0:T(8,128)} %copy.54), calls=%async_computation.2 | async-start | bytes 4194304 | tf_op jit(solution)/shard_map/all_to_all | solution.py:39
  91.8 3.6 %copy-start = (f32[1024,1024]{0,1:T(8,128)S(1)}, f32[1024,1024]{0,1:T(8,128)}, u32[]{:S(2)}) copy-start(f32[1024,1024]{0,1:T(8,128)} %cosine_multiply_fusion) | copy-start | bytes 12582916
  95.4 3.6 %copy-start.1 = (f32[1,512,1024]{2,1,0:T(8,128)S(1)}, f32[1,512,1024]{2,1,0:T(8,128)}, u32[]{:S(2)}) copy-start(f32[1,512,1024]{2,1,0:T(8,128)} %get-tuple-element.65) | copy-start | bytes 6291460
  99.0 3.5 %copy-start.2 = (f32[512,1024,1]{1,0,2:T(8,128)}, f32[512,1024,1]{1,0,2:T(8,128)S(1)}, u32[]{:S(2)}) copy-start(f32[512,1024,1]{1,0,2:T(8,128)S(1)} %fusion.7) | copy-start | bytes 6291460
  108.6 35.9 %all-to-all-start.3 = ((f32[32,128,128]{2,1,0:T(8,128)}), f32[32,128,128]{2,1,0:T(8,128)}, u32[]{:S(2)}, u32[]{:S(2)}) async-start(f32[32,128,128]{2,1,0:T(8,128)} %bitcast.119), calls=%async_computation.3 | async-start | bytes 4194304 | tf_op jit(solution)/shard_map/all_to_all | solution.py:57

commit v6 on v1

--- a/solution.py
+++ b/solution.py
@@ -35,7 +35,7 @@
     width_y = lax.axis_size("gy")
     rows_x = field.shape[2]
     cols_y = field.shape[3]
-    part = jnp.einsum("kz,zxy->kxy", table_z, field[0], precision=HIGH)
+    part = jnp.einsum("kz,zxy->kxy", table_z, field[0], precision=FAST)
     part = lax.all_to_all(part, ("gx", "gy"), split_axis=0, concat_axis=0, tiled=True)
     part = part.reshape(width_x, width_y, rows_x, cols_y)
     split_x = table_x.reshape(table_x.shape[0], width_x, rows_x)
@@ -55,7 +55,7 @@
     part = jnp.einsum("bix,bjy->ijxy", split_x, part, precision=FAST)
     part = part.reshape(width_x * width_y, rows_x, cols_y)
     cells = lax.all_to_all(part, ("gx", "gy"), split_axis=0, concat_axis=0, tiled=True)
-    return jnp.einsum("kz,kxy->zxy", table_z, cells, precision=HIGH)[None]
+    return jnp.einsum("kz,kxy->zxy", table_z, cells, precision=FAST)[None]
 
 
 def advance_terms(depth_index, depth, long_x, long_y):

time: 148 us -> 146 us (0.986)
  matrix products: 22.1 us -> 20.4 us
    dot_general x2, matrix products: 6.01 us -> 4.3 us  [the longest x1 2.15 us: to_cells(): return jnp.einsum('kz,kxy->zxy', table_z, cells, precision=FAST)[None]]
where the time goes in v6:
time: 146 us
  blocking collectives  35.6 us (24%)
  other arithmetic  31.5 us (22%)
  waiting for transfers between devices  24.7 us (17%)
  starting transfers between devices  21.1 us (14%)
  matrix products  20.4 us (14%)
  local copies, waits for them, and re-layouts  11.6 us (8%)
    all_to_all x1, blocking collectives, to_cells(): lax.all_to_all(part, ('gx', 'gy'), split_axis=0, concat_axis=0, tiled=True)  35.6 us
    mul x4, other arithmetic, cosine_table(): return scale * jnp.cos(jnp.pi * rows * (cols + 0.5) / count)  18.7 us
    all_to_all x1, waiting for transfers between devices, shards(): lax.all_to_all(buffer, ('grp', 'gx', 'gy'), split_axis=0, concat_axis=0,...  13.2 us
    all_to_all x1, starting transfers between devices, shards(): lax.all_to_all(buffer, ('grp', 'gx', 'gy'), split_axis=0, concat_axis=0,...  11.5 us
    all_to_all x1, waiting for transfers between devices, shards(): lax.all_to_all(force, ('grp', 'gx', 'gy'), split_axis=0, concat_axis=0, t...  11.4 us
    mul x1, other arithmetic, advance_terms(): return (2.0 * jnp.cos(theta), COURANT * COURANT * shape * shape)  11.3 us
    dot_general x1, matrix products, to_modes(): return jnp.einsum('cjy,bjy->bc', split_y, part, precision=FAST)[None, None]  7.03 us
    unnamed x18, local copies, waits for them, and re-layouts  5.02 us
  transfers between devices with their start and end apart: 3, of which 2 were waited for; matrix products, arithmetic and copies ran while one was open for 21% of the time, Pallas kernels for 0%

profile of v6, /device:TPU:1, one launch (start us, length us, event | category | flops | bytes accessed | tf_op | source)
XLA Modules:
  0.0 145.9 jit_solution(7743177427978218038)
XLA Ops:
  0.7 0.8 copy-done.5
  1.5 0.8 copy-done.3
  2.6 0.5 fusion.38
  3.1 1.1 all_to_all.20
  4.2 11.5 %all-to-all-start = ((f32[128,2,512]{2,1,0:T(2,128)}), f32[128,2,512]{2,1,0:T(2,128)S(1)}, u32[]{:S(2)}, u32[]{:S(2)}) async-start(f32[128,2,512]{2,1,0:T(2,128)} %all_to_all.20), calls=%async_computation | async-start | bytes 1048576 | tf_op jit(solution)/shard_map/all_to_all | solution.py:108
  15.7 0.1 cosine_multiply_fusion.3
  16.0 13.2 %all-to-all-done = f32[128,2,512]{2,1,0:T(2,128)S(1)} async-done(((f32[128,2,512]{2,1,0:T(2,128)}), f32[128,2,512]{2,1,0:T(2,128)S(1)}, u32[]{:S(2)}, u32[]{:S(2)}) %all-to-all-start) | async-done | bytes 524320 | tf_op jit(solution)/shard_map/all_to_all | solution.py:108
  29.2 0.4 all_to_all.22
  29.9 0.4 convolution_subtract_fusion
  30.4 1.0 maximum_multiply_fusion.1
  31.4 4.7 %all-to-all-start.1 = ((f32[128,2,384]{2,1,0:T(2,128)}), f32[128,2,384]{2,1,0:T(2,128)S(1)}, u32[]{:S(2)}, u32[]{:S(2)}) async-start(f32[128,2,384]{2,1,0:T(2,128)} %maximum_multiply_fusion.1), calls=%async_computation.1 | async-start | bytes 786432 | tf_op jit(solution)/shard_map/all_to_all | solution.py:126
  36.1 0.6 fusion.32
  36.9 11.4 %all-to-all-done.1 = f32[128,2,384]{2,1,0:T(2,128)S(1)} async-done(((f32[128,2,384]{2,1,0:T(2,128)}), f32[128,2,384]{2,1,0:T(2,128)S(1)}, u32[]{:S(2)}, u32[]{:S(2)}) %all-to-all-start.1) | async-done | bytes 393248 | tf_op jit(solution)/shard_map/all_to_all | solution.py:126
  48.4 0.3 all_to_all.24
  48.7 0.2 copy.51
  48.8 0.4 fusion.49
  49.2 0.2 copy.89
  49.5 2.2 %fusion.16 = f32[32,128,128]{2,0,1:T(8,128)S(1)} fusion(f32[32,128,128]{2,1,0:T(8,128)S(1)} %fusion.55, f32[32,32]{0,1:T(8,128)S(1)} %cosine_multiply_fusion.3), kind=kOutput, calls=%fused_computation.27 | convolution fusion | flops 100663296 | bytes 4198400 | tf_op jit(solution)/shard_map/kz,zxy->kxy/dot_general | solution.py:38
  51.6 2.6 %copy.54 = f32[32,128,128]{2,1,0:T(8,128)} copy(f32[32,128,128]{2,0,1:T(8,128)S(1)} %fusion.16) | data formatting | bytes 4194304 | tf_op jit(solution)/shard_map/kz,zxy->kxy/dot_general | solution.py:38
  54.2 4.9 %all-to-all-start.2 = ((f32[32,128,128]{2,1,0:T(8,128)}), f32[32,128,128]{2,1,0:T(8,128)S(1)}, u32[]{:S(2)}, u32[]{:S(2)}) async-start(f32[32,128,128]{2,1,0:T(8,128)} %copy.54), calls=%async_computation.2 | async-start | bytes 4194304 | tf_op jit(solution)/shard_map/all_to_all | solution.py:39
  59.1 3.5 %cosine_multiply_fusion.2 = f32[512,512]{0,1:T(8,128)S(1)} fusion(f32[512]{0:T(512)S(1)} %get-tuple-element.68, f32[512]{0:T(512)S(1)} %get-tuple-element.69, f32[512]{0:T(512)S(1)} %fusion.67), kind=kLoop, calls=%fused_computation.44 | loop fusion | flops 786432 | bytes 1054720 | tf_op jit(solution)/shard_map/mul | solution.py:16
  62.7 15.1 %cosine_multiply_fusion = f32[1024,1024]{0,1:T(8,128)} fusion(f32[1024]{0:T(1024)S(1)} %get-tuple-element.66, f32[1024]{0:T(1024)S(1)} %get-tuple-element.67, f32[1024]{0:T(1024)S(1)} %fusion.66), kind=kLoop, calls=%fused_computation | loop fusion | flops 3145728 | bytes 4206592 | tf_op jit(solution)/shard_map/mul | solution.py:16
  77.8 11.3 %cosine_multiply_fusion.1 = (f32[1,512,1024]{2,1,0:T(8,128)}, f32[1,512,1024]{2,1,0:T(8,128)}) fusion(f32[1024]{0:T(1024)S(1)} %multiply_multiply_fusion.5, f32[512]{0:T(512)S(1)} %multiply_add_fusion.2), kind=kLoop, calls=%fused_computation.39 | loop fusion | flops 20447232 | bytes 4200448 | tf_op jit(solution)/shard_map/mul | solution.py:73
  89.1 1.9 %fusion.71 = f32[512,8,128,1]{2,0,1,3:T(8,128)S(1)} fusion(f32[512,4,128,1]{0,2,3,1:T(8,128)S(1)} %bitcast.115, f32[4,8,128,128]{3,2,1,0:T(8,128)S(1)} %bitcast.117), kind=kOutput, calls=%fused_computation.109 | convolution fusion | flops 1610612736 | bytes 5242880 | tf_op jit(solution)/shard_map/bix,ijxy->bjy/dot_general | solution.py:43
  91.0 0.3 copy-done
  91.3 7.0 %fusion.13 = f32[1,512,1024]{2,1,0:T(8,128)S(1)} fusion(f32[1,512,1024]{2,1,0:T(8,128)} %get-tuple-element.65, f32[1,1,512,1024]{3,2,1,0:T(8,128)} %param.15, f32[1,512,1024]{2,1,0:T(8,128)} %get-tuple-element.64, f32[1,1,512,1024]{3,2,1,0:T(8,128)} %param.14, f32[1024,8,128]{0,2,1:T(8,128)S(1)} %bitcast.112, f32[512,8,128,1]{2,0,1,3:T(8,128)S(1)} %fusion.71), kind=kOutput, calls=%fused_computation.22 | convolution fusion | flops 3223322624 | bytes 16777216 | tf_op jit(solution)/shard_map/cjy,bjy->bc/dot_general | solution.py:44
  98.4 3.5 %fusion.11 = f32[512,8,128]{0,2,1:T(8,128)S(1)} fusion(f32[1024,8,128]{0,2,1:T(8,128)S(1)} %bitcast.113, f32[1,512,1024]{2,1,0:T(8,128)S(1)} %fusion.13), kind=kOutput, calls=%fused_computation.19 | convolution fusion | flops 3221225472 | bytes 8388608 | tf_op jit(solution)/shard_map/cjy,bc->bjy/dot_general | solution.py:54
  101.9 1.8 %fusion.26 = f32[4,8,128,128]{2,3,0,1:T(8,128)S(1)} fusion(f32[512,4,128,1]{0,2,1,3:T(8,128)S(1)} %bitcast.116, f32[512,8,128]{0,2,1:T(8,128)S(1)} %fusion.11), kind=kOutput, calls=%fused_computation.42 | convolution fusion | flops 1610612736 | bytes 5242880 | tf_op jit(solution)/shard_map/bix,bjy->ijxy/dot_general | solution.py:55
  103.8 1.8 %copy.61 = f32[4,8,128,128]{3,2,1,0:T(8,128)} copy(f32[4,8,128,128]{2,3,0,1:T(8,128)S(1)} %fusion.26) | data formatting | bytes 4194304 | tf_op jit(solution)/shard_map/bix,bjy->ijxy/transpose | solution.py:55
  105.6 35.6 %all_to_all.31 = f32[32,128,128]{2,1,0:T(8,128)S(1)} all-to-all(f32[32,128,128]{2,1,0:T(8,128)} %bitcast.118), channel_id=1, replica_groups=mesh['grp'=4,'gx'=4,'gy'=8] {'gx','gy'}, dimensions={0} | all-to-all | bytes 4194304 | tf_op jit(solution)/shard_map/all_to_all | solution.py:57
  141.2 2.2 %fusion.23 = f32[1,32,128,128]{3,1,2,0:T(8,128)S(1)} fusion(f32[32,128,128]{2,1,0:T(8,128)S(1)} %all_to_all.31, f32[32,32]{0,1:T(8,128)S(1)} %cosine_multiply_fusion.3), kind=kOutput, calls=%fused_computation.41 | convolution fusion | flops 100663296 | bytes 4198400 | tf_op jit(solution)/shard_map/kz,kxy->zxy/dot_general | solution.py:58
  143.4 2.5 %copy.63 = f32[1,32,128,128]{3,2,1,0:T(8,128)} copy(f32[1,32,128,128]{3,1,2,0:T(8,128)S(1)} %fusion.23) | data formatting | bytes 4194304
  (37 shorter events, 1.1 us)
Async XLA Ops:
  0.6 1.6 %copy-start.3 = (f32[1,32,128,128]{3,2,1,0:T(8,128)S(1)}, f32[1,32,128,128]{3,2,1,0:T(8,128)}, u32[]{:S(2)}) copy-start(f32[1,32,128,128]{3,2,1,0:T(8,128)} %param.16) | copy-start | bytes 6291460
  0.6 2.0 %copy-start.4 = (s32[1,128,1]{1,2,0:T(1,128)S(1)}, s32[1,128,1]{1,2,0:T(1,128)}, u32[]{:S(2)}) copy-start(s32[1,128,1]{1,2,0:T(1,128)} %param.18) | copy-start | bytes 1540
  0.7 0.8 copy-start.5
  2.3 13.6 %slice-start = ((f32[1,32,128,128]{3,2,1,0:T(8,128)}), f32[1,3,128,128]{3,2,1,0:T(8,128)S(1)}, s32[]{:S(2)}) async-start(f32[1,32,128,128]{3,2,1,0:T(8,128)} %param.16), calls=%async_computation.4 | async-start | bytes 393216 | tf_op jit(solution)/shard_map/slice | solution.py:98
  4.2 25.0 %all-to-all-start = ((f32[128,2,512]{2,1,0:T(2,128)}), f32[128,2,512]{2,1,0:T(2,128)S(1)}, u32[]{:S(2)}, u32[]{:S(2)}) async-start(f32[128,2,512]{2,1,0:T(2,128)} %all_to_all.20), calls=%async_computation | async-start | bytes 1048576 | tf_op jit(solution)/shard_map/all_to_all | solution.py:108
  29.8 7.0 %copy-start.1 = (f32[1,32,128,128]{3,2,1,0:T(8,128)S(1)}, f32[1,32,128,128]{3,2,1,0:T(8,128)}, u32[]{:S(2)}) copy-start(f32[1,32,128,128]{3,2,1,0:T(8,128)} %param.17) | copy-start | bytes 6291460
  31.4 17.0 %all-to-all-start.1 = ((f32[128,2,384]{2,1,0:T(2,128)}), f32[128,2,384]{2,1,0:T(2,128)S(1)}, u32[]{:S(2)}, u32[]{:S(2)}) async-start(f32[128,2,384]{2,1,0:T(2,128)} %maximum_multiply_fusion.1), calls=%async_computation.1 | async-start | bytes 786432 | tf_op jit(solution)/shard_map/all_to_all | solution.py:126
  54.2 34.9 %all-to-all-start.2 = ((f32[32,128,128]{2,1,0:T(8,128)}), f32[32,128,128]{2,1,0:T(8,128)S(1)}, u32[]{:S(2)}, u32[]{:S(2)}) async-start(f32[32,128,128]{2,1,0:T(8,128)} %copy.54), calls=%async_computation.2 | async-start | bytes 4194304 | tf_op jit(solution)/shard_map/all_to_all | solution.py:39
  89.1 2.2 %copy-start = (f32[1024,1024]{0,1:T(8,128)S(1)}, f32[1024,1024]{0,1:T(8,128)}, u32[]{:S(2)}) copy-start(f32[1024,1024]{0,1:T(8,128)} %cosine_multiply_fusion) | copy-start | bytes 12582916
  98.4 3.6 %copy-start.2 = (f32[1,512,1024]{2,1,0:T(8,128)}, f32[1,512,1024]{2,1,0:T(8,128)S(1)}, u32[]{:S(2)}) copy-start(f32[1,512,1024]{2,1,0:T(8,128)S(1)} %fusion.13) | copy-start | bytes 6291460

commit v7 on v6

--- a/solution.py
+++ b/solution.py
@@ -108,6 +108,7 @@
     got = lax.all_to_all(buffer, ("grp", "gx", "gy"), split_axis=0, concat_axis=0, tiled=True)
     rims = got[:, : 3 * cols_y]
     marks = jnp.round(got[:, 3 * cols_y]).astype(jnp.int32) - 1
+    marks, scale_now, scale_spec = lax.optimization_barrier((marks, scale_now, scale_spec))
     live = (marks >= 0).astype(jnp.float32)[:, None]
     meet = one_hot(marks, rows_x)
     met = jnp.einsum("kr,rf->kf", meet, bottom, precision=HIGH)

time: 146 us -> 145 us (level)
  starting transfers between devices: 21.1 us -> 24.3 us
  blocking collectives: 35.6 us -> 32.7 us
  waiting for transfers between devices: 24.7 us -> 23 us
    all_to_all x1, waiting for transfers between devices: 13.2 us -> 1.87 us  [shards(): lax.all_to_all(buffer, ('grp', 'gx', 'gy'), split_axis=0, concat_axis=0,...]
    all_to_all x1, waiting for transfers between devices: 0.01 us -> 9.76 us  [to_modes(): lax.all_to_all(part, ('gx', 'gy'), split_axis=0, concat_axis=0, tiled=True)]
    all_to_all x1, starting transfers between devices: 4.71 us -> 7.9 us  [shards(): lax.all_to_all(force, ('grp', 'gx', 'gy'), split_axis=0, concat_axis=0, t...]
    all_to_all x1, blocking collectives: 35.6 us -> 32.7 us  [to_cells(): lax.all_to_all(part, ('gx', 'gy'), split_axis=0, concat_axis=0, tiled=True)]
  transfers between devices with their start and end apart: 3 -> 3, of which waited for: 2 -> 3; matrix products, arithmetic and copies ran while one was open for 21% -> 21% of each run, Pallas kernels for 0% -> 0%
where the time goes in v7:
time: 145 us; the launch traced here: 144 us
  blocking collectives  32.7 us (23%)
  other arithmetic  31.4 us (22%)
  starting transfers between devices  24.3 us (17%)
  waiting for transfers between devices  23 us (16%)
  matrix products  20.4 us (14%)
  local copies, waits for them, and re-layouts  11.6 us (8%)
    all_to_all x1, blocking collectives, to_cells(): lax.all_to_all(part, ('gx', 'gy'), split_axis=0, concat_axis=0, tiled=True)  32.7 us
    mul x4, other arithmetic, cosine_table(): return scale * jnp.cos(jnp.pi * rows * (cols + 0.5) / count)  18.8 us
    all_to_all x1, starting transfers between devices, shards(): lax.all_to_all(buffer, ('grp', 'gx', 'gy'), split_axis=0, concat_axis=0,...  11.5 us
    all_to_all x1, waiting for transfers between devices, shards(): lax.all_to_all(force, ('grp', 'gx', 'gy'), split_axis=0, concat_axis=0, t...  11.4 us
    mul x1, other arithmetic, advance_terms(): return (2.0 * jnp.cos(theta), COURANT * COURANT * shape * shape)  11.3 us
    all_to_all x1, waiting for transfers between devices, to_modes(): lax.all_to_all(part, ('gx', 'gy'), split_axis=0, concat_axis=0, tiled=True)  9.76 us
    all_to_all x1, starting transfers between devices, shards(): lax.all_to_all(force, ('grp', 'gx', 'gy'), split_axis=0, concat_axis=0, t...  7.9 us
    dot_general x1, matrix products, to_modes(): return jnp.einsum('cjy,bjy->bc', split_y, part, precision=FAST)[None, None]  7.03 us
  transfers between devices with their start and end apart: 3, of which 3 were waited for; matrix products, arithmetic and copies ran while one was open for 21% of the time, Pallas kernels for 0%

profile of v7, /device:TPU:1, one launch (start us, length us, event | category | flops | bytes accessed | tf_op | source)
XLA Modules:
  0.0 144.4 jit_solution(2188950187002890350)
XLA Ops:
  0.7 1.6 %copy-done.3 = f32[1,32,128,128]{3,2,1,0:T(8,128)S(1)} copy-done((f32[1,32,128,128]{3,2,1,0:T(8,128)S(1)}, f32[1,32,128,128]{3,2,1,0:T(8,128)}, u32[]{:S(2)}) %copy-start.3) | copy-done | bytes 2097176
  2.6 0.5 fusion.38
  3.1 1.1 all_to_all.20
  4.2 11.5 %all-to-all-start = ((f32[128,2,512]{2,1,0:T(2,128)}), f32[128,2,512]{2,1,0:T(2,128)S(1)}, u32[]{:S(2)}, u32[]{:S(2)}) async-start(f32[128,2,512]{2,1,0:T(2,128)} %all_to_all.20), calls=%async_computation | async-start | bytes 1048576 | tf_op jit(solution)/shard_map/all_to_all | solution.py:108
  15.7 11.3 %multiply_multiply_fusion = (f32[1,512,1024]{2,1,0:T(8,128)}, f32[1,512,1024]{2,1,0:T(8,128)}) fusion(f32[1024]{0:T(1024)S(1)} %multiply_multiply_fusion.5, f32[512]{0:T(512)S(1)} %multiply_add_fusion.2), kind=kLoop, calls=%fused_computation.1 | loop fusion | flops 20447232 | bytes 4200448 | tf_op jit(solution)/shard_map/mul | solution.py:73
  27.2 0.1 cosine_multiply_fusion.3
  27.4 1.9 %all-to-all-done = f32[128,2,512]{2,1,0:T(2,128)S(1)} async-done(((f32[128,2,512]{2,1,0:T(2,128)}), f32[128,2,512]{2,1,0:T(2,128)S(1)}, u32[]{:S(2)}, u32[]{:S(2)}) %all-to-all-start) | async-done | bytes 524320 | tf_op jit(solution)/shard_map/all_to_all | solution.py:108
  29.2 0.4 all_to_all.22
  29.7 0.4 convolution_subtract_fusion
  30.3 1.0 maximum_multiply_fusion.1
  31.3 7.9 %all-to-all-start.1 = ((f32[128,2,384]{2,1,0:T(2,128)}), f32[128,2,384]{2,1,0:T(2,128)S(1)}, u32[]{:S(2)}, u32[]{:S(2)}) async-start(f32[128,2,384]{2,1,0:T(2,128)} %maximum_multiply_fusion.1), calls=%async_computation.1 | async-start | bytes 786432 | tf_op jit(solution)/shard_map/all_to_all | solution.py:127
  39.2 0.6 fusion.32
  40.0 11.4 %all-to-all-done.1 = f32[128,2,384]{2,1,0:T(2,128)S(1)} async-done(((f32[128,2,384]{2,1,0:T(2,128)}), f32[128,2,384]{2,1,0:T(2,128)S(1)}, u32[]{:S(2)}, u32[]{:S(2)}) %all-to-all-start.1) | async-done | bytes 393248 | tf_op jit(solution)/shard_map/all_to_all | solution.py:127
  51.4 0.3 all_to_all.24
  51.7 0.2 copy.51
  51.8 0.4 fusion.50
  52.2 0.2 copy.89
  52.5 2.2 %fusion.16 = f32[32,128,128]{2,0,1:T(8,128)S(1)} fusion(f32[32,128,128]{2,1,0:T(8,128)S(1)} %fusion.55, f32[32,32]{0,1:T(8,128)S(1)} %cosine_multiply_fusion.3), kind=kOutput, calls=%fused_computation.27 | convolution fusion | flops 100663296 | bytes 4198400 | tf_op jit(solution)/shard_map/kz,zxy->kxy/dot_general | solution.py:38
  54.6 2.6 %copy.54 = f32[32,128,128]{2,1,0:T(8,128)} copy(f32[32,128,128]{2,0,1:T(8,128)S(1)} %fusion.16) | data formatting | bytes 4194304 | tf_op jit(solution)/shard_map/kz,zxy->kxy/dot_general | solution.py:38
  57.2 4.9 %all-to-all-start.2 = ((f32[32,128,128]{2,1,0:T(8,128)}), f32[32,128,128]{2,1,0:T(8,128)S(1)}, u32[]{:S(2)}, u32[]{:S(2)}) async-start(f32[32,128,128]{2,1,0:T(8,128)} %copy.54), calls=%async_computation.2 | async-start | bytes 4194304 | tf_op jit(solution)/shard_map/all_to_all | solution.py:39
  62.2 3.5 %cosine_multiply_fusion.2 = f32[512,512]{0,1:T(8,128)S(1)} fusion(f32[512]{0:T(512)S(1)} %get-tuple-element.74, f32[512]{0:T(512)S(1)} %get-tuple-element.75, f32[512]{0:T(512)S(1)} %fusion.67), kind=kLoop, calls=%fused_computation.44 | loop fusion | flops 786432 | bytes 1054720 | tf_op jit(solution)/shard_map/mul | solution.py:16
  65.7 15.1 %cosine_multiply_fusion = f32[1024,1024]{0,1:T(8,128)} fusion(f32[1024]{0:T(1024)S(1)} %get-tuple-element.72, f32[1024]{0:T(1024)S(1)} %get-tuple-element.73, f32[1024]{0:T(1024)S(1)} %fusion.66), kind=kLoop, calls=%fused_computation | loop fusion | flops 3145728 | bytes 4206592 | tf_op jit(solution)/shard_map/mul | solution.py:16
  80.8 9.8 %all-to-all-done.2 = f32[32,128,128]{2,1,0:T(8,128)S(1)} async-done(((f32[32,128,128]{2,1,0:T(8,128)}), f32[32,128,128]{2,1,0:T(8,128)S(1)}, u32[]{:S(2)}, u32[]{:S(2)}) %all-to-all-start.2) | async-done | bytes 2097184 | tf_op jit(solution)/shard_map/all_to_all | solution.py:39
  90.6 1.9 %fusion.71 = f32[512,8,128,1]{2,0,1,3:T(8,128)S(1)} fusion(f32[512,4,128,1]{0,2,3,1:T(8,128)S(1)} %bitcast.115, f32[4,8,128,128]{3,2,1,0:T(8,128)S(1)} %bitcast.117), kind=kOutput, calls=%fused_computation.109 | convolution fusion | flops 1610612736 | bytes 5242880 | tf_op jit(solution)/shard_map/bix,ijxy->bjy/dot_general | solution.py:43
  92.5 0.3 copy-done
  92.7 7.0 %fusion.13 = f32[1,512,1024]{2,1,0:T(8,128)S(1)} fusion(f32[1,512,1024]{2,1,0:T(8,128)} %get-tuple-element.54, f32[1,1,512,1024]{3,2,1,0:T(8,128)} %param.15, f32[1,512,1024]{2,1,0:T(8,128)} %get-tuple-element.53, f32[1,1,512,1024]{3,2,1,0:T(8,128)} %param.14, f32[1024,8,128]{0,2,1:T(8,128)S(1)} %bitcast.112, f32[512,8,128,1]{2,0,1,3:T(8,128)S(1)} %fusion.71), kind=kOutput, calls=%fused_computation.22 | convolution fusion | flops 3223322624 | bytes 16777216 | tf_op jit(solution)/shard_map/cjy,bjy->bc/dot_general | solution.py:44
  99.8 3.5 %fusion.11 = f32[512,8,128]{0,2,1:T(8,128)S(1)} fusion(f32[1024,8,128]{0,2,1:T(8,128)S(1)} %bitcast.113, f32[1,512,1024]{2,1,0:T(8,128)S(1)} %fusion.13), kind=kOutput, calls=%fused_computation.19 | convolution fusion | flops 3221225472 | bytes 8388608 | tf_op jit(solution)/shard_map/cjy,bc->bjy/dot_general | solution.py:54
  103.3 1.8 %fusion.26 = f32[4,8,128,128]{2,3,0,1:T(8,128)S(1)} fusion(f32[512,4,128,1]{0,2,1,3:T(8,128)S(1)} %bitcast.116, f32[512,8,128]{0,2,1:T(8,128)S(1)} %fusion.11), kind=kOutput, calls=%fused_computation.42 | convolution fusion | flops 1610612736 | bytes 5242880 | tf_op jit(solution)/shard_map/bix,bjy->ijxy/dot_general | solution.py:55
  105.2 1.8 %copy.61 = f32[4,8,128,128]{3,2,1,0:T(8,128)} copy(f32[4,8,128,128]{2,3,0,1:T(8,128)S(1)} %fusion.26) | data formatting | bytes 4194304 | tf_op jit(solution)/shard_map/bix,bjy->ijxy/transpose | solution.py:55
  107.0 32.7 %all_to_all.31 = f32[32,128,128]{2,1,0:T(8,128)S(1)} all-to-all(f32[32,128,128]{2,1,0:T(8,128)} %bitcast.118), channel_id=1, replica_groups=mesh['grp'=4,'gx'=4,'gy'=8] {'gx','gy'}, dimensions={0} | all-to-all | bytes 4194304 | tf_op jit(solution)/shard_map/all_to_all | solution.py:57
  139.7 2.2 %fusion.23 = f32[1,32,128,128]{3,1,2,0:T(8,128)S(1)} fusion(f32[32,128,128]{2,1,0:T(8,128)S(1)} %all_to_all.31, f32[32,32]{0,1:T(8,128)S(1)} %cosine_multiply_fusion.3), kind=kOutput, calls=%fused_computation.41 | convolution fusion | flops 100663296 | bytes 4198400 | tf_op jit(solution)/shard_map/kz,kxy->zxy/dot_general | solution.py:58
  141.9 2.5 %copy.63 = f32[1,32,128,128]{3,2,1,0:T(8,128)} copy(f32[1,32,128,128]{3,1,2,0:T(8,128)S(1)} %fusion.23) | data formatting | bytes 4194304
  (37 shorter events, 1.0 us)
Async XLA Ops:
  0.6 1.6 %copy-start.3 = (f32[1,32,128,128]{3,2,1,0:T(8,128)S(1)}, f32[1,32,128,128]{3,2,1,0:T(8,128)}, u32[]{:S(2)}) copy-start(f32[1,32,128,128]{3,2,1,0:T(8,128)} %param.16) | copy-start | bytes 6291460
  0.6 2.0 %copy-start.4 = (s32[1,128,1]{1,2,0:T(1,128)S(1)}, s32[1,128,1]{1,2,0:T(1,128)}, u32[]{:S(2)}) copy-start(s32[1,128,1]{1,2,0:T(1,128)} %param.18) | copy-start | bytes 1540
  0.7 1.9 %copy-start.5 = (s32[1,128,1]{1,2,0:T(1,128)S(1)}, s32[1,128,1]{1,2,0:T(1,128)}, u32[]{:S(2)}) copy-start(s32[1,128,1]{1,2,0:T(1,128)} %param.19) | copy-start | bytes 1540
  4.2 25.0 %all-to-all-start = ((f32[128,2,512]{2,1,0:T(2,128)}), f32[128,2,512]{2,1,0:T(2,128)S(1)}, u32[]{:S(2)}, u32[]{:S(2)}) async-start(f32[128,2,512]{2,1,0:T(2,128)} %all_to_all.20), calls=%async_computation | async-start | bytes 1048576 | tf_op jit(solution)/shard_map/all_to_all | solution.py:108
  15.7 11.3 %slice-start = ((f32[1,32,128,128]{3,2,1,0:T(8,128)}), f32[1,3,128,128]{3,2,1,0:T(8,128)S(1)}, s32[]{:S(2)}) async-start(f32[1,32,128,128]{3,2,1,0:T(8,128)} %param.16), calls=%async_computation.4 | async-start | bytes 393216 | tf_op jit(solution)/shard_map/slice | solution.py:98
  29.7 10.2 %copy-start.1 = (f32[1,32,128,128]{3,2,1,0:T(8,128)S(1)}, f32[1,32,128,128]{3,2,1,0:T(8,128)}, u32[]{:S(2)}) copy-start(f32[1,32,128,128]{3,2,1,0:T(8,128)} %param.17) | copy-start | bytes 6291460
  31.3 20.1 %all-to-all-start.1 = ((f32[128,2,384]{2,1,0:T(2,128)}), f32[128,2,384]{2,1,0:T(2,128)S(1)}, u32[]{:S(2)}, u32[]{:S(2)}) async-start(f32[128,2,384]{2,1,0:T(2,128)} %maximum_multiply_fusion.1), calls=%async_computation.1 | async-start | bytes 786432 | tf_op jit(solution)/shard_map/all_to_all | solution.py:127
  57.2 33.3 %all-to-all-start.2 = ((f32[32,128,128]{2,1,0:T(8,128)}), f32[32,128,128]{2,1,0:T(8,128)S(1)}, u32[]{:S(2)}, u32[]{:S(2)}) async-start(f32[32,128,128]{2,1,0:T(8,128)} %copy.54), calls=%async_computation.2 | async-start | bytes 4194304 | tf_op jit(solution)/shard_map/all_to_all | solution.py:39
  90.6 2.2 %copy-start = (f32[1024,1024]{0,1:T(8,128)S(1)}, f32[1024,1024]{0,1:T(8,128)}, u32[]{:S(2)}) copy-start(f32[1024,1024]{0,1:T(8,128)} %cosine_multiply_fusion) | copy-start | bytes 12582916
  99.8 3.6 %copy-start.2 = (f32[1,512,1024]{2,1,0:T(8,128)}, f32[1,512,1024]{2,1,0:T(8,128)S(1)}, u32[]{:S(2)}) copy-start(f32[1,512,1024]{2,1,0:T(8,128)S(1)} %fusion.13) | copy-start | bytes 6291460

commit v8 on v6

--- a/solution.py
+++ b/solution.py
@@ -90,8 +90,6 @@
     table_x = lax.optimization_barrier(cosine_table(long_x))
     table_y = lax.optimization_barrier(cosine_table(long_y))
     scale_now, scale_spec = advance_terms(depth_index, depth, long_x, long_y)
-    scale_now = lax.optimization_barrier(scale_now)
-    scale_spec = lax.optimization_barrier(scale_spec)
     top = jnp.stack(
         [pressure_now[0, depth - 1], pressure_now[0, depth - 2], pressure_now[0, depth - 3]], axis=1
     ).reshape(rows_x, 3 * cols_y)
@@ -108,6 +106,8 @@
     got = lax.all_to_all(buffer, ("grp", "gx", "gy"), split_axis=0, concat_axis=0, tiled=True)
     rims = got[:, : 3 * cols_y]
     marks = jnp.round(got[:, 3 * cols_y]).astype(jnp.int32) - 1
+    base = scale_now * modes_now[0] - modes_old[0]
+    marks, base, scale_spec = lax.optimization_barrier((marks, base, scale_spec))
     live = (marks >= 0).astype(jnp.float32)[:, None]
     meet = one_hot(marks, rows_x)
     met = jnp.einsum("kr,rf->kf", meet, bottom, precision=HIGH)
@@ -131,7 +131,7 @@
     forcing = forcing.at[:, depth - 2].add(top_force[:, 1][None])
     forcing = forcing.at[:, depth - 3].add(top_force[:, 2][None])
     spectrum = to_modes(forcing, table_z, table_x, table_y)
-    modes_new = (scale_now * modes_now[0] - modes_old[0] + scale_spec * spectrum[0])[None]
+    modes_new = (base + scale_spec * spectrum[0])[None]
     pressure_next = to_cells(modes_new, table_z, table_x, table_y)
     return (modes_new, pressure_next)
 

time: 146 us -> 157 us (1.075)
  blocking collectives: 35.6 us -> 0 us
  waiting for transfers between devices: 24.7 us -> 44.4 us
  other arithmetic: 31.5 us -> 42.3 us
  starting transfers between devices: 21.1 us -> 31.3 us
  local copies, waits for them, and re-layouts: 11.6 us -> 15.5 us
    all_to_all x1 -> x0, blocking collectives: 35.6 us -> none  [to_cells(): lax.all_to_all(part, ('gx', 'gy'), split_axis=0, concat_axis=0, tiled=True)]
    all_to_all x0 -> x1, waiting for transfers between devices: none -> 24 us  [to_cells(): lax.all_to_all(part, ('gx', 'gy'), split_axis=0, concat_axis=0, tiled=True)]
    all_to_all x1, waiting for transfers between devices: 13.2 us -> 0.74 us  [shards(): lax.all_to_all(buffer, ('grp', 'gx', 'gy'), split_axis=0, concat_axis=0,...]
    all_to_all x1, waiting for transfers between devices: 0.01 us -> 9.81 us  [to_modes(): lax.all_to_all(part, ('gx', 'gy'), split_axis=0, concat_axis=0, tiled=True)]
    all_to_all x0 -> x1, starting transfers between devices: none -> 5.17 us  [to_cells(): lax.all_to_all(part, ('gx', 'gy'), split_axis=0, concat_axis=0, tiled=True)]
    broadcast_in_dim x0 -> x1, other arithmetic: none -> 4.42 us  [shards(): modes_new = (base + scale_spec * spectrum[0])[None]]
    all_to_all x1, starting transfers between devices: 4.71 us -> 9.02 us  [shards(): lax.all_to_all(force, ('grp', 'gx', 'gy'), split_axis=0, concat_axis=0, t...]
    dot_general x1, matrix products: 7.03 us -> 3.55 us  [to_modes(): return jnp.einsum('cjy,bjy->bc', split_y, part, precision=FAST)[None, None]]
  transfers between devices with their start and end apart: 3 -> 4, of which waited for: 2 -> 4; matrix products, arithmetic and copies ran while one was open for 21% -> 24% of each run, Pallas kernels for 0% -> 0%
where the time goes in v8:
time: 157 us; the launch traced here: 156 us
  waiting for transfers between devices  44.4 us (28%)
  other arithmetic  42.3 us (27%)
  starting transfers between devices  31.3 us (20%)
  matrix products  21.5 us (14%)
  local copies, waits for them, and re-layouts  15.5 us (10%)
    all_to_all x1, waiting for transfers between devices, to_cells(): lax.all_to_all(part, ('gx', 'gy'), split_axis=0, concat_axis=0, tiled=True)  24 us
    mul x4, other arithmetic, cosine_table(): return scale * jnp.cos(jnp.pi * rows * (cols + 0.5) / count)  18.7 us
    mul x1, other arithmetic, advance_terms(): return (2.0 * jnp.cos(theta), COURANT * COURANT * shape * shape)  12.5 us
    all_to_all x1, starting transfers between devices, shards(): lax.all_to_all(buffer, ('grp', 'gx', 'gy'), split_axis=0, concat_axis=0,...  11.5 us
    all_to_all x1, waiting for transfers between devices, to_modes(): lax.all_to_all(part, ('gx', 'gy'), split_axis=0, concat_axis=0, tiled=True)  9.81 us
    all_to_all x1, waiting for transfers between devices, shards(): lax.all_to_all(force, ('grp', 'gx', 'gy'), split_axis=0, concat_axis=0, t...  9.79 us
    all_to_all x1, starting transfers between devices, shards(): lax.all_to_all(force, ('grp', 'gx', 'gy'), split_axis=0, concat_axis=0, t...  9.02 us
    unnamed x19, local copies, waits for them, and re-layouts  7.85 us
  transfers between devices with their start and end apart: 4, of which 4 were waited for; matrix products, arithmetic and copies ran while one was open for 24% of the time, Pallas kernels for 0%

profile of v8, /device:TPU:1, one launch (start us, length us, event | category | flops | bytes accessed | tf_op | source)
XLA Modules:
  0.0 155.9 jit_solution(13686140292579598857)
XLA Ops:
  0.7 3.3 %copy.91 = f32[1,32,128,128]{3,2,1,0:T(8,128)} copy(f32[1,32,128,128]{3,2,1,0:T(8,128)} %param.17) | data formatting | bytes 4194304
  4.3 0.5 fusion.38
  4.8 1.1 all_to_all.20
  5.9 11.5 %all-to-all-start = ((f32[128,2,512]{2,1,0:T(2,128)}), f32[128,2,512]{2,1,0:T(2,128)S(1)}, u32[]{:S(2)}, u32[]{:S(2)}) async-start(f32[128,2,512]{2,1,0:T(2,128)} %all_to_all.20), calls=%async_computation | async-start | bytes 1048576 | tf_op jit(solution)/shard_map/all_to_all | solution.py:106
  17.8 12.5 %multiply_multiply_fusion = (f32[1,512,1024]{2,1,0:T(8,128)S(1)}, f32[1,512,1024]{2,1,0:T(8,128)}) fusion(f32[1024]{0:T(1024)S(1)} %multiply_multiply_fusion.5, f32[512]{0:T(512)S(1)} %multiply_add_fusion.2, f32[1,1,512,1024]{3,2,1,0:T(8,128)} %param.15, f32[1,1,512,1024]{3,2,1,0:T(8,128)} %param.14), kind=kLoop, calls=%fused_computation.1 | loop fusion | flops 21495808 | bytes 8394752 | tf_op jit(solution)/shard_map/mul | solution.py:73
  30.2 0.7 all-to-all-done
  32.0 1.0 maximum_multiply_fusion.1
  33.0 9.0 %all-to-all-start.1 = ((f32[128,2,384]{2,1,0:T(2,128)}), f32[128,2,384]{2,1,0:T(2,128)S(1)}, u32[]{:S(2)}, u32[]{:S(2)}) async-start(f32[128,2,384]{2,1,0:T(2,128)} %maximum_multiply_fusion.1), calls=%async_computation.1 | async-start | bytes 786432 | tf_op jit(solution)/shard_map/all_to_all | solution.py:126
  42.1 0.6 fusion.32
  42.8 1.6 %fusion.42 = f32[1,32,128,128]{3,2,1,0:T(8,128)} fusion(f32[1,32,128,128]{3,2,1,0:T(8,128)} %copy.91, f32[128,3,128]{2,0,1:T(8,128)S(1)} %copy.50), kind=kLoop, calls=%fused_computation.59 | loop fusion | flops 49152 | bytes 589824 | tf_op jit(solution)/shard_map/scatter-add | solution.py:129
  44.4 9.8 %all-to-all-done.1 = f32[128,2,384]{2,1,0:T(2,128)S(1)} async-done(((f32[128,2,384]{2,1,0:T(2,128)}), f32[128,2,384]{2,1,0:T(2,128)S(1)}, u32[]{:S(2)}, u32[]{:S(2)}) %all-to-all-start.1) | async-done | bytes 393248 | tf_op jit(solution)/shard_map/all_to_all | solution.py:126
  54.7 0.4 fusion.50
  55.0 1.5 fusion.59
  56.5 1.5 fusion.57
  58.0 1.6 %copy.89 = f32[32,128,128]{2,1,0:T(8,128)S(1)} copy(f32[32,128,128]{2,1,0:T(8,128)} %bitcast.116) | data formatting | bytes 4194304
  59.6 0.8 fusion.55
  60.4 2.1 %fusion.16 = f32[32,128,128]{2,0,1:T(8,128)S(1)} fusion(f32[32,128,128]{2,1,0:T(8,128)S(1)} %fusion.55, f32[32,32]{0,1:T(8,128)S(1)} %cosine_multiply_fusion.2), kind=kOutput, calls=%fused_computation.27 | convolution fusion | flops 100663296 | bytes 4198400 | tf_op jit(solution)/shard_map/kz,zxy->kxy/dot_general | solution.py:38
  62.6 2.5 %copy.54 = f32[32,128,128]{2,1,0:T(8,128)} copy(f32[32,128,128]{2,0,1:T(8,128)S(1)} %fusion.16) | data formatting | bytes 4194304 | tf_op jit(solution)/shard_map/kz,zxy->kxy/dot_general | solution.py:38
  65.1 5.6 %all-to-all-start.2 = ((f32[32,128,128]{2,1,0:T(8,128)}), f32[32,128,128]{2,1,0:T(8,128)}, u32[]{:S(2)}, u32[]{:S(2)}) async-start(f32[32,128,128]{2,1,0:T(8,128)} %copy.54), calls=%async_computation.2 | async-start | bytes 4194304 | tf_op jit(solution)/shard_map/all_to_all | solution.py:39
  70.8 3.5 %cosine_multiply_fusion.1 = f32[512,512]{0,1:T(8,128)S(1)} fusion(f32[512]{0:T(512)S(1)} %get-tuple-element.74, f32[512]{0:T(512)S(1)} %get-tuple-element.75, f32[512]{0:T(512)S(1)} %fusion.67), kind=kLoop, calls=%fused_computation.44 | loop fusion | flops 786432 | bytes 1054720 | tf_op jit(solution)/shard_map/mul | solution.py:16
  74.3 15.1 %cosine_multiply_fusion = f32[1024,1024]{0,1:T(8,128)} fusion(f32[1024]{0:T(1024)S(1)} %get-tuple-element.72, f32[1024]{0:T(1024)S(1)} %get-tuple-element.73, f32[1024]{0:T(1024)S(1)} %fusion.66), kind=kLoop, calls=%fused_computation | loop fusion | flops 3145728 | bytes 4206592 | tf_op jit(solution)/shard_map/mul | solution.py:16
  89.4 9.8 %all-to-all-done.2 = f32[32,128,128]{2,1,0:T(8,128)} async-done(((f32[32,128,128]{2,1,0:T(8,128)}), f32[32,128,128]{2,1,0:T(8,128)}, u32[]{:S(2)}, u32[]{:S(2)}) %all-to-all-start.2) | async-done | bytes 2097184 | tf_op jit(solution)/shard_map/all_to_all | solution.py:39
  99.2 3.6 %fusion.71 = f32[512,8,128,1]{2,0,1,3:T(8,128)S(1)} fusion(f32[512,4,128,1]{0,2,3,1:T(8,128)S(1)} %bitcast.117, f32[4,8,128,128]{3,2,1,0:T(8,128)} %bitcast.28), kind=kOutput, calls=%fused_computation.109 | convolution fusion | flops 1610612736 | bytes 5242880 | tf_op jit(solution)/shard_map/bix,ijxy->bjy/dot_general | solution.py:43
  102.8 3.6 %fusion.7 = f32[512,1024,1]{1,0,2:T(8,128)S(1)} fusion(f32[1024,8,128]{0,2,1:T(8,128)S(1)} %bitcast.114, f32[512,8,128,1]{2,0,1,3:T(8,128)S(1)} %fusion.71), kind=kOutput, calls=%fused_computation.15 | convolution fusion | flops 3221225472 | bytes 8388608 | tf_op jit(solution)/shard_map/cjy,bjy->bc/dot_general | solution.py:44
  106.4 3.5 %fusion.11 = f32[512,8,128]{0,2,1:T(8,128)S(1)} fusion(f32[1024,8,128]{0,2,1:T(8,128)S(1)} %bitcast.115, f32[1,512,1024]{2,1,0:T(8,128)S(1)} %copy-done.1, f32[1,512,1024]{2,1,0:T(8,128)S(1)} %get-tuple-element.54, f32[512,1024,1]{1,0,2:T(8,128)S(1)} %fusion.7), kind=kOutput, calls=%fused_computation.19 | convolution fusion | flops 3222274048 | bytes 12582912 | tf_op jit(solution)/shard_map/cjy,bc->bjy/dot_general | solution.py:54
  109.9 3.2 %fusion.28 = f32[4,8,128,128]{2,3,0,1:T(8,128)} fusion(f32[512,4,128,1]{0,2,1,3:T(8,128)S(1)} %bitcast.118, f32[512,8,128]{0,2,1:T(8,128)S(1)} %fusion.11), kind=kOutput, calls=%fused_computation.42 | convolution fusion | flops 1610612736 | bytes 5242880 | tf_op jit(solution)/shard_map/bix,bjy->ijxy/dot_general | solution.py:55
  113.1 2.9 %copy.61 = f32[4,8,128,128]{3,2,1,0:T(8,128)} copy(f32[4,8,128,128]{2,3,0,1:T(8,128)} %fusion.28) | data formatting | bytes 4194304 | tf_op jit(solution)/shard_map/bix,bjy->ijxy/transpose | solution.py:55
  116.0 5.2 %all-to-all-start.3 = ((f32[32,128,128]{2,1,0:T(8,128)}), f32[32,128,128]{2,1,0:T(8,128)}, u32[]{:S(2)}, u32[]{:S(2)}) async-start(f32[32,128,128]{2,1,0:T(8,128)} %bitcast.119), calls=%async_computation.3 | async-start | bytes 4194304 | tf_op jit(solution)/shard_map/all_to_all | solution.py:57
  121.2 4.4 %fusion.24 = f32[1,1,512,1024]{3,2,1,0:T(8,128)} fusion(f32[1,512,1024]{2,1,0:T(8,128)} %get-tuple-element.53, f32[1,512,1024]{2,1,0:T(8,128)S(1)} %get-tuple-element.54, f32[512,1024,1]{1,0,2:T(8,128)} %copy-done.2), kind=kLoop, calls=%fused_computation.40 | loop fusion | flops 1048576 | bytes 8388608 | tf_op jit(solution)/shard_map/broadcast_in_dim | solution.py:134
  125.6 24.0 %all-to-all-done.3 = f32[32,128,128]{2,1,0:T(8,128)} async-done(((f32[32,128,128]{2,1,0:T(8,128)}), f32[32,128,128]{2,1,0:T(8,128)}, u32[]{:S(2)}, u32[]{:S(2)}) %all-to-all-start.3) | async-done | bytes 2097184 | tf_op jit(solution)/shard_map/all_to_all | solution.py:57
  149.6 3.7 %fusion.25 = f32[1,32,128,128]{3,1,2,0:T(8,128)S(1)} fusion(f32[32,128,128]{2,1,0:T(8,128)} %all-to-all-done.3, f32[32,32]{0,1:T(8,128)S(1)} %cosine_multiply_fusion.2), kind=kOutput, calls=%fused_computation.41 | convolution fusion | flops 100663296 | bytes 4198400 | tf_op jit(solution)/shard_map/kz,kxy->zxy/dot_general | solution.py:58
  153.4 2.5 %copy.63 = f32[1,32,128,128]{3,2,1,0:T(8,128)} copy(f32[1,32,128,128]{3,1,2,0:T(8,128)S(1)} %fusion.25) | data formatting | bytes 4194304
  (40 shorter events, 2.2 us)
Async XLA Ops:
  0.6 3.3 %copy-start.3 = (f32[1,32,128,128]{3,2,1,0:T(8,128)S(1)}, f32[1,32,128,128]{3,2,1,0:T(8,128)}, u32[]{:S(2)}) copy-start(f32[1,32,128,128]{3,2,1,0:T(8,128)} %param.16) | copy-start | bytes 6291460
  0.6 3.7 %copy-start.4 = (s32[1,128,1]{1,2,0:T(1,128)S(1)}, s32[1,128,1]{1,2,0:T(1,128)}, u32[]{:S(2)}) copy-start(s32[1,128,1]{1,2,0:T(1,128)} %param.18) | copy-start | bytes 1540
  0.7 3.6 %copy-start.5 = (s32[1,128,1]{1,2,0:T(1,128)S(1)}, s32[1,128,1]{1,2,0:T(1,128)}, u32[]{:S(2)}) copy-start(s32[1,128,1]{1,2,0:T(1,128)} %param.19) | copy-start | bytes 1540
  4.0 13.5 %slice-start = ((f32[1,32,128,128]{3,2,1,0:T(8,128)}), f32[1,3,128,128]{3,2,1,0:T(8,128)S(1)}, s32[]{:S(2)}) async-start(f32[1,32,128,128]{3,2,1,0:T(8,128)} %param.16), calls=%async_computation.4 | async-start | bytes 393216 | tf_op jit(solution)/shard_map/slice | solution.py:96
  5.9 25.0 %all-to-all-start = ((f32[128,2,512]{2,1,0:T(2,128)}), f32[128,2,512]{2,1,0:T(2,128)S(1)}, u32[]{:S(2)}, u32[]{:S(2)}) async-start(f32[128,2,512]{2,1,0:T(2,128)} %all_to_all.20), calls=%async_computation | async-start | bytes 1048576 | tf_op jit(solution)/shard_map/all_to_all | solution.py:106
  33.0 21.2 %all-to-all-start.1 = ((f32[128,2,384]{2,1,0:T(2,128)}), f32[128,2,384]{2,1,0:T(2,128)S(1)}, u32[]{:S(2)}, u32[]{:S(2)}) async-start(f32[128,2,384]{2,1,0:T(2,128)} %maximum_multiply_fusion.1), calls=%async_computation.1 | async-start | bytes 786432 | tf_op jit(solution)/shard_map/all_to_all | solution.py:126
  65.1 34.1 %all-to-all-start.2 = ((f32[32,128,128]{2,1,0:T(8,128)}), f32[32,128,128]{2,1,0:T(8,128)}, u32[]{:S(2)}, u32[]{:S(2)}) async-start(f32[32,128,128]{2,1,0:T(8,128)} %copy.54), calls=%async_computation.2 | async-start | bytes 4194304 | tf_op jit(solution)/shard_map/all_to_all | solution.py:39
  99.2 3.6 %copy-start = (f32[1024,1024]{0,1:T(8,128)S(1)}, f32[1024,1024]{0,1:T(8,128)}, u32[]{:S(2)}) copy-start(f32[1024,1024]{0,1:T(8,128)} %cosine_multiply_fusion) | copy-start | bytes 12582916
  102.8 3.6 %copy-start.1 = (f32[1,512,1024]{2,1,0:T(8,128)S(1)}, f32[1,512,1024]{2,1,0:T(8,128)}, u32[]{:S(2)}) copy-start(f32[1,512,1024]{2,1,0:T(8,128)} %get-tuple-element.53) | copy-start | bytes 6291460
  106.4 3.5 %copy-start.2 = (f32[512,1024,1]{1,0,2:T(8,128)}, f32[512,1024,1]{1,0,2:T(8,128)S(1)}, u32[]{:S(2)}) copy-start(f32[512,1024,1]{1,0,2:T(8,128)S(1)} %fusion.7) | copy-start | bytes 6291460
  116.0 33.6 %all-to-all-start.3 = ((f32[32,128,128]{2,1,0:T(8,128)}), f32[32,128,128]{2,1,0:T(8,128)}, u32[]{:S(2)}, u32[]{:S(2)}) async-start(f32[32,128,128]{2,1,0:T(8,128)} %bitcast.119), calls=%async_computation.3 | async-start | bytes 4194304 | tf_op jit(solution)/shard_map/all_to_all | solution.py:57

commit v9 on v7

--- a/solution.py
+++ b/solution.py
@@ -30,17 +30,23 @@
     )
 
 
+def gy_major(table_z, width_x, width_y):
+    depth = table_z.shape[1]
+    return table_z.reshape(width_x, width_y, depth).transpose(1, 0, 2).reshape(-1, depth)
+
+
 def to_modes(field, table_z, table_x, table_y):
     width_x = lax.axis_size("gx")
     width_y = lax.axis_size("gy")
     rows_x = field.shape[2]
     cols_y = field.shape[3]
-    part = jnp.einsum("kz,zxy->kxy", table_z, field[0], precision=FAST)
-    part = lax.all_to_all(part, ("gx", "gy"), split_axis=0, concat_axis=0, tiled=True)
-    part = part.reshape(width_x, width_y, rows_x, cols_y)
+    table_p = gy_major(table_z, width_x, width_y)
+    part = jnp.einsum("kz,zxy->kxy", table_p, field[0], precision=FAST)
+    part = lax.all_to_all(part, ("gy", "gx"), split_axis=0, concat_axis=0, tiled=True)
+    part = part.reshape(width_y, width_x, rows_x, cols_y)
     split_x = table_x.reshape(table_x.shape[0], width_x, rows_x)
     split_y = table_y.reshape(table_y.shape[0], width_y, cols_y)
-    part = jnp.einsum("bix,ijxy->bjy", split_x, part, precision=FAST)
+    part = jnp.einsum("bix,jixy->bjy", split_x, part, precision=FAST)
     return jnp.einsum("cjy,bjy->bc", split_y, part, precision=FAST)[None, None]
 
 
@@ -52,10 +58,11 @@
     split_x = table_x.reshape(table_x.shape[0], width_x, rows_x)
     split_y = table_y.reshape(table_y.shape[0], width_y, cols_y)
     part = jnp.einsum("cjy,bc->bjy", split_y, modes[0, 0], precision=FAST)
-    part = jnp.einsum("bix,bjy->ijxy", split_x, part, precision=FAST)
+    part = jnp.einsum("bix,bjy->jixy", split_x, part, precision=FAST)
     part = part.reshape(width_x * width_y, rows_x, cols_y)
-    cells = lax.all_to_all(part, ("gx", "gy"), split_axis=0, concat_axis=0, tiled=True)
-    return jnp.einsum("kz,kxy->zxy", table_z, cells, precision=FAST)[None]
+    cells = lax.all_to_all(part, ("gy", "gx"), split_axis=0, concat_axis=0, tiled=True)
+    table_p = gy_major(table_z, width_x, width_y)
+    return jnp.einsum("kz,kxy->zxy", table_p, cells, precision=FAST)[None]
 
 
 def advance_terms(depth_index, depth, long_x, long_y):

time: 145 us -> 144 us (level)
  waiting for transfers between devices: 23 us -> 21.4 us
    reshape x0 -> x1, local copies, waits for them, and re-layouts: none -> 1.81 us  [to_cells(): part = part.reshape(width_x * width_y, rows_x, cols_y)]
    transpose x1, local copies, waits for them, and re-layouts: 1.81 us -> 0.01 us  [gy_major(): table_z.reshape(width_x, width_y, depth).transpose(1, 0, 2)]
    all_to_all x1, waiting for transfers between devices: 9.76 us -> 8.14 us  [to_modes(): lax.all_to_all(part, ('gy', 'gx'), split_axis=0, concat_axis=0, tiled=True)]
    unnamed x18 -> x22, local copies, waits for them, and re-layouts: 5.02 us -> 6.31 us
  transfers between devices with their start and end apart: 3 -> 3, of which waited for: 3 -> 3; matrix products, arithmetic and copies ran while one was open for 21% -> 22% of each run, Pallas kernels for 0% -> 0%
where the time goes in v9:
time: 144 us
  blocking collectives  32.9 us (23%)
  other arithmetic  31.4 us (22%)
  starting transfers between devices  24.3 us (17%)
  waiting for transfers between devices  21.4 us (15%)
  matrix products  19.8 us (14%)
  local copies, waits for them, and re-layouts  12.9 us (9%)
    all_to_all x1, blocking collectives, to_cells(): lax.all_to_all(part, ('gy', 'gx'), split_axis=0, concat_axis=0, tiled=True)  32.9 us
    mul x4, other arithmetic, cosine_table(): return scale * jnp.cos(jnp.pi * rows * (cols + 0.5) / count)  18.7 us
    all_to_all x1, starting transfers between devices, shards(): lax.all_to_all(buffer, ('grp', 'gx', 'gy'), split_axis=0, concat_axis=0,...  11.5 us
    all_to_all x1, waiting for transfers between devices, shards(): lax.all_to_all(force, ('grp', 'gx', 'gy'), split_axis=0, concat_axis=0, t...  11.4 us
    mul x1, other arithmetic, advance_terms(): return (2.0 * jnp.cos(theta), COURANT * COURANT * shape * shape)  11.3 us
    all_to_all x1, waiting for transfers between devices, to_modes(): lax.all_to_all(part, ('gy', 'gx'), split_axis=0, concat_axis=0, tiled=True)  8.14 us
    all_to_all x1, starting transfers between devices, shards(): lax.all_to_all(force, ('grp', 'gx', 'gy'), split_axis=0, concat_axis=0, t...  7.91 us
    dot_general x1, matrix products, to_modes(): return jnp.einsum('cjy,bjy->bc', split_y, part, precision=FAST)[None, None]  6.42 us
  transfers between devices with their start and end apart: 3, of which 3 were waited for; matrix products, arithmetic and copies ran while one was open for 22% of the time, Pallas kernels for 0%

profile of v9, /device:TPU:1, one launch (start us, length us, event | category | flops | bytes accessed | tf_op | source)
XLA Modules:
  0.0 143.7 jit_solution(7591922314737217437)
XLA Ops:
  0.7 1.6 %copy-done.5 = f32[1,32,128,128]{3,2,1,0:T(8,128)S(1)} copy-done((f32[1,32,128,128]{3,2,1,0:T(8,128)S(1)}, f32[1,32,128,128]{3,2,1,0:T(8,128)}, u32[]{:S(2)}) %copy-start.5) | copy-done | bytes 2097176
  2.6 0.5 fusion.35
  3.1 1.1 all_to_all.20
  4.2 11.5 %all-to-all-start = ((f32[128,2,512]{2,1,0:T(2,128)}), f32[128,2,512]{2,1,0:T(2,128)S(1)}, u32[]{:S(2)}, u32[]{:S(2)}) async-start(f32[128,2,512]{2,1,0:T(2,128)} %all_to_all.20), calls=%async_computation | async-start | bytes 1048576 | tf_op jit(solution)/shard_map/all_to_all | solution.py:115
  15.8 11.3 %multiply_multiply_fusion = (f32[1,512,1024]{2,1,0:T(8,128)}, f32[1,512,1024]{2,1,0:T(8,128)}) fusion(f32[1024]{0:T(1024)S(1)} %multiply_multiply_fusion.5, f32[512]{0:T(512)S(1)} %multiply_add_fusion.2), kind=kLoop, calls=%fused_computation.1 | loop fusion | flops 20447232 | bytes 4200448 | tf_op jit(solution)/shard_map/mul | solution.py:80
  27.4 1.9 %all-to-all-done = f32[128,2,512]{2,1,0:T(2,128)S(1)} async-done(((f32[128,2,512]{2,1,0:T(2,128)}), f32[128,2,512]{2,1,0:T(2,128)S(1)}, u32[]{:S(2)}, u32[]{:S(2)}) %all-to-all-start) | async-done | bytes 524320 | tf_op jit(solution)/shard_map/all_to_all | solution.py:115
  29.3 0.4 all_to_all.22
  29.8 0.4 convolution_subtract_fusion
  30.3 1.0 maximum_multiply_fusion.1
  31.3 7.9 %all-to-all-start.1 = ((f32[128,2,384]{2,1,0:T(2,128)}), f32[128,2,384]{2,1,0:T(2,128)S(1)}, u32[]{:S(2)}, u32[]{:S(2)}) async-start(f32[128,2,384]{2,1,0:T(2,128)} %maximum_multiply_fusion.1), calls=%async_computation.1 | async-start | bytes 786432 | tf_op jit(solution)/shard_map/all_to_all | solution.py:134
  39.2 0.6 fusion.29
  40.0 11.4 %all-to-all-done.1 = f32[128,2,384]{2,1,0:T(2,128)S(1)} async-done(((f32[128,2,384]{2,1,0:T(2,128)}), f32[128,2,384]{2,1,0:T(2,128)S(1)}, u32[]{:S(2)}, u32[]{:S(2)}) %all-to-all-start.1) | async-done | bytes 393248 | tf_op jit(solution)/shard_map/all_to_all | solution.py:134
  51.4 0.3 all_to_all.24
  51.8 0.4 fusion.47
  52.2 0.2 copy.72
  52.5 2.2 %fusion.16 = f32[32,128,128]{2,0,1:T(8,128)S(1)} fusion(f32[32,32,1]{1,0,2:T(8,128)S(1)} %bitcast.127, f32[32,128,128]{2,1,0:T(8,128)S(1)} %fusion.52), kind=kOutput, calls=%fused_computation.27 | convolution fusion | flops 100663296 | bytes 4198400 | tf_op jit(solution)/shard_map/kz,zxy->kxy/dot_general | solution.py:44
  54.6 2.6 %copy.37 = f32[32,128,128]{2,1,0:T(8,128)} copy(f32[32,128,128]{2,0,1:T(8,128)S(1)} %fusion.16) | data formatting | bytes 4194304 | tf_op jit(solution)/shard_map/kz,zxy->kxy/dot_general | solution.py:44
  57.2 4.9 %all-to-all-start.2 = ((f32[32,128,128]{2,1,0:T(8,128)}), f32[32,128,128]{2,1,0:T(8,128)S(1)}, u32[]{:S(2)}, u32[]{:S(2)}) async-start(f32[32,128,128]{2,1,0:T(8,128)} %copy.37), calls=%async_computation.2 | async-start | bytes 4194304 | tf_op jit(solution)/shard_map/all_to_all | solution.py:45
  62.2 3.5 %cosine_multiply_fusion.2 = f32[512,512]{0,1:T(8,128)S(1)} fusion(f32[512]{0:T(512)S(1)} %get-tuple-element.72, f32[512]{0:T(512)S(1)} %get-tuple-element.73, f32[512]{0:T(512)S(1)} %fusion.62), kind=kLoop, calls=%fused_computation.43 | loop fusion | flops 786432 | bytes 1054720 | tf_op jit(solution)/shard_map/mul | solution.py:16
  65.7 15.1 %cosine_multiply_fusion = f32[1024,1024]{0,1:T(8,128)} fusion(f32[1024]{0:T(1024)S(1)} %get-tuple-element.70, f32[1024]{0:T(1024)S(1)} %get-tuple-element.71, f32[1024]{0:T(1024)S(1)} %fusion.61), kind=kLoop, calls=%fused_computation | loop fusion | flops 3145728 | bytes 4206592 | tf_op jit(solution)/shard_map/mul | solution.py:16
  80.8 8.1 %all-to-all-done.2 = f32[32,128,128]{2,1,0:T(8,128)S(1)} async-done(((f32[32,128,128]{2,1,0:T(8,128)}), f32[32,128,128]{2,1,0:T(8,128)S(1)}, u32[]{:S(2)}, u32[]{:S(2)}) %all-to-all-start.2) | async-done | bytes 2097184 | tf_op jit(solution)/shard_map/all_to_all | solution.py:45
  89.0 1.9 %fusion.66 = f32[512,8,128,1]{2,0,3,1:T(8,128)S(1)} fusion(f32[512,4,128,1]{0,2,1,3:T(8,128)S(1)} %bitcast.113, f32[8,4,128,128]{3,2,1,0:T(8,128)S(1)} %bitcast.111), kind=kOutput, calls=%fused_computation.106 | convolution fusion | flops 1610612736 | bytes 5242880 | tf_op jit(solution)/shard_map/bix,jixy->bjy/dot_general | solution.py:49
  90.9 0.3 copy-done
  91.1 0.7 copy-done.2
  91.8 0.6 copy-done.3
  92.4 6.4 %fusion.11 = f32[1,512,1024]{2,1,0:T(8,128)S(1)} fusion(f32[1,512,1024]{2,1,0:T(8,128)S(1)} %copy-done.2, f32[1,1,512,1024]{3,2,1,0:T(8,128)} %param.15, f32[1,512,1024]{2,1,0:T(8,128)S(1)} %copy-done.3, f32[1,1,512,1024]{3,2,1,0:T(8,128)} %param.14, f32[1024,8,128]{0,2,1:T(8,128)S(1)} %bitcast.109, f32[512,8,128,1]{2,0,3,1:T(8,128)S(1)} %fusion.66), kind=kOutput, calls=%fused_computation.20 | convolution fusion | flops 3223322624 | bytes 16777216 | tf_op jit(solution)/shard_map/cjy,bjy->bc/dot_general | solution.py:50
  98.9 3.5 %fusion.9 = f32[512,8,128]{0,2,1:T(8,128)S(1)} fusion(f32[1024,8,128]{0,2,1:T(8,128)S(1)} %bitcast.110, f32[1,512,1024]{2,1,0:T(8,128)S(1)} %fusion.11), kind=kOutput, calls=%fused_computation.17 | convolution fusion | flops 3221225472 | bytes 8388608 | tf_op jit(solution)/shard_map/cjy,bc->bjy/dot_general | solution.py:60
  102.4 1.8 %fusion.7 = f32[8,128,4,128]{3,1,2,0:T(8,128)S(1)} fusion(f32[512,4,128,1]{0,2,1,3:T(8,128)S(1)} %bitcast.114, f32[512,8,128]{0,2,1:T(8,128)S(1)} %fusion.9), kind=kOutput, calls=%fused_computation.15 | convolution fusion | flops 1610612736 | bytes 5242880 | tf_op jit(solution)/shard_map/bix,bjy->jixy/dot_general | solution.py:61
  104.3 1.8 %copy.43 = f32[32,128,128]{2,1,0:T(8,128)} copy(f32[32,128,128]{1,2,0:T(8,128)S(1)} %bitcast.115) | data formatting | bytes 4194304 | tf_op jit(solution)/shard_map/reshape | solution.py:62
  106.1 32.9 %all_to_all.31 = f32[32,128,128]{2,1,0:T(8,128)S(1)} all-to-all(f32[32,128,128]{2,1,0:T(8,128)} %copy.43), channel_id=1, replica_groups=mesh['grp'=4,'gx'=4,'gy'=8] {'gy','gx'}, dimensions={0} | all-to-all | bytes 4194304 | tf_op jit(solution)/shard_map/all_to_all | solution.py:63
  139.0 2.1 %fusion.23 = f32[1,32,128,128]{3,1,2,0:T(8,128)S(1)} fusion(f32[32,32,1]{1,0,2:T(8,128)S(1)} %bitcast.128, f32[32,128,128]{2,1,0:T(8,128)S(1)} %all_to_all.31), kind=kOutput, calls=%fused_computation.41 | convolution fusion | flops 100663296 | bytes 4198400 | tf_op jit(solution)/shard_map/kz,kxy->zxy/dot_general | solution.py:65
  141.1 2.5 %copy.46 = f32[1,32,128,128]{3,2,1,0:T(8,128)} copy(f32[1,32,128,128]{3,1,2,0:T(8,128)S(1)} %fusion.23) | data formatting | bytes 4194304
  (42 shorter events, 1.3 us)
Async XLA Ops:
  0.6 1.6 %copy-start.5 = (f32[1,32,128,128]{3,2,1,0:T(8,128)S(1)}, f32[1,32,128,128]{3,2,1,0:T(8,128)}, u32[]{:S(2)}) copy-start(f32[1,32,128,128]{3,2,1,0:T(8,128)} %param.16) | copy-start | bytes 6291460
  0.6 2.0 %copy-start.6 = (s32[1,128,1]{1,2,0:T(1,128)S(1)}, s32[1,128,1]{1,2,0:T(1,128)}, u32[]{:S(2)}) copy-start(s32[1,128,1]{1,2,0:T(1,128)} %param.18) | copy-start | bytes 1540
  0.7 1.9 %copy-start.7 = (s32[1,128,1]{1,2,0:T(1,128)S(1)}, s32[1,128,1]{1,2,0:T(1,128)}, u32[]{:S(2)}) copy-start(s32[1,128,1]{1,2,0:T(1,128)} %param.19) | copy-start | bytes 1540
  4.2 25.0 %all-to-all-start = ((f32[128,2,512]{2,1,0:T(2,128)}), f32[128,2,512]{2,1,0:T(2,128)S(1)}, u32[]{:S(2)}, u32[]{:S(2)}) async-start(f32[128,2,512]{2,1,0:T(2,128)} %all_to_all.20), calls=%async_computation | async-start | bytes 1048576 | tf_op jit(solution)/shard_map/all_to_all | solution.py:115
  15.7 11.3 %slice-start = ((f32[1,32,128,128]{3,2,1,0:T(8,128)}), f32[1,3,128,128]{3,2,1,0:T(8,128)S(1)}, s32[]{:S(2)}) async-start(f32[1,32,128,128]{3,2,1,0:T(8,128)} %param.16), calls=%async_computation.4 | async-start | bytes 393216 | tf_op jit(solution)/shard_map/slice | solution.py:105
  29.7 10.2 %copy-start.1 = (f32[1,32,128,128]{3,2,1,0:T(8,128)S(1)}, f32[1,32,128,128]{3,2,1,0:T(8,128)}, u32[]{:S(2)}) copy-start(f32[1,32,128,128]{3,2,1,0:T(8,128)} %param.17) | copy-start | bytes 6291460
  31.3 20.1 %all-to-all-start.1 = ((f32[128,2,384]{2,1,0:T(2,128)}), f32[128,2,384]{2,1,0:T(2,128)S(1)}, u32[]{:S(2)}, u32[]{:S(2)}) async-start(f32[128,2,384]{2,1,0:T(2,128)} %maximum_multiply_fusion.1), calls=%async_computation.1 | async-start | bytes 786432 | tf_op jit(solution)/shard_map/all_to_all | solution.py:134
  57.2 31.7 %all-to-all-start.2 = ((f32[32,128,128]{2,1,0:T(8,128)}), f32[32,128,128]{2,1,0:T(8,128)S(1)}, u32[]{:S(2)}, u32[]{:S(2)}) async-start(f32[32,128,128]{2,1,0:T(8,128)} %copy.37), calls=%async_computation.2 | async-start | bytes 4194304 | tf_op jit(solution)/shard_map/all_to_all | solution.py:45
  89.0 2.2 %copy-start = (f32[1024,1024]{0,1:T(8,128)S(1)}, f32[1024,1024]{0,1:T(8,128)}, u32[]{:S(2)}) copy-start(f32[1024,1024]{0,1:T(8,128)} %cosine_multiply_fusion) | copy-start | bytes 12582916
  89.0 2.9 %copy-start.2 = (f32[1,512,1024]{2,1,0:T(8,128)S(1)}, f32[1,512,1024]{2,1,0:T(8,128)}, u32[]{:S(2)}) copy-start(f32[1,512,1024]{2,1,0:T(8,128)} %get-tuple-element.54) | copy-start | bytes 6291460
  89.0 3.5 %copy-start.3 = (f32[1,512,1024]{2,1,0:T(8,128)S(1)}, f32[1,512,1024]{2,1,0:T(8,128)}, u32[]{:S(2)}) copy-start(f32[1,512,1024]{2,1,0:T(8,128)} %get-tuple-element.53) | copy-start | bytes 6291460
  98.9 3.6 %copy-start.4 = (f32[1,512,1024]{2,1,0:T(8,128)}, f32[1,512,1024]{2,1,0:T(8,128)S(1)}, u32[]{:S(2)}) copy-start(f32[1,512,1024]{2,1,0:T(8,128)S(1)} %fusion.11) | copy-start | bytes 6291460

commit v10 on v9

--- a/solution.py
+++ b/solution.py
@@ -99,9 +99,8 @@
     scale_now, scale_spec = advance_terms(depth_index, depth, long_x, long_y)
     scale_now = lax.optimization_barrier(scale_now)
     scale_spec = lax.optimization_barrier(scale_spec)
-    top = jnp.stack(
-        [pressure_now[0, depth - 1], pressure_now[0, depth - 2], pressure_now[0, depth - 3]], axis=1
-    ).reshape(rows_x, 3 * cols_y)
+    upper = lax.optimization_barrier(lax.slice_in_dim(pressure_now[0], depth - 3, depth, axis=0))
+    top = jnp.stack([upper[2], upper[1], upper[0]], axis=1).reshape(rows_x, 3 * cols_y)
     bottom = jnp.transpose(pressure_now[0, 0:3], (1, 0, 2)).reshape(rows_x, 3 * cols_y)
     devices = lax.axis_size(("grp", "gx", "gy"))
     slots_per = max(2, rows_x // devices)

time: 144 us -> 143 us (level)
    unnamed x22 -> x18, local copies, waits for them, and re-layouts: 6.31 us -> 4.58 us
where the time goes in v10:
time: 143 us
  blocking collectives  32.9 us (23%)
  other arithmetic  31.4 us (22%)
  starting transfers between devices  24.3 us (17%)
  waiting for transfers between devices  21.4 us (15%)
  matrix products  19.8 us (14%)
  local copies, waits for them, and re-layouts  12.2 us (9%)
    all_to_all x1, blocking collectives, to_cells(): lax.all_to_all(part, ('gy', 'gx'), split_axis=0, concat_axis=0, tiled=True)  32.9 us
    mul x4, other arithmetic, cosine_table(): return scale * jnp.cos(jnp.pi * rows * (cols + 0.5) / count)  18.7 us
    all_to_all x1, starting transfers between devices, shards(): lax.all_to_all(buffer, ('grp', 'gx', 'gy'), split_axis=0, concat_axis=0,...  11.5 us
    all_to_all x1, waiting for transfers between devices, shards(): lax.all_to_all(force, ('grp', 'gx', 'gy'), split_axis=0, concat_axis=0, t...  11.4 us
    mul x1, other arithmetic, advance_terms(): return (2.0 * jnp.cos(theta), COURANT * COURANT * shape * shape)  11.3 us
    all_to_all x1, waiting for transfers between devices, to_modes(): lax.all_to_all(part, ('gy', 'gx'), split_axis=0, concat_axis=0, tiled=True)  8.13 us
    all_to_all x1, starting transfers between devices, shards(): lax.all_to_all(force, ('grp', 'gx', 'gy'), split_axis=0, concat_axis=0, t...  7.89 us
    dot_general x1, matrix products, to_modes(): return jnp.einsum('cjy,bjy->bc', split_y, part, precision=FAST)[None, None]  6.42 us
  transfers between devices with their start and end apart: 3, of which 3 were waited for; matrix products, arithmetic and copies ran while one was open for 22% of the time, Pallas kernels for 0%

profile of v10, /device:TPU:1, one launch (start us, length us, event | category | flops | bytes accessed | tf_op | source)
XLA Modules:
  0.0 142.9 jit_solution(7929566414395386203)
XLA Ops:
  0.7 1.1 fusion.65
  1.9 0.5 fusion.35
  2.4 1.1 all_to_all.20
  3.5 11.5 %all-to-all-start = ((f32[128,2,512]{2,1,0:T(2,128)}), f32[128,2,512]{2,1,0:T(2,128)S(1)}, u32[]{:S(2)}, u32[]{:S(2)}) async-start(f32[128,2,512]{2,1,0:T(2,128)} %all_to_all.20), calls=%async_computation | async-start | bytes 1048576 | tf_op jit(solution)/shard_map/all_to_all | solution.py:114
  15.1 11.3 %multiply_multiply_fusion = (f32[1,512,1024]{2,1,0:T(8,128)}, f32[1,512,1024]{2,1,0:T(8,128)}) fusion(f32[1024]{0:T(1024)S(1)} %multiply_multiply_fusion.5, f32[512]{0:T(512)S(1)} %multiply_add_fusion.2), kind=kLoop, calls=%fused_computation.1 | loop fusion | flops 20447232 | bytes 4200448 | tf_op jit(solution)/shard_map/mul | solution.py:80
  26.7 1.9 %all-to-all-done = f32[128,2,512]{2,1,0:T(2,128)S(1)} async-done(((f32[128,2,512]{2,1,0:T(2,128)}), f32[128,2,512]{2,1,0:T(2,128)S(1)}, u32[]{:S(2)}, u32[]{:S(2)}) %all-to-all-start) | async-done | bytes 524320 | tf_op jit(solution)/shard_map/all_to_all | solution.py:114
  28.6 0.4 all_to_all.22
  29.1 0.4 convolution_subtract_fusion
  29.6 1.0 maximum_multiply_fusion.1
  30.6 7.9 %all-to-all-start.1 = ((f32[128,2,384]{2,1,0:T(2,128)}), f32[128,2,384]{2,1,0:T(2,128)S(1)}, u32[]{:S(2)}, u32[]{:S(2)}) async-start(f32[128,2,384]{2,1,0:T(2,128)} %maximum_multiply_fusion.1), calls=%async_computation.1 | async-start | bytes 786432 | tf_op jit(solution)/shard_map/all_to_all | solution.py:133
  38.5 0.6 fusion.29
  39.3 11.4 %all-to-all-done.1 = f32[128,2,384]{2,1,0:T(2,128)S(1)} async-done(((f32[128,2,384]{2,1,0:T(2,128)}), f32[128,2,384]{2,1,0:T(2,128)S(1)}, u32[]{:S(2)}, u32[]{:S(2)}) %all-to-all-start.1) | async-done | bytes 393248 | tf_op jit(solution)/shard_map/all_to_all | solution.py:133
  50.7 0.3 all_to_all.24
  51.1 0.4 fusion.47
  51.5 0.2 copy.66
  51.8 2.2 %fusion.16 = f32[32,128,128]{2,0,1:T(8,128)S(1)} fusion(f32[32,32,1]{1,0,2:T(8,128)S(1)} %bitcast.129, f32[32,128,128]{2,1,0:T(8,128)S(1)} %fusion.52), kind=kOutput, calls=%fused_computation.27 | convolution fusion | flops 100663296 | bytes 4198400 | tf_op jit(solution)/shard_map/kz,zxy->kxy/dot_general | solution.py:44
  53.9 2.6 %copy.33 = f32[32,128,128]{2,1,0:T(8,128)} copy(f32[32,128,128]{2,0,1:T(8,128)S(1)} %fusion.16) | data formatting | bytes 4194304 | tf_op jit(solution)/shard_map/kz,zxy->kxy/dot_general | solution.py:44
  56.5 4.9 %all-to-all-start.2 = ((f32[32,128,128]{2,1,0:T(8,128)}), f32[32,128,128]{2,1,0:T(8,128)S(1)}, u32[]{:S(2)}, u32[]{:S(2)}) async-start(f32[32,128,128]{2,1,0:T(8,128)} %copy.33), calls=%async_computation.2 | async-start | bytes 4194304 | tf_op jit(solution)/shard_map/all_to_all | solution.py:45
  61.5 3.5 %cosine_multiply_fusion.2 = f32[512,512]{0,1:T(8,128)S(1)} fusion(f32[512]{0:T(512)S(1)} %get-tuple-element.74, f32[512]{0:T(512)S(1)} %get-tuple-element.75, f32[512]{0:T(512)S(1)} %fusion.62), kind=kLoop, calls=%fused_computation.43 | loop fusion | flops 786432 | bytes 1054720 | tf_op jit(solution)/shard_map/mul | solution.py:16
  65.0 15.1 %cosine_multiply_fusion = f32[1024,1024]{0,1:T(8,128)} fusion(f32[1024]{0:T(1024)S(1)} %get-tuple-element.72, f32[1024]{0:T(1024)S(1)} %get-tuple-element.73, f32[1024]{0:T(1024)S(1)} %fusion.61), kind=kLoop, calls=%fused_computation | loop fusion | flops 3145728 | bytes 4206592 | tf_op jit(solution)/shard_map/mul | solution.py:16
  80.1 8.1 %all-to-all-done.2 = f32[32,128,128]{2,1,0:T(8,128)S(1)} async-done(((f32[32,128,128]{2,1,0:T(8,128)}), f32[32,128,128]{2,1,0:T(8,128)S(1)}, u32[]{:S(2)}, u32[]{:S(2)}) %all-to-all-start.2) | async-done | bytes 2097184 | tf_op jit(solution)/shard_map/all_to_all | solution.py:45
  88.3 1.9 %fusion.66 = f32[512,8,128,1]{2,0,3,1:T(8,128)S(1)} fusion(f32[512,4,128,1]{0,2,1,3:T(8,128)S(1)} %bitcast.117, f32[8,4,128,128]{3,2,1,0:T(8,128)S(1)} %bitcast.115), kind=kOutput, calls=%fused_computation.109 | convolution fusion | flops 1610612736 | bytes 5242880 | tf_op jit(solution)/shard_map/bix,jixy->bjy/dot_general | solution.py:49
  90.2 0.3 copy-done
  90.4 0.7 copy-done.2
  91.1 0.6 copy-done.3
  91.7 6.4 %fusion.11 = f32[1,512,1024]{2,1,0:T(8,128)S(1)} fusion(f32[1,512,1024]{2,1,0:T(8,128)S(1)} %copy-done.2, f32[1,1,512,1024]{3,2,1,0:T(8,128)} %param.15, f32[1,512,1024]{2,1,0:T(8,128)S(1)} %copy-done.3, f32[1,1,512,1024]{3,2,1,0:T(8,128)} %param.14, f32[1024,8,128]{0,2,1:T(8,128)S(1)} %bitcast.113, f32[512,8,128,1]{2,0,3,1:T(8,128)S(1)} %fusion.66), kind=kOutput, calls=%fused_computation.20 | convolution fusion | flops 3223322624 | bytes 16777216 | tf_op jit(solution)/shard_map/cjy,bjy->bc/dot_general | solution.py:50
  98.2 3.5 %fusion.9 = f32[512,8,128]{0,2,1:T(8,128)S(1)} fusion(f32[1024,8,128]{0,2,1:T(8,128)S(1)} %bitcast.114, f32[1,512,1024]{2,1,0:T(8,128)S(1)} %fusion.11), kind=kOutput, calls=%fused_computation.17 | convolution fusion | flops 3221225472 | bytes 8388608 | tf_op jit(solution)/shard_map/cjy,bc->bjy/dot_general | solution.py:60
  101.7 1.8 %fusion.7 = f32[8,128,4,128]{3,1,2,0:T(8,128)S(1)} fusion(f32[512,4,128,1]{0,2,1,3:T(8,128)S(1)} %bitcast.118, f32[512,8,128]{0,2,1:T(8,128)S(1)} %fusion.9), kind=kOutput, calls=%fused_computation.15 | convolution fusion | flops 1610612736 | bytes 5242880 | tf_op jit(solution)/shard_map/bix,bjy->jixy/dot_general | solution.py:61
  103.6 1.8 %copy.39 = f32[32,128,128]{2,1,0:T(8,128)} copy(f32[32,128,128]{1,2,0:T(8,128)S(1)} %bitcast.119) | data formatting | bytes 4194304 | tf_op jit(solution)/shard_map/reshape | solution.py:62
  105.4 32.9 %all_to_all.31 = f32[32,128,128]{2,1,0:T(8,128)S(1)} all-to-all(f32[32,128,128]{2,1,0:T(8,128)} %copy.39), channel_id=1, replica_groups=mesh['grp'=4,'gx'=4,'gy'=8] {'gy','gx'}, dimensions={0} | all-to-all | bytes 4194304 | tf_op jit(solution)/shard_map/all_to_all | solution.py:63
  138.3 2.1 %fusion.23 = f32[1,32,128,128]{3,1,2,0:T(8,128)S(1)} fusion(f32[32,32,1]{1,0,2:T(8,128)S(1)} %bitcast.130, f32[32,128,128]{2,1,0:T(8,128)S(1)} %all_to_all.31), kind=kOutput, calls=%fused_computation.41 | convolution fusion | flops 100663296 | bytes 4198400 | tf_op jit(solution)/shard_map/kz,kxy->zxy/dot_general | solution.py:65
  140.4 2.5 %copy.42 = f32[1,32,128,128]{3,2,1,0:T(8,128)} copy(f32[1,32,128,128]{3,1,2,0:T(8,128)S(1)} %fusion.23) | data formatting | bytes 4194304
  (37 shorter events, 1.2 us)
Async XLA Ops:
  0.6 1.3 copy-start.5
  0.6 1.2 copy-start.6
  3.5 25.0 %all-to-all-start = ((f32[128,2,512]{2,1,0:T(2,128)}), f32[128,2,512]{2,1,0:T(2,128)S(1)}, u32[]{:S(2)}, u32[]{:S(2)}) async-start(f32[128,2,512]{2,1,0:T(2,128)} %all_to_all.20), calls=%async_computation | async-start | bytes 1048576 | tf_op jit(solution)/shard_map/all_to_all | solution.py:114
  29.1 10.2 %copy-start.1 = (f32[1,32,128,128]{3,2,1,0:T(8,128)S(1)}, f32[1,32,128,128]{3,2,1,0:T(8,128)}, u32[]{:S(2)}) copy-start(f32[1,32,128,128]{3,2,1,0:T(8,128)} %param.17) | copy-start | bytes 6291460
  30.6 20.0 %all-to-all-start.1 = ((f32[128,2,384]{2,1,0:T(2,128)}), f32[128,2,384]{2,1,0:T(2,128)S(1)}, u32[]{:S(2)}, u32[]{:S(2)}) async-start(f32[128,2,384]{2,1,0:T(2,128)} %maximum_multiply_fusion.1), calls=%async_computation.1 | async-start | bytes 786432 | tf_op jit(solution)/shard_map/all_to_all | solution.py:133
  56.5 31.7 %all-to-all-start.2 = ((f32[32,128,128]{2,1,0:T(8,128)}), f32[32,128,128]{2,1,0:T(8,128)S(1)}, u32[]{:S(2)}, u32[]{:S(2)}) async-start(f32[32,128,128]{2,1,0:T(8,128)} %copy.33), calls=%async_computation.2 | async-start | bytes 4194304 | tf_op jit(solution)/shard_map/all_to_all | solution.py:45
  88.2 2.2 %copy-start = (f32[1024,1024]{0,1:T(8,128)S(1)}, f32[1024,1024]{0,1:T(8,128)}, u32[]{:S(2)}) copy-start(f32[1024,1024]{0,1:T(8,128)} %cosine_multiply_fusion) | copy-start | bytes 12582916
  88.2 2.9 %copy-start.2 = (f32[1,512,1024]{2,1,0:T(8,128)S(1)}, f32[1,512,1024]{2,1,0:T(8,128)}, u32[]{:S(2)}) copy-start(f32[1,512,1024]{2,1,0:T(8,128)} %get-tuple-element.54) | copy-start | bytes 6291460
  88.2 3.5 %copy-start.3 = (f32[1,512,1024]{2,1,0:T(8,128)S(1)}, f32[1,512,1024]{2,1,0:T(8,128)}, u32[]{:S(2)}) copy-start(f32[1,512,1024]{2,1,0:T(8,128)} %get-tuple-element.53) | copy-start | bytes 6291460
  98.1 3.6 %copy-start.4 = (f32[1,512,1024]{2,1,0:T(8,128)}, f32[1,512,1024]{2,1,0:T(8,128)S(1)}, u32[]{:S(2)}) copy-start(f32[1,512,1024]{2,1,0:T(8,128)S(1)} %fusion.11) | copy-start | bytes 6291460

commit v11 on v10

--- a/solution.py
+++ b/solution.py
@@ -76,8 +76,10 @@
         * jnp.pi
         * jnp.sqrt(part_z[:, None, None] + part_x[None, :, None] + part_y[None, None, :])
     )
-    shape = jnp.sinc(theta / (2.0 * jnp.pi))
-    return 2.0 * jnp.cos(theta), COURANT * COURANT * shape * shape
+    turns = theta / (2.0 * jnp.pi)
+    shape = jnp.sinc(turns)
+    half_sine = jnp.pi * turns * shape
+    return 2.0 * (1.0 - 2.0 * half_sine * half_sine), COURANT * COURANT * shape * shape
 
 
 def one_hot(index, count):

time: 143 us -> 140 us (0.979)
  waiting for transfers between devices: 21.4 us -> 27.8 us
  other arithmetic: 31.4 us -> 25 us
  starting transfers between devices: 24.3 us -> 21.1 us
    mul x1, other arithmetic: 11.3 us -> 4.97 us  [advance_terms(): COURANT * COURANT * shape * shape]
    all_to_all x1, waiting for transfers between devices: 1.88 us -> 8.24 us  [shards(): lax.all_to_all(buffer, ('grp', 'gx', 'gy'), split_axis=0, concat_axis=0,...]
    all_to_all x1, starting transfers between devices: 7.89 us -> 4.71 us  [shards(): lax.all_to_all(force, ('grp', 'gx', 'gy'), split_axis=0, concat_axis=0, t...]
  transfers between devices with their start and end apart: 3 -> 3, of which waited for: 3 -> 3; matrix products, arithmetic and copies ran while one was open for 22% -> 18% of each run, Pallas kernels for 0% -> 0%
where the time goes in v11:
time: 140 us
  blocking collectives  32.9 us (24%)
  waiting for transfers between devices  27.8 us (20%)
  other arithmetic  25 us (18%)
  starting transfers between devices  21.1 us (15%)
  matrix products  19.8 us (14%)
  local copies, waits for them, and re-layouts  12.2 us (9%)
    all_to_all x1, blocking collectives, to_cells(): lax.all_to_all(part, ('gy', 'gx'), split_axis=0, concat_axis=0, tiled=True)  32.9 us
    mul x4, other arithmetic, cosine_table(): return scale * jnp.cos(jnp.pi * rows * (cols + 0.5) / count)  18.7 us
    all_to_all x1, starting transfers between devices, shards(): lax.all_to_all(buffer, ('grp', 'gx', 'gy'), split_axis=0, concat_axis=0,...  11.5 us
    all_to_all x1, waiting for transfers between devices, shards(): lax.all_to_all(force, ('grp', 'gx', 'gy'), split_axis=0, concat_axis=0, t...  11.4 us
    all_to_all x1, waiting for transfers between devices, shards(): lax.all_to_all(buffer, ('grp', 'gx', 'gy'), split_axis=0, concat_axis=0,...  8.24 us
    all_to_all x1, waiting for transfers between devices, to_modes(): lax.all_to_all(part, ('gy', 'gx'), split_axis=0, concat_axis=0, tiled=True)  8.13 us
    dot_general x1, matrix products, to_modes(): return jnp.einsum('cjy,bjy->bc', split_y, part, precision=FAST)[None, None]  6.42 us
    mul x1, other arithmetic, advance_terms(): COURANT * COURANT * shape * shape  4.97 us
  transfers between devices with their start and end apart: 3, of which 3 were waited for; matrix products, arithmetic and copies ran while one was open for 18% of the time, Pallas kernels for 0%

profile of v11, /device:TPU:1, one launch (start us, length us, event | category | flops | bytes accessed | tf_op | source)
XLA Modules:
  0.0 139.9 jit_solution(9592219234091220647)
XLA Ops:
  0.7 1.1 fusion.67
  1.9 0.5 fusion.37
  2.4 1.1 all_to_all.20
  3.5 11.5 %all-to-all-start = ((f32[128,2,512]{2,1,0:T(2,128)}), f32[128,2,512]{2,1,0:T(2,128)S(1)}, u32[]{:S(2)}, u32[]{:S(2)}) async-start(f32[128,2,512]{2,1,0:T(2,128)} %all_to_all.20), calls=%async_computation | async-start | bytes 1048576 | tf_op jit(solution)/shard_map/all_to_all | solution.py:116
  15.1 5.0 %multiply_multiply_fusion = (f32[1,512,1024]{2,1,0:T(8,128)}, f32[1,512,1024]{2,1,0:T(8,128)}) fusion(f32[1024]{0:T(1024)S(1)} %multiply_multiply_fusion.6, f32[512]{0:T(512)S(1)} %multiply_add_fusion.2), kind=kLoop, calls=%fused_computation.1 | loop fusion | flops 22544384 | bytes 4200448 | tf_op jit(solution)/shard_map/mul | solution.py:82
  20.3 8.2 %all-to-all-done = f32[128,2,512]{2,1,0:T(2,128)S(1)} async-done(((f32[128,2,512]{2,1,0:T(2,128)}), f32[128,2,512]{2,1,0:T(2,128)S(1)}, u32[]{:S(2)}, u32[]{:S(2)}) %all-to-all-start) | async-done | bytes 524320 | tf_op jit(solution)/shard_map/all_to_all | solution.py:116
  28.6 0.4 all_to_all.22
  29.1 0.4 convolution_subtract_fusion
  29.6 1.0 maximum_multiply_fusion.1
  30.6 4.7 %all-to-all-start.1 = ((f32[128,2,384]{2,1,0:T(2,128)}), f32[128,2,384]{2,1,0:T(2,128)S(1)}, u32[]{:S(2)}, u32[]{:S(2)}) async-start(f32[128,2,384]{2,1,0:T(2,128)} %maximum_multiply_fusion.1), calls=%async_computation.1 | async-start | bytes 786432 | tf_op jit(solution)/shard_map/all_to_all | solution.py:135
  35.4 0.6 fusion.31
  36.2 11.4 %all-to-all-done.1 = f32[128,2,384]{2,1,0:T(2,128)S(1)} async-done(((f32[128,2,384]{2,1,0:T(2,128)}), f32[128,2,384]{2,1,0:T(2,128)S(1)}, u32[]{:S(2)}, u32[]{:S(2)}) %all-to-all-start.1) | async-done | bytes 393248 | tf_op jit(solution)/shard_map/all_to_all | solution.py:135
  47.6 0.3 all_to_all.24
  48.0 0.4 fusion.49
  48.5 0.2 copy.66
  48.7 2.2 %fusion.18 = f32[32,128,128]{2,0,1:T(8,128)S(1)} fusion(f32[32,32,1]{1,0,2:T(8,128)S(1)} %bitcast.129, f32[32,128,128]{2,1,0:T(8,128)S(1)} %fusion.54), kind=kOutput, calls=%fused_computation.30 | convolution fusion | flops 100663296 | bytes 4198400 | tf_op jit(solution)/shard_map/kz,zxy->kxy/dot_general | solution.py:44
  50.8 2.6 %copy.33 = f32[32,128,128]{2,1,0:T(8,128)} copy(f32[32,128,128]{2,0,1:T(8,128)S(1)} %fusion.18) | data formatting | bytes 4194304 | tf_op jit(solution)/shard_map/kz,zxy->kxy/dot_general | solution.py:44
  53.4 4.9 %all-to-all-start.2 = ((f32[32,128,128]{2,1,0:T(8,128)}), f32[32,128,128]{2,1,0:T(8,128)S(1)}, u32[]{:S(2)}, u32[]{:S(2)}) async-start(f32[32,128,128]{2,1,0:T(8,128)} %copy.33), calls=%async_computation.2 | async-start | bytes 4194304 | tf_op jit(solution)/shard_map/all_to_all | solution.py:45
  58.4 3.5 %cosine_multiply_fusion.1 = f32[512,512]{0,1:T(8,128)S(1)} fusion(f32[512]{0:T(512)S(1)} %get-tuple-element.74, f32[512]{0:T(512)S(1)} %get-tuple-element.75, f32[512]{0:T(512)S(1)} %fusion.64), kind=kLoop, calls=%fused_computation.45 | loop fusion | flops 786432 | bytes 1054720 | tf_op jit(solution)/shard_map/mul | solution.py:16
  61.9 15.1 %cosine_multiply_fusion = f32[1024,1024]{0,1:T(8,128)} fusion(f32[1024]{0:T(1024)S(1)} %get-tuple-element.72, f32[1024]{0:T(1024)S(1)} %get-tuple-element.73, f32[1024]{0:T(1024)S(1)} %fusion.63), kind=kLoop, calls=%fused_computation | loop fusion | flops 3145728 | bytes 4206592 | tf_op jit(solution)/shard_map/mul | solution.py:16
  77.0 8.1 %all-to-all-done.2 = f32[32,128,128]{2,1,0:T(8,128)S(1)} async-done(((f32[32,128,128]{2,1,0:T(8,128)}), f32[32,128,128]{2,1,0:T(8,128)S(1)}, u32[]{:S(2)}, u32[]{:S(2)}) %all-to-all-start.2) | async-done | bytes 2097184 | tf_op jit(solution)/shard_map/all_to_all | solution.py:45
  85.2 1.9 %fusion.68 = f32[512,8,128,1]{2,0,3,1:T(8,128)S(1)} fusion(f32[512,4,128,1]{0,2,1,3:T(8,128)S(1)} %bitcast.117, f32[8,4,128,128]{3,2,1,0:T(8,128)S(1)} %bitcast.115), kind=kOutput, calls=%fused_computation.111 | convolution fusion | flops 1610612736 | bytes 5242880 | tf_op jit(solution)/shard_map/bix,jixy->bjy/dot_general | solution.py:49
  87.1 0.3 copy-done
  87.3 0.7 copy-done.2
  88.0 0.6 copy-done.3
  88.6 6.4 %fusion.13 = f32[1,512,1024]{2,1,0:T(8,128)S(1)} fusion(f32[1,512,1024]{2,1,0:T(8,128)S(1)} %copy-done.2, f32[1,1,512,1024]{3,2,1,0:T(8,128)} %param.15, f32[1,512,1024]{2,1,0:T(8,128)S(1)} %copy-done.3, f32[1,1,512,1024]{3,2,1,0:T(8,128)} %param.14, f32[1024,8,128]{0,2,1:T(8,128)S(1)} %bitcast.113, f32[512,8,128,1]{2,0,3,1:T(8,128)S(1)} %fusion.68), kind=kOutput, calls=%fused_computation.23 | convolution fusion | flops 3223322624 | bytes 16777216 | tf_op jit(solution)/shard_map/cjy,bjy->bc/dot_general | solution.py:50
  95.1 3.5 %fusion.11 = f32[512,8,128]{0,2,1:T(8,128)S(1)} fusion(f32[1024,8,128]{0,2,1:T(8,128)S(1)} %bitcast.114, f32[1,512,1024]{2,1,0:T(8,128)S(1)} %fusion.13), kind=kOutput, calls=%fused_computation.20 | convolution fusion | flops 3221225472 | bytes 8388608 | tf_op jit(solution)/shard_map/cjy,bc->bjy/dot_general | solution.py:60
  98.6 1.8 %fusion.9 = f32[8,128,4,128]{3,1,2,0:T(8,128)S(1)} fusion(f32[512,4,128,1]{0,2,1,3:T(8,128)S(1)} %bitcast.118, f32[512,8,128]{0,2,1:T(8,128)S(1)} %fusion.11), kind=kOutput, calls=%fused_computation.18 | convolution fusion | flops 1610612736 | bytes 5242880 | tf_op jit(solution)/shard_map/bix,bjy->jixy/dot_general | solution.py:61
  100.5 1.8 %copy.39 = f32[32,128,128]{2,1,0:T(8,128)} copy(f32[32,128,128]{1,2,0:T(8,128)S(1)} %bitcast.119) | data formatting | bytes 4194304 | tf_op jit(solution)/shard_map/reshape | solution.py:62
  102.3 32.9 %all_to_all.31 = f32[32,128,128]{2,1,0:T(8,128)S(1)} all-to-all(f32[32,128,128]{2,1,0:T(8,128)} %copy.39), channel_id=1, replica_groups=mesh['grp'=4,'gx'=4,'gy'=8] {'gy','gx'}, dimensions={0} | all-to-all | bytes 4194304 | tf_op jit(solution)/shard_map/all_to_all | solution.py:63
  135.2 2.1 %fusion.25 = f32[1,32,128,128]{3,1,2,0:T(8,128)S(1)} fusion(f32[32,32,1]{1,0,2:T(8,128)S(1)} %bitcast.130, f32[32,128,128]{2,1,0:T(8,128)S(1)} %all_to_all.31), kind=kOutput, calls=%fused_computation.43 | convolution fusion | flops 100663296 | bytes 4198400 | tf_op jit(solution)/shard_map/kz,kxy->zxy/dot_general | solution.py:65
  137.3 2.5 %copy.42 = f32[1,32,128,128]{3,2,1,0:T(8,128)} copy(f32[1,32,128,128]{3,1,2,0:T(8,128)S(1)} %fusion.25) | data formatting | bytes 4194304
  (37 shorter events, 1.2 us)
Async XLA Ops:
  0.6 1.3 copy-start.5
  0.6 1.2 copy-start.6
  3.5 25.0 %all-to-all-start = ((f32[128,2,512]{2,1,0:T(2,128)}), f32[128,2,512]{2,1,0:T(2,128)S(1)}, u32[]{:S(2)}, u32[]{:S(2)}) async-start(f32[128,2,512]{2,1,0:T(2,128)} %all_to_all.20), calls=%async_computation | async-start | bytes 1048576 | tf_op jit(solution)/shard_map/all_to_all | solution.py:116
  29.1 7.0 %copy-start.1 = (f32[1,32,128,128]{3,2,1,0:T(8,128)S(1)}, f32[1,32,128,128]{3,2,1,0:T(8,128)}, u32[]{:S(2)}) copy-start(f32[1,32,128,128]{3,2,1,0:T(8,128)} %param.17) | copy-start | bytes 6291460
  30.6 17.0 %all-to-all-start.1 = ((f32[128,2,384]{2,1,0:T(2,128)}), f32[128,2,384]{2,1,0:T(2,128)S(1)}, u32[]{:S(2)}, u32[]{:S(2)}) async-start(f32[128,2,384]{2,1,0:T(2,128)} %maximum_multiply_fusion.1), calls=%async_computation.1 | async-start | bytes 786432 | tf_op jit(solution)/shard_map/all_to_all | solution.py:135
  53.4 31.7 %all-to-all-start.2 = ((f32[32,128,128]{2,1,0:T(8,128)}), f32[32,128,128]{2,1,0:T(8,128)S(1)}, u32[]{:S(2)}, u32[]{:S(2)}) async-start(f32[32,128,128]{2,1,0:T(8,128)} %copy.33), calls=%async_computation.2 | async-start | bytes 4194304 | tf_op jit(solution)/shard_map/all_to_all | solution.py:45
  85.2 2.2 %copy-start = (f32[1024,1024]{0,1:T(8,128)S(1)}, f32[1024,1024]{0,1:T(8,128)}, u32[]{:S(2)}) copy-start(f32[1024,1024]{0,1:T(8,128)} %cosine_multiply_fusion) | copy-start | bytes 12582916
  85.2 2.9 %copy-start.2 = (f32[1,512,1024]{2,1,0:T(8,128)S(1)}, f32[1,512,1024]{2,1,0:T(8,128)}, u32[]{:S(2)}) copy-start(f32[1,512,1024]{2,1,0:T(8,128)} %get-tuple-element.54) | copy-start | bytes 6291460
  85.2 3.5 %copy-start.3 = (f32[1,512,1024]{2,1,0:T(8,128)S(1)}, f32[1,512,1024]{2,1,0:T(8,128)}, u32[]{:S(2)}) copy-start(f32[1,512,1024]{2,1,0:T(8,128)} %get-tuple-element.53) | copy-start | bytes 6291460
  95.1 3.6 %copy-start.4 = (f32[1,512,1024]{2,1,0:T(8,128)}, f32[1,512,1024]{2,1,0:T(8,128)S(1)}, u32[]{:S(2)}) copy-start(f32[1,512,1024]{2,1,0:T(8,128)S(1)} %fusion.13) | copy-start | bytes 6291460

commit v12 on v11

--- a/solution.py
+++ b/solution.py
@@ -135,10 +135,15 @@
     back = lax.all_to_all(force, ("grp", "gx", "gy"), split_axis=0, concat_axis=0, tiled=True)
     top_force = jnp.einsum("sk,kf->sf", send, back, precision=HIGH).reshape(rows_x, 3, cols_y)
     bottom_force = jnp.einsum("kr,kf->rf", meet, -force, precision=HIGH).reshape(rows_x, 3, cols_y)
-    forcing = source.at[:, 0:3].add(jnp.transpose(bottom_force, (1, 0, 2))[None])
-    forcing = forcing.at[:, depth - 1].add(top_force[:, 0][None])
-    forcing = forcing.at[:, depth - 2].add(top_force[:, 1][None])
-    forcing = forcing.at[:, depth - 3].add(top_force[:, 2][None])
+    upper_force = jnp.stack([top_force[:, 2], top_force[:, 1], top_force[:, 0]], axis=0)
+    forcing = jnp.concatenate(
+        [
+            source[0, 0:3] + jnp.transpose(bottom_force, (1, 0, 2)),
+            source[0, 3 : depth - 3],
+            source[0, depth - 3 :] + upper_force,
+        ],
+        axis=0,
+    )[None]
     spectrum = to_modes(forcing, table_z, table_x, table_y)
     modes_new = (scale_now * modes_now[0] - modes_old[0] + scale_spec * spectrum[0])[None]
     pressure_next = to_cells(modes_new, table_z, table_x, table_y)

time: 140 us -> 142 us (1.014)
  waiting for transfers between devices: 27.8 us -> 23.7 us
  local copies, waits for them, and re-layouts: 12.2 us -> 16 us
  other arithmetic: 25 us -> 26.7 us
    all_to_all x1, waiting for transfers between devices: 8.24 us -> 4.35 us  [shards(): lax.all_to_all(buffer, ('grp', 'gx', 'gy'), split_axis=0, concat_axis=0,...]
    unnamed x18 -> x16, local copies, waits for them, and re-layouts: 4.58 us -> 6.83 us
  transfers between devices with their start and end apart: 3 -> 3, of which waited for: 3 -> 3; matrix products, arithmetic and copies ran while one was open for 18% -> 20% of each run, Pallas kernels for 0% -> 0%
where the time goes in v12:
time: 142 us
  blocking collectives  32.9 us (23%)
  other arithmetic  26.7 us (19%)
  waiting for transfers between devices  23.7 us (17%)
  starting transfers between devices  21.8 us (15%)
  matrix products  19.4 us (14%)
  local copies, waits for them, and re-layouts  16 us (11%)
    all_to_all x1, blocking collectives, to_cells(): lax.all_to_all(part, ('gy', 'gx'), split_axis=0, concat_axis=0, tiled=True)  32.9 us
    mul x4, other arithmetic, cosine_table(): return scale * jnp.cos(jnp.pi * rows * (cols + 0.5) / count)  18.7 us
    all_to_all x1, starting transfers between devices, shards(): lax.all_to_all(buffer, ('grp', 'gx', 'gy'), split_axis=0, concat_axis=0,...  11.5 us
    all_to_all x1, waiting for transfers between devices, shards(): lax.all_to_all(force, ('grp', 'gx', 'gy'), split_axis=0, concat_axis=0, t...  11.2 us
    all_to_all x1, waiting for transfers between devices, to_modes(): lax.all_to_all(part, ('gy', 'gx'), split_axis=0, concat_axis=0, tiled=True)  8.14 us
    unnamed x16, local copies, waits for them, and re-layouts  6.83 us
    dot_general x1, matrix products, to_modes(): return jnp.einsum('cjy,bjy->bc', split_y, part, precision=FAST)[None, None]  6.42 us
    all_to_all x1, starting transfers between devices, shards(): lax.all_to_all(force, ('grp', 'gx', 'gy'), split_axis=0, concat_axis=0, t...  5.43 us
  transfers between devices with their start and end apart: 3, of which 3 were waited for; matrix products, arithmetic and copies ran while one was open for 20% of the time, Pallas kernels for 0%

profile of v12, /device:TPU:1, one launch (start us, length us, event | category | flops | bytes accessed | tf_op | source)
XLA Modules:
  0.0 141.5 jit_solution(10650836582483068167)
XLA Ops:
  0.6 1.0 fusion.65
  1.8 0.7 convert_bitcast_fusion
  2.5 1.1 fusion.41
  3.7 1.1 all_to_all.20
  4.8 11.5 %all-to-all-start = ((f32[128,2,512]{2,1,0:T(2,128)}), f32[128,2,512]{2,1,0:T(2,128)S(1)}, u32[]{:S(2)}, u32[]{:S(2)}) async-start(f32[128,2,512]{2,1,0:T(2,128)} %all_to_all.20), calls=%async_computation | async-start | bytes 1048576 | tf_op jit(solution)/shard_map/all_to_all | solution.py:116
  16.3 5.0 %multiply_multiply_fusion = (f32[1,512,1024]{2,1,0:T(8,128)}, f32[1,512,1024]{2,1,0:T(8,128)}) fusion(f32[1024]{0:T(1024)S(1)} %multiply_multiply_fusion.6, f32[512]{0:T(512)S(1)} %multiply_add_fusion.2), kind=kLoop, calls=%fused_computation.1 | loop fusion | flops 22544384 | bytes 4200448 | tf_op jit(solution)/shard_map/mul | solution.py:82
  21.3 1.4 slice.63
  23.0 2.5 %copy.72 = f32[1,26,128,128]{3,1,2,0:T(8,128)S(1)} copy(f32[1,26,128,128]{3,2,1,0:T(8,128)} %slice.63) | data formatting | bytes 3407872
  25.5 4.4 %all-to-all-done = f32[128,2,512]{2,1,0:T(2,128)S(1)} async-done(((f32[128,2,512]{2,1,0:T(2,128)}), f32[128,2,512]{2,1,0:T(2,128)S(1)}, u32[]{:S(2)}, u32[]{:S(2)}) %all-to-all-start) | async-done | bytes 524320 | tf_op jit(solution)/shard_map/all_to_all | solution.py:116
  29.8 0.4 all_to_all.22
  30.9 1.0 maximum_multiply_fusion.1
  31.9 5.4 %all-to-all-start.1 = ((f32[128,2,384]{2,1,0:T(2,128)}), f32[128,2,384]{2,1,0:T(2,128)S(1)}, u32[]{:S(2)}, u32[]{:S(2)}) async-start(f32[128,2,384]{2,1,0:T(2,128)} %maximum_multiply_fusion.1), calls=%async_computation.1 | async-start | bytes 786432 | tf_op jit(solution)/shard_map/all_to_all | solution.py:135
  37.3 0.6 fusion.35
  38.2 11.2 %all-to-all-done.1 = f32[128,2,384]{2,1,0:T(2,128)S(1)} async-done(((f32[128,2,384]{2,1,0:T(2,128)}), f32[128,2,384]{2,1,0:T(2,128)S(1)}, u32[]{:S(2)}, u32[]{:S(2)}) %all-to-all-start.1) | async-done | bytes 393248 | tf_op jit(solution)/shard_map/all_to_all | solution.py:135
  49.9 0.4 fusion.53
  50.3 1.0 maximum_add_fusion
  51.4 1.1 fusion.9
  52.5 2.6 %copy.38 = f32[32,128,128]{2,1,0:T(8,128)} copy(f32[32,128,128]{2,0,1:T(8,128)S(1)} %fusion.9) | data formatting | bytes 4194304 | tf_op jit(solution)/shard_map/kz,zxy->kxy/dot_general | solution.py:44
  55.0 4.9 %all-to-all-start.2 = ((f32[32,128,128]{2,1,0:T(8,128)}), f32[32,128,128]{2,1,0:T(8,128)S(1)}, u32[]{:S(2)}, u32[]{:S(2)}) async-start(f32[32,128,128]{2,1,0:T(8,128)} %copy.38), calls=%async_computation.2 | async-start | bytes 4194304 | tf_op jit(solution)/shard_map/all_to_all | solution.py:45
  60.0 3.5 %cosine_multiply_fusion.1 = f32[512,512]{0,1:T(8,128)S(1)} fusion(f32[512]{0:T(512)S(1)} %get-tuple-element.29, f32[512]{0:T(512)S(1)} %get-tuple-element.30, f32[512]{0:T(512)S(1)} %fusion.61), kind=kLoop, calls=%fused_computation.50 | loop fusion | flops 786432 | bytes 1054720 | tf_op jit(solution)/shard_map/mul | solution.py:16
  63.6 15.1 %cosine_multiply_fusion = f32[1024,1024]{0,1:T(8,128)} fusion(f32[1024]{0:T(1024)S(1)} %get-tuple-element.27, f32[1024]{0:T(1024)S(1)} %get-tuple-element.28, f32[1024]{0:T(1024)S(1)} %fusion.60), kind=kLoop, calls=%fused_computation | loop fusion | flops 3145728 | bytes 4206592 | tf_op jit(solution)/shard_map/mul | solution.py:16
  78.6 8.1 %all-to-all-done.2 = f32[32,128,128]{2,1,0:T(8,128)S(1)} async-done(((f32[32,128,128]{2,1,0:T(8,128)}), f32[32,128,128]{2,1,0:T(8,128)S(1)}, u32[]{:S(2)}, u32[]{:S(2)}) %all-to-all-start.2) | async-done | bytes 2097184 | tf_op jit(solution)/shard_map/all_to_all | solution.py:45
  86.8 1.9 %fusion.66 = f32[512,8,128,1]{2,0,3,1:T(8,128)S(1)} fusion(f32[512,4,128,1]{0,2,1,3:T(8,128)S(1)} %bitcast.102, f32[8,4,128,128]{3,2,1,0:T(8,128)S(1)} %bitcast.101), kind=kOutput, calls=%fused_computation.111 | convolution fusion | flops 1610612736 | bytes 5242880 | tf_op jit(solution)/shard_map/bix,jixy->bjy/dot_general | solution.py:49
  89.0 0.7 copy-done.1
  89.7 0.6 copy-done.2
  90.3 6.4 %fusion.19 = f32[1,512,1024]{2,1,0:T(8,128)S(1)} fusion(f32[1,512,1024]{2,1,0:T(8,128)S(1)} %copy-done.1, f32[1,1,512,1024]{3,2,1,0:T(8,128)} %param.7, f32[1,512,1024]{2,1,0:T(8,128)S(1)} %copy-done.2, f32[1,1,512,1024]{3,2,1,0:T(8,128)} %param.6, f32[1024,8,128]{0,2,1:T(8,128)S(1)} %bitcast.99, f32[512,8,128,1]{2,0,3,1:T(8,128)S(1)} %fusion.66), kind=kOutput, calls=%fused_computation.30 | convolution fusion | flops 3223322624 | bytes 16777216 | tf_op jit(solution)/shard_map/cjy,bjy->bc/dot_general | solution.py:50
  96.7 3.6 %fusion.17 = f32[512,8,128]{0,2,1:T(8,128)S(1)} fusion(f32[1024,8,128]{0,2,1:T(8,128)S(1)} %bitcast.100, f32[1,512,1024]{2,1,0:T(8,128)S(1)} %fusion.19), kind=kOutput, calls=%fused_computation.27 | convolution fusion | flops 3221225472 | bytes 8388608 | tf_op jit(solution)/shard_map/cjy,bc->bjy/dot_general | solution.py:60
  100.3 1.8 %fusion.15 = f32[8,128,4,128]{3,1,2,0:T(8,128)S(1)} fusion(f32[512,4,128,1]{0,2,1,3:T(8,128)S(1)} %bitcast.103, f32[512,8,128]{0,2,1:T(8,128)S(1)} %fusion.17), kind=kOutput, calls=%fused_computation.25 | convolution fusion | flops 1610612736 | bytes 5242880 | tf_op jit(solution)/shard_map/bix,bjy->jixy/dot_general | solution.py:61
  102.1 1.8 %copy.44 = f32[32,128,128]{2,1,0:T(8,128)} copy(f32[32,128,128]{1,2,0:T(8,128)S(1)} %bitcast.105) | data formatting | bytes 4194304 | tf_op jit(solution)/shard_map/reshape | solution.py:62
  103.9 32.9 %all_to_all.31 = f32[32,128,128]{2,1,0:T(8,128)S(1)} all-to-all(f32[32,128,128]{2,1,0:T(8,128)} %copy.44), channel_id=1, replica_groups=mesh['grp'=4,'gx'=4,'gy'=8] {'gy','gx'}, dimensions={0} | all-to-all | bytes 4194304 | tf_op jit(solution)/shard_map/all_to_all | solution.py:63
  136.8 2.1 %fusion.29 = f32[1,32,128,128]{3,1,2,0:T(8,128)S(1)} fusion(f32[32,32,1]{1,0,2:T(8,128)S(1)} %bitcast.116, f32[32,128,128]{2,1,0:T(8,128)S(1)} %all_to_all.31), kind=kOutput, calls=%fused_computation.48 | convolution fusion | flops 100663296 | bytes 4198400 | tf_op jit(solution)/shard_map/kz,kxy->zxy/dot_general | solution.py:65
  139.0 2.5 %copy.47 = f32[1,32,128,128]{3,2,1,0:T(8,128)} copy(f32[1,32,128,128]{3,1,2,0:T(8,128)S(1)} %fusion.29) | data formatting | bytes 4194304
  (38 shorter events, 2.3 us)
Async XLA Ops:
  4.8 25.0 %all-to-all-start = ((f32[128,2,512]{2,1,0:T(2,128)}), f32[128,2,512]{2,1,0:T(2,128)S(1)}, u32[]{:S(2)}, u32[]{:S(2)}) async-start(f32[128,2,512]{2,1,0:T(2,128)} %all_to_all.20), calls=%async_computation | async-start | bytes 1048576 | tf_op jit(solution)/shard_map/all_to_all | solution.py:116
  16.3 5.0 %copy-start.4 = (f32[1,32,128,128]{3,2,1,0:T(8,128)S(1)}, f32[1,32,128,128]{3,2,1,0:T(8,128)}, u32[]{:S(2)}) copy-start(f32[1,32,128,128]{3,2,1,0:T(8,128)} %param.9) | copy-start | bytes 6291460
  30.7 7.4 %slice-start = ((f32[1,32,128,128]{3,2,1,0:T(8,128)}), f32[1,3,128,128]{3,2,1,0:T(8,128)S(1)}, s32[]{:S(2)}) async-start(f32[1,32,128,128]{3,2,1,0:T(8,128)} %param.9), calls=%async_computation.4 | async-start | bytes 393216 | tf_op jit(solution)/shard_map/slice | solution.py:141
  31.9 18.0 %copy-start.5 = (s32[1,128,1]{1,2,0:T(1,128)S(1)}, s32[1,128,1]{1,2,0:T(1,128)}, u32[]{:S(2)}) copy-start(s32[1,128,1]{1,2,0:T(1,128)} %param.10) | copy-start | bytes 1540
  31.9 17.6 %all-to-all-start.1 = ((f32[128,2,384]{2,1,0:T(2,128)}), f32[128,2,384]{2,1,0:T(2,128)S(1)}, u32[]{:S(2)}, u32[]{:S(2)}) async-start(f32[128,2,384]{2,1,0:T(2,128)} %maximum_multiply_fusion.1), calls=%async_computation.1 | async-start | bytes 786432 | tf_op jit(solution)/shard_map/all_to_all | solution.py:135
  55.0 31.7 %all-to-all-start.2 = ((f32[32,128,128]{2,1,0:T(8,128)}), f32[32,128,128]{2,1,0:T(8,128)S(1)}, u32[]{:S(2)}, u32[]{:S(2)}) async-start(f32[32,128,128]{2,1,0:T(8,128)} %copy.38), calls=%async_computation.2 | async-start | bytes 4194304 | tf_op jit(solution)/shard_map/all_to_all | solution.py:45
  86.8 2.2 %copy-start = (f32[1024,1024]{0,1:T(8,128)S(1)}, f32[1024,1024]{0,1:T(8,128)}, u32[]{:S(2)}) copy-start(f32[1024,1024]{0,1:T(8,128)} %cosine_multiply_fusion) | copy-start | bytes 12582916
  86.8 2.9 %copy-start.1 = (f32[1,512,1024]{2,1,0:T(8,128)S(1)}, f32[1,512,1024]{2,1,0:T(8,128)}, u32[]{:S(2)}) copy-start(f32[1,512,1024]{2,1,0:T(8,128)} %get-tuple-element.6) | copy-start | bytes 6291460
  86.8 3.5 %copy-start.2 = (f32[1,512,1024]{2,1,0:T(8,128)S(1)}, f32[1,512,1024]{2,1,0:T(8,128)}, u32[]{:S(2)}) copy-start(f32[1,512,1024]{2,1,0:T(8,128)} %get-tuple-element.5) | copy-start | bytes 6291460
  96.7 3.6 %copy-start.3 = (f32[1,512,1024]{2,1,0:T(8,128)}, f32[1,512,1024]{2,1,0:T(8,128)S(1)}, u32[]{:S(2)}) copy-start(f32[1,512,1024]{2,1,0:T(8,128)S(1)} %fusion.19) | copy-start | bytes 6291460
